TPU v7x, 256 devices: a whole 4x4x8 slice. The times are simulated.
256 devices in a mesh: dp: 4 (over x), node: 2 (over core), local: 32 (over z, y).
Axes of the slice: x: 4, y: 4, z: 8, core: 2. Of those that a mesh axis runs over, the one named last changes fastest.
Arguments:
- tokens: bfloat16 [32768, 2048], P(('dp', 'node', 'local')), may hold values from -6 to 6
- cotangent: bfloat16 [32768, 2048], P(('dp', 'node', 'local')), may hold values from -4 to 4
- routes: int32 [32768, 8], P(('dp', 'node', 'local')), may hold values from 0 to 63, all different within a row; in each aligned block of 128 rows (0 to 127, 128 to 255, ...) at most 24 rows name the same one
- gates: bfloat16 [32768, 8], P(('dp', 'node', 'local')), may hold values from 0.029907227 to 0.3984375
- w_gate: bfloat16 [64, 2048, 384], P(('node', 'local'), 'dp'), may hold values from -0.125 to 0.125
- w_up: bfloat16 [64, 2048, 384], P(('node', 'local'), 'dp'), may hold values from -0.125 to 0.125
- w_down: bfloat16 [64, 2048, 384], P(('node', 'local'), 'dp'), may hold values from -0.3125 to 0.3125
Outputs:
- input_grad: bfloat16 [32768, 2048], P(('dp', 'node', 'local'))
- gate_grad: bfloat16 [32768, 8], P(('dp', 'node', 'local'))
- gate_weight_grad: float32 [64, 2048, 384], P(('node', 'local'), 'dp')
- up_weight_grad: float32 [64, 2048, 384], P(('node', 'local'), 'dp')
- down_weight_grad: float32 [64, 2048, 384], P(('node', 'local'), 'dp')
Inputs may be any that keep to these rules, and one draw needn't show every extreme that they name: `routes`: each token names 8 different experts. Among the tokens of one device no expert is named more than 24 times, and on some device some expert is named exactly 24 times.
All inputs are finite; a program needn't handle non-finite values.
Results may differ from a plain program's by a relative error of at most 0.0057.
Values may be sent and summed in bfloat16 or wider, within the bound.
No kernel may reach another device: no remote copies, remote signals or barrier semaphores. Data moves between devices by JAX's collectives and lax.ppermute only.
A program may use at most 128 MiB of HBM per device.

v0:
```python
import jax
import jax.numpy as jnp
from jax import lax
from jax.sharding import PartitionSpec as P


def expert_rows(rows_x, rows_dy, rows_gate, gate_proj, up_proj, down_proj):
    pre_gate = jnp.dot(rows_x, gate_proj, preferred_element_type=jnp.float32)
    pre_up = jnp.dot(rows_x, up_proj, preferred_element_type=jnp.float32)
    gate_sigmoid = jax.nn.sigmoid(pre_gate)
    activated = pre_gate * gate_sigmoid
    hidden = activated * pre_up
    upstream = jnp.dot(rows_dy, down_proj, preferred_element_type=jnp.float32)
    gate_grad = jnp.sum(upstream * hidden, axis=1).astype(jnp.bfloat16)
    weight = rows_gate.astype(jnp.float32)[:, None]
    scaled_hidden = (weight * hidden).astype(jnp.bfloat16)
    hidden_grad = weight * upstream
    pre_gate_grad = (
        hidden_grad * pre_up * gate_sigmoid * (1.0 + pre_gate * (1.0 - gate_sigmoid))
    ).astype(jnp.bfloat16)
    pre_up_grad = (hidden_grad * activated).astype(jnp.bfloat16)
    over_rows = (((0,), (0,)), ((), ()))
    down_grad = lax.dot_general(
        rows_dy, scaled_hidden, over_rows, preferred_element_type=jnp.float32
    )
    gate_wgrad = lax.dot_general(
        rows_x, pre_gate_grad, over_rows, preferred_element_type=jnp.float32
    )
    up_wgrad = lax.dot_general(rows_x, pre_up_grad, over_rows, preferred_element_type=jnp.float32)
    over_hidden = (((1,), (1,)), ((), ()))
    input_rows = lax.dot_general(
        pre_gate_grad, gate_proj, over_hidden, preferred_element_type=jnp.float32
    )
    input_rows = input_rows + lax.dot_general(
        pre_up_grad, up_proj, over_hidden, preferred_element_type=jnp.float32
    )
    return (input_rows.astype(jnp.bfloat16), gate_grad, gate_wgrad, up_wgrad, down_grad)


def run_tiles(
    packed_x, packed_dy, packed_gate, tile_count, tile_rows, gate_proj, up_proj, down_proj
):
    length, width = packed_x.shape
    hidden_units = gate_proj.shape[1]
    tile_total = length // tile_rows
    tiled = (
        packed_x.reshape(tile_total, tile_rows, width),
        packed_dy.reshape(tile_total, tile_rows, width),
        packed_gate.reshape(tile_total, tile_rows),
        jnp.arange(tile_total, dtype=jnp.int32),
    )

    def work(item):
        return expert_rows(item[0], item[1], item[2], gate_proj, up_proj, down_proj)

    def skip(item):
        return (
            jnp.zeros((tile_rows, width), jnp.bfloat16),
            jnp.zeros((tile_rows,), jnp.bfloat16),
            jnp.zeros((width, hidden_units), jnp.float32),
            jnp.zeros((width, hidden_units), jnp.float32),
            jnp.zeros((width, hidden_units), jnp.float32),
        )

    def one_tile(running, item):
        results = lax.cond(item[3] < tile_count, work, skip, item)
        gate_acc, up_acc, down_acc = running
        return (
            (gate_acc + results[2], up_acc + results[3], down_acc + results[4]),
            (results[0], results[1]),
        )

    start_state = (
        jnp.zeros((width, hidden_units), jnp.float32),
        jnp.zeros((width, hidden_units), jnp.float32),
        jnp.zeros((width, hidden_units), jnp.float32),
    )
    sums, rows_out = lax.scan(one_tile, start_state, tiled)
    return (
        rows_out[0].reshape(length, width),
        rows_out[1].reshape(length),
        sums[0],
        sums[1],
        sums[2],
    )


def local(tokens, cotangent, routes, gates, w_gate, w_up, w_down):
    tokens_dev, top_count = routes.shape
    width = tokens.shape[1]
    groups = lax.axis_size("node")
    members = lax.axis_size("local")
    experts = groups * members
    capacity = min(
        tokens_dev,
        max(3 * tokens_dev * top_count // (2 * experts), tokens_dev * top_count // experts),
    )
    pick_count = tokens_dev * top_count
    slots = experts * capacity
    flat_routes = routes.reshape(pick_count)
    one_hot = (flat_routes[:, None] == jnp.arange(experts, dtype=jnp.int32)[None, :]).astype(
        jnp.int32
    )
    rank = jnp.sum((jnp.cumsum(one_hot, axis=0) - one_hot) * one_hot, axis=1)
    target = flat_routes * capacity + rank
    filler = (
        jnp.full((slots,), -1, jnp.int32).at[target].set(jnp.arange(pick_count, dtype=jnp.int32))
    )
    is_filled = filler >= 0
    safe_pick = jnp.where(is_filled, filler, 0)
    owner_token = safe_pick // top_count
    send_x = jnp.where(is_filled[:, None], tokens[owner_token], jnp.zeros((), tokens.dtype))
    send_dy = jnp.where(is_filled[:, None], cotangent[owner_token], jnp.zeros((), cotangent.dtype))
    send_gate = jnp.where(
        is_filled, gates.reshape(pick_count)[safe_pick], jnp.zeros((), gates.dtype)
    )
    full_weights = (
        lax.all_gather(w_gate, "dp", axis=1, tiled=True),
        lax.all_gather(w_up, "dp", axis=1, tiled=True),
        lax.all_gather(w_down, "dp", axis=1, tiled=True),
    )
    gate_proj = full_weights[0][0]
    up_proj = full_weights[1][0]
    down_proj = full_weights[2][0]
    recv_x, recv_dy, recv_gate = (
        lax.all_to_all(
            send_x.reshape(experts, capacity, width),
            ("node", "local"),
            split_axis=0,
            concat_axis=0,
            tiled=True,
        ),
        lax.all_to_all(
            send_dy.reshape(experts, capacity, width),
            ("node", "local"),
            split_axis=0,
            concat_axis=0,
            tiled=True,
        ),
        lax.all_to_all(
            send_gate.reshape(experts, capacity),
            ("node", "local"),
            split_axis=0,
            concat_axis=0,
            tiled=True,
        ),
    )
    flat_x = recv_x.reshape(slots, width)
    flat_dy = recv_dy.reshape(slots, width)
    flat_gate = recv_gate.reshape(slots)
    tile_rows = min(512, slots)
    length = (slots + tile_rows - 1) // tile_rows * tile_rows
    is_live = flat_gate > 0
    position = jnp.cumsum(is_live.astype(jnp.int32)) - 1
    live_total = jnp.sum(is_live.astype(jnp.int32))
    source = (
        jnp.full((length,), slots, jnp.int32)
        .at[jnp.where(is_live, position, length)]
        .set(jnp.arange(slots, dtype=jnp.int32), mode="drop")
    )
    packed_x = jnp.concatenate([flat_x, jnp.zeros((1, width), flat_x.dtype)])[source]
    packed_dy = jnp.concatenate([flat_dy, jnp.zeros((1, width), flat_dy.dtype)])[source]
    packed_gate = jnp.concatenate([flat_gate, jnp.zeros((1,), flat_gate.dtype)])[source]
    tile_count = (live_total + tile_rows - 1) // tile_rows
    results = run_tiles(
        packed_x, packed_dy, packed_gate, tile_count, tile_rows, gate_proj, up_proj, down_proj
    )
    back_index = jnp.where(is_live, position, length)
    input_rows = jnp.concatenate([results[0], jnp.zeros((1, width), jnp.bfloat16)])[back_index]
    gate_rows = jnp.concatenate([results[1], jnp.zeros((1,), jnp.bfloat16)])[back_index]
    home_x, home_gate = (
        lax.all_to_all(
            input_rows.reshape(experts, capacity, width),
            ("node", "local"),
            split_axis=0,
            concat_axis=0,
            tiled=True,
        ),
        lax.all_to_all(
            gate_rows.reshape(experts, capacity),
            ("node", "local"),
            split_axis=0,
            concat_axis=0,
            tiled=True,
        ),
    )
    per_pick = home_x.reshape(slots, width)[target].reshape(tokens_dev, top_count, width)
    input_grad = jnp.sum(per_pick, axis=1, dtype=jnp.float32).astype(jnp.bfloat16)
    gate_grad = home_gate.reshape(slots)[target].reshape(tokens_dev, top_count)
    summed = (
        lax.psum_scatter(results[2], "dp", scatter_dimension=0, tiled=True),
        lax.psum_scatter(results[3], "dp", scatter_dimension=0, tiled=True),
        lax.psum_scatter(results[4], "dp", scatter_dimension=0, tiled=True),
    )
    return (input_grad, gate_grad, summed[0][None], summed[1][None], summed[2][None])


def solution(mesh):
    placed = (
        P(("dp", "node", "local"), None),
        P(("dp", "node", "local"), None),
        P(("dp", "node", "local"), None),
        P(("dp", "node", "local"), None),
        P(("node", "local"), "dp", None),
        P(("node", "local"), "dp", None),
        P(("node", "local"), "dp", None),
    )
    return jax.shard_map(
        local,
        mesh=mesh,
        in_specs=placed,
        out_specs=(
            P(("dp", "node", "local"), None),
            P(("dp", "node", "local"), None),
            P(("node", "local"), "dp", None),
            P(("node", "local"), "dp", None),
            P(("node", "local"), "dp", None),
        ),
        check_vma=False,
    )
```

profile of v0, /device:TPU:1, one launch (start us, length us, event | category | flops | bytes accessed | tf_op | source)
XLA Modules:
  0.0 722.9 jit_solution(6186933304298628688)
XLA Ops:
  7.2 0.8 copy.20
  8.9 18.0 %reduce-window.15 = s32[64,8,128]{2,1,0:T(8,128)S(1)} reduce-window(s32[64,8,128]{2,1,0:T(8,128)S(1)} %fusion.32, s32[]{:T(128)} %constant.91.clone.1), window={size=1x1x128 pad=0_0x0_0x127_0}, to_apply=%region_0.0 | reduce-window | flops 8323072 | bytes 524292 | tf_op jit(solution)/shard_map/reduce-window
  27.8 4.3 scatter_custom_fusion
  32.2 0.8 copy.24
  33.1 9.5 %gather_fusion = bf16[1536]{0:T(1024)(128)(2,1)S(1)} fusion(bf16[1024]{0:T(1024)(128)(2,1)S(1)} %reshape.221, s32[2048]{0:T(1024)S(1)} %pad_clamp_fusion.3), kind=kCustom, calls=%fused_computation | custom fusion | bytes 12288 | tf_op jit(solution)/shard_map/gather | solution.py:115
  43.3 13.3 %all-to-all-start = ((bf16[64,1,24]{2,1,0:T(2,128)(2,1)}), bf16[64,1,24]{2,1,0:T(2,128)(2,1)S(1)}, u32[]{:S(2)}, u32[]{:S(2)}) async-start(bf16[64,1,24]{2,1,0:T(2,128)(2,1)} %all_to_all.28), calls=%async_computation | async-start | bytes 65536 | tf_op jit(solution)/shard_map/all_to_all | solution.py:140
  56.7 7.1 gather_fusion.4
  63.8 7.0 gather_fusion.1
  70.8 10.2 %broadcast_select_fusion = (bf16[64,24,2048]{2,1,0:T(8,128)(2,1)}, bf16[64,24,2048]{2,1,0:T(8,128)(2,1)}) fusion(bf16[64,24,2048]{2,1,0:T(8,128)(2,1)} %bitcast.85, pred[64,24]{1,0:T(8,128)(4,1)S(1)} %broadcast_in_dim.91, bf16[64,24,2048]{2,1,0:T(8,128)(2,1)} %bitcast.86), kind=kLoop, calls=%fused_computation.51 | loop fusion | flops 6291456 | bytes 25167360 | tf_op jit(solution)/shard_map/jit(_where)/select_n | solution.py:113
  81.0 150.5 %all_to_all.35 = bf16[64,24,2048]{2,1,0:T(8,128)(2,1)} all-to-all(bf16[64,24,2048]{2,1,0:T(8,128)(2,1)} %get-tuple-element.258), channel_id=1, replica_groups=mesh['dp'=4,'node'=2,'local'=32] {'node','local'}, dimensions={0} | all-to-all | bytes 12582912 | tf_op jit(solution)/shard_map/all_to_all | solution.py:133
  231.5 6.6 all-to-all-start.1
  243.5 6.6 scatter_custom_fusion.1
  250.2 9.5 %gather_fusion.3 = bf16[1536]{0:T(1024)(128)(2,1)S(1)} fusion(bf16[1537]{0:T(1024)(128)(2,1)S(1)} %pad_maximum_fusion.1, s32[2048]{0:T(1024)S(1)} %pad_clamp_fusion.1), kind=kCustom, calls=%fused_computation.3 | custom fusion | bytes 12288 | tf_op jit(solution)/shard_map/gather | solution.py:163
  259.7 6.6 concatenate.17
  266.4 16.3 %gather_fusion.5 = bf16[1536,2048]{1,0:T(8,128)(2,1)} fusion(bf16[1537,2048]{1,0:T(8,128)(2,1)} %concatenate.17, s32[2048]{0:T(1024)S(1)} %pad_clamp_fusion.1), kind=kCustom, calls=%fused_computation.5 | custom fusion | bytes 12589056 | tf_op jit(solution)/shard_map/gather | solution.py:162
  282.7 96.4 %all-to-all-done.1 = bf16[64,24,2048]{2,1,0:T(8,128)(2,1)} async-done(((bf16[64,24,2048]{2,1,0:T(8,128)(2,1)}), bf16[64,24,2048]{2,1,0:T(8,128)(2,1)}, u32[]{:S(2)}, u32[]{:S(2)}) %all-to-all-start.1) | async-done | bytes 6291488 | tf_op jit(solution)/shard_map/all_to_all | solution.py:126
  379.1 6.6 concatenate.15
  385.7 16.3 %gather_fusion.2 = bf16[1536,2048]{1,0:T(8,128)(2,1)} fusion(bf16[1537,2048]{1,0:T(8,128)(2,1)} %concatenate.15, s32[2048]{0:T(1024)S(1)} %pad_clamp_fusion.1), kind=kCustom, calls=%fused_computation.2 | custom fusion | bytes 12589056 | tf_op jit(solution)/shard_map/gather | solution.py:161
  402.1 100.0 %while.19 = (s32[]{:T(128)}, f32[2048,384]{1,0:T(8,128)}, f32[2048,384]{1,0:T(8,128)}, f32[2048,384]{1,0:T(8,128)}, bf16[3,512,2048]{2,1,0:T(8,128)(2,1)}, /*ind...) while((s32[]{:T(128)}, f32[2048,384]{1,0:T(8,128)}, ...), condition=%wide.region_12.13_spmd.clone, body=%wide.region_8.12_spmd.clone.sunk | while | flops 6453985280 | bytes 168048624 | solution.py:78
  403.5 19.4 %conditional.3 = (f32[2048,384]{1,0:T(8,128)}, f32[2048,384]{1,0:T(8,128)}, f32[2048,384]{1,0:T(8,128)}, bf16[1,512,2048]{2,1,0:T(8,128)(2,1)S(1)}, bf16[1,512]{1,0:T(2,128)(2,1)S(1)}) conditional(s32[]{:T(128)} %convert_element_type.89, () %tuple.57, (bf16[3,512,2048]{2,1,0:T(8,128)(2,1)}, s32[]{:T(128)}, bf16[3,512]{1,0:T(4,128)(2,1)S(1)}, ...), branch_computations={%region_9.9_spmd, %region_10.11_spmd} | conditional | flops 6449266688 | bytes 110374096 | solution.py:66
  403.5 3.2 fusion.11
  406.8 2.8 fusion.9
  409.6 1.4 multiply_reduce_fusion
  411.0 1.3 fusion.43
  412.4 1.3 fusion
  413.7 3.1 fusion.5
  416.8 3.1 fusion.7
  419.9 3.0 fusion.1
  422.9 6.3 select_add_fusion.6
  429.2 2.7 select_add_fusion.5
  431.9 1.6 constant_dynamic-update-slice_fusion.2
  435.5 19.4 %conditional.3 = (f32[2048,384]{1,0:T(8,128)}, f32[2048,384]{1,0:T(8,128)}, f32[2048,384]{1,0:T(8,128)}, bf16[1,512,2048]{2,1,0:T(8,128)(2,1)S(1)}, bf16[1,512]{1,0:T(2,128)(2,1)S(1)}) conditional(s32[]{:T(128)} %convert_element_type.89, () %tuple.57, (bf16[3,512,2048]{2,1,0:T(8,128)(2,1)}, s32[]{:T(128)}, bf16[3,512]{1,0:T(4,128)(2,1)S(1)}, ...), branch_computations={%region_9.9_spmd, %region_10.11_spmd} | conditional | flops 6449266688 | bytes 110374096 | solution.py:66
  435.5 3.2 fusion.11
  438.8 2.8 fusion.9
  441.6 1.4 multiply_reduce_fusion
  443.0 1.3 fusion.43
  444.4 1.3 fusion
  445.7 3.1 fusion.5
  448.8 3.1 fusion.7
  451.9 3.0 fusion.1
  454.9 8.1 %select_add_fusion.6 = (f32[2048,384]{1,0:T(8,128)}, f32[2048,384]{1,0:T(8,128)}) fusion(f32[2048,384]{1,0:T(8,128)} %get-tuple-element.353, f32[2048,384]{1,0:T(8,128)} %get-tuple-element.388, pred[]{:T(512)S(6)} %compare.10, f32[2048,384]{1,0:T(8,128)} %get-tuple-element.354, f32[2048,384]{1,0:T(8,128)} %get-tuple-element.387), kind=kLoop, calls=%fused_computation.47.clone.1 | loop fusion | flops 3145728 | bytes 18874368 | tf_op jit(solution)/shard_map/while/body/eval_jaxpr/add | solution.py:69
  463.0 2.7 select_add_fusion.5
  465.7 1.6 constant_dynamic-update-slice_fusion.2
  469.3 19.4 %conditional.3 = (f32[2048,384]{1,0:T(8,128)}, f32[2048,384]{1,0:T(8,128)}, f32[2048,384]{1,0:T(8,128)}, bf16[1,512,2048]{2,1,0:T(8,128)(2,1)S(1)}, bf16[1,512]{1,0:T(2,128)(2,1)S(1)}) conditional(s32[]{:T(128)} %convert_element_type.89, () %tuple.57, (bf16[3,512,2048]{2,1,0:T(8,128)(2,1)}, s32[]{:T(128)}, bf16[3,512]{1,0:T(4,128)(2,1)S(1)}, ...), branch_computations={%region_9.9_spmd, %region_10.11_spmd} | conditional | flops 6449266688 | bytes 110374096 | solution.py:66
  469.3 3.2 fusion.11
  472.6 2.8 fusion.9
  475.4 1.4 multiply_reduce_fusion
  476.8 1.3 fusion.43
  478.2 1.3 fusion
  479.5 3.1 fusion.5
  482.6 3.1 fusion.7
  485.7 3.0 fusion.1
  488.7 8.1 %select_add_fusion.6 = (f32[2048,384]{1,0:T(8,128)}, f32[2048,384]{1,0:T(8,128)}) fusion(f32[2048,384]{1,0:T(8,128)} %get-tuple-element.353, f32[2048,384]{1,0:T(8,128)} %get-tuple-element.388, pred[]{:T(512)S(6)} %compare.10, f32[2048,384]{1,0:T(8,128)} %get-tuple-element.354, f32[2048,384]{1,0:T(8,128)} %get-tuple-element.387), kind=kLoop, calls=%fused_computation.47.clone.1 | loop fusion | flops 3145728 | bytes 18874368 | tf_op jit(solution)/shard_map/while/body/eval_jaxpr/add | solution.py:69
  496.8 2.7 select_add_fusion.5
  499.5 1.6 constant_dynamic-update-slice_fusion.2
  502.8 9.5 %gather_fusion.8 = bf16[1536]{0:T(1024)(128)(2,1)S(1)} fusion(bf16[1537]{0:T(1024)(128)(2,1)S(1)} %pad_maximum_fusion, s32[2048]{0:T(1024)S(1)} %pad_clamp_fusion), kind=kCustom, calls=%fused_computation.8 | custom fusion | bytes 12288 | tf_op jit(solution)/shard_map/gather | solution.py:170
  512.9 10.1 %all-to-all-start.4 = ((bf16[64,1,24]{2,1,0:T(2,128)(2,1)}), bf16[64,1,24]{2,1,0:T(2,128)(2,1)S(1)}, u32[]{:S(2)}, u32[]{:S(2)}) async-start(bf16[64,1,24]{2,1,0:T(2,128)(2,1)} %all_to_all.29), calls=%async_computation.4 | async-start | bytes 65536 | tf_op jit(solution)/shard_map/all_to_all | solution.py:179
  523.1 6.6 concatenate.18
  529.7 16.4 %gather_fusion.6 = bf16[1536,2048]{1,0:T(8,128)(2,1)} fusion(bf16[1537,2048]{1,0:T(8,128)(2,1)} %concatenate.18, s32[2048]{0:T(1024)S(1)} %pad_clamp_fusion), kind=kCustom, calls=%fused_computation.6 | custom fusion | bytes 12589056 | tf_op jit(solution)/shard_map/gather | solution.py:169
  546.1 10.3 %all-to-all-start.3 = ((bf16[64,24,2048]{2,1,0:T(8,128)(2,1)}), bf16[64,24,2048]{2,1,0:T(8,128)(2,1)}, u32[]{:S(2)}, u32[]{:S(2)}) async-start(bf16[64,24,2048]{2,1,0:T(8,128)(2,1)} %bitcast.84), calls=%async_computation.3 | async-start | bytes 12582912 | tf_op jit(solution)/shard_map/all_to_all | solution.py:172
  557.8 6.8 gather_fusion.9
  565.4 132.1 %all-to-all-done.3 = bf16[64,24,2048]{2,1,0:T(8,128)(2,1)} async-done(((bf16[64,24,2048]{2,1,0:T(8,128)(2,1)}), bf16[64,24,2048]{2,1,0:T(8,128)(2,1)}, u32[]{:S(2)}, u32[]{:S(2)}) %all-to-all-start.3) | async-done | bytes 6291488 | tf_op jit(solution)/shard_map/all_to_all | solution.py:172
  697.5 12.5 %gather_fusion.7 = bf16[1024,2048]{1,0:T(8,128)(2,1)} fusion(bf16[1536,2048]{1,0:T(8,128)(2,1)} %bitcast.19, s32[1024]{0:T(1024)S(1)} %broadcast_clamp_fusion), kind=kCustom, calls=%fused_computation.7 | custom fusion | bytes 8392704 | tf_op jit(solution)/shard_map/gather | solution.py:187
  709.9 5.9 bitcast_reduce_fusion
  (150 shorter events, 15.3 us)
Async XLA Ops:
  7.2 49.5 %copy-start = (bf16[128,2048]{1,0:T(8,128)(2,1)S(1)}, bf16[128,2048]{1,0:T(8,128)(2,1)}, u32[]{:S(2)}) copy-start(bf16[128,2048]{1,0:T(8,128)(2,1)} %param.12) | copy-start | bytes 1572868
  27.8 4.4 copy-start.9
  43.3 37.7 %all-to-all-start = ((bf16[64,1,24]{2,1,0:T(2,128)(2,1)}), bf16[64,1,24]{2,1,0:T(2,128)(2,1)S(1)}, u32[]{:S(2)}, u32[]{:S(2)}) async-start(bf16[64,1,24]{2,1,0:T(2,128)(2,1)} %all_to_all.28), calls=%async_computation | async-start | bytes 65536 | tf_op jit(solution)/shard_map/all_to_all | solution.py:140
  56.7 7.1 copy-start.2
  231.5 147.6 %all-to-all-start.1 = ((bf16[64,24,2048]{2,1,0:T(8,128)(2,1)}), bf16[64,24,2048]{2,1,0:T(8,128)(2,1)}, u32[]{:S(2)}, u32[]{:S(2)}) async-start(bf16[64,24,2048]{2,1,0:T(8,128)(2,1)} %get-tuple-element.259), calls=%async_computation.1 | async-start | bytes 12582912 | tf_op jit(solution)/shard_map/all_to_all | solution.py:126
  238.1 164.0 %all-gather.4.cloned.1.call-start = ((), (), s32[]{:S(2)}) async-start(), calls=%async_computation.8 | async-start | bytes 1966080 | tf_op jit(solution)/shard_map/all_gather | solution.py:120
  238.8 163.2 %all-gather.6.cloned.1.call-start = ((), (), s32[]{:S(2)}) async-start(), calls=%async_computation.9 | async-start | bytes 1966080 | tf_op jit(solution)/shard_map/all_gather | solution.py:119
  239.6 162.5 %all-gather.8.cloned.1.call-start = ((), (), s32[]{:S(2)}) async-start(), calls=%async_computation.10 | async-start | bytes 1966080 | tf_op jit(solution)/shard_map/all_gather | solution.py:118
  240.3 475.5 %reduce-scatter.4.cloned.1.call-start = ((), (), s32[]{:S(2)}) async-start(), calls=%async_computation.11 | async-start | bytes 3932160 | tf_op jit(solution)/shard_map/reduce_scatter | solution.py:191
  403.5 3.3 copy-start.5
  403.5 6.1 copy-start.7
  406.7 2.8 copy-start.11
  409.6 4.1 slice-start
  411.0 1.4 copy-start.6
  411.0 2.7 slice-start.1
  422.9 6.3 copy-start.3
  431.9 2.3 copy-start.4
  435.5 3.3 copy-start.5
  435.5 6.1 copy-start.7
  438.8 2.8 copy-start.11
  441.6 4.1 slice-start
  443.0 1.4 copy-start.6
  443.0 2.7 slice-start.1
  454.9 8.1 %copy-start.3 = (f32[2048,384]{1,0:T(8,128)S(1)}, f32[2048,384]{1,0:T(8,128)}, u32[]{:S(2)}) copy-start(f32[2048,384]{1,0:T(8,128)} %get-tuple-element.386) | copy-start | bytes 9437188 | tf_op jit(solution)/shard_map/while
  465.7 2.3 copy-start.4
  469.3 3.3 copy-start.5
  469.3 6.1 copy-start.7
  472.5 2.8 copy-start.11
  475.4 4.1 slice-start
  476.8 1.4 copy-start.6
  476.8 2.7 slice-start.1
  488.7 8.1 %copy-start.3 = (f32[2048,384]{1,0:T(8,128)S(1)}, f32[2048,384]{1,0:T(8,128)}, u32[]{:S(2)}) copy-start(f32[2048,384]{1,0:T(8,128)} %get-tuple-element.386) | copy-start | bytes 9437188 | tf_op jit(solution)/shard_map/while
  499.5 2.3 copy-start.4
  502.0 0.7 copy-start.8
  512.9 33.1 %all-to-all-start.4 = ((bf16[64,1,24]{2,1,0:T(2,128)(2,1)}), bf16[64,1,24]{2,1,0:T(2,128)(2,1)S(1)}, u32[]{:S(2)}, u32[]{:S(2)}) async-start(bf16[64,1,24]{2,1,0:T(2,128)(2,1)} %all_to_all.29), calls=%async_computation.4 | async-start | bytes 65536 | tf_op jit(solution)/shard_map/all_to_all | solution.py:179
  546.1 151.4 %all-to-all-start.3 = ((bf16[64,24,2048]{2,1,0:T(8,128)(2,1)}), bf16[64,24,2048]{2,1,0:T(8,128)(2,1)}, u32[]{:S(2)}, u32[]{:S(2)}) async-start(bf16[64,24,2048]{2,1,0:T(8,128)(2,1)} %bitcast.84), calls=%async_computation.3 | async-start | bytes 12582912 | tf_op jit(solution)/shard_map/all_to_all | solution.py:172
  556.4 159.4 %reduce-scatter.6.cloned.1.call-start = ((), (), s32[]{:S(2)}) async-start(), calls=%async_computation.12 | async-start | bytes 3932160 | tf_op jit(solution)/shard_map/reduce_scatter | solution.py:192
  556.5 1.1 copy-start.10
  557.0 158.8 %reduce-scatter.8.cloned.1.call-start = ((), (), s32[]{:S(2)}) async-start(), calls=%async_computation.13 | async-start | bytes 3932160 | tf_op jit(solution)/shard_map/reduce_scatter | solution.py:193
  697.5 18.3 %copy-start.1 = (bf16[128,2048]{1,0:T(8,128)(2,1)S(1)}, bf16[128,2048]{1,0:T(8,128)(2,1)}, u32[]{:S(2)}) copy-start(bf16[128,2048]{1,0:T(8,128)(2,1)} %param.12) | copy-start | bytes 1572868
Sparse Core Ops, SparseCore 0:
  240.7 29.7 all-gather.3
  272.4 29.1 all-gather.5
  303.4 29.1 all-gather.7
  502.2 41.4 reduce-scatter.3
  560.1 41.5 reduce-scatter.5
  604.7 40.5 reduce-scatter.7
where the time goes:
time: 731 us; the launch traced here: 723 us
  waiting for transfers between devices  232 us (32%)
  local copies, waits for them, and re-layouts  157 us (21%)
  blocking collectives  150 us (21%)
  other arithmetic  67.8 us (9%)
  matrix products  57.5 us (8%)
  starting transfers between devices  40.5 us (6%)
  between operations  15.4 us (2%)
    all_to_all x1, blocking collectives, local(): lax.all_to_all(send_dy.reshape(experts, capacity, width), ('node', 'local...  150 us
    all_to_all x1, waiting for transfers between devices, local(): lax.all_to_all(input_rows.reshape(experts, capacity, width), ('node', 'lo...  132 us
    all_to_all x1, waiting for transfers between devices, local(): lax.all_to_all(send_x.reshape(experts, capacity, width), ('node', 'local'...  96.4 us
    add x3, other arithmetic, one_tile(): down_acc + results[4]  22.4 us
    another operation x5, other arithmetic  18.5 us
    gather x1, local copies, waits for them, and re-layouts, local(): jnp.concatenate([results[0], jnp.zeros((1, width), jnp.bfloat16)])  16.4 us
    gather x1, local copies, waits for them, and re-layouts, local(): jnp.concatenate([flat_x, jnp.zeros((1, width), flat_x.dtype)])[source]  16.3 us
    gather x1, local copies, waits for them, and re-layouts, local(): jnp.concatenate([flat_dy, jnp.zeros((1, width), flat_dy.dtype)])[source]  16.3 us
  transfers between devices with their start and end apart: 10, of which 2 were waited for; matrix products, arithmetic and copies ran while one was open for 20% of the time, Pallas kernels for 0%

commit v1 on v0

v1 whole, which is shorter than its diff:
```python
import jax
import jax.numpy as jnp
from jax import lax
from jax.sharding import PartitionSpec as P


def expert_rows(rows_x, rows_dy, rows_gate, gate_proj, up_proj, down_proj):
    pre_gate = jnp.dot(rows_x, gate_proj, preferred_element_type=jnp.float32)
    pre_up = jnp.dot(rows_x, up_proj, preferred_element_type=jnp.float32)
    gate_sigmoid = jax.nn.sigmoid(pre_gate)
    activated = pre_gate * gate_sigmoid
    hidden = activated * pre_up
    upstream = jnp.dot(rows_dy, down_proj, preferred_element_type=jnp.float32)
    gate_grad = jnp.sum(upstream * hidden, axis=1).astype(jnp.bfloat16)
    weight = rows_gate.astype(jnp.float32)[:, None]
    scaled_hidden = (weight * hidden).astype(jnp.bfloat16)
    hidden_grad = weight * upstream
    pre_gate_grad = (
        hidden_grad * pre_up * gate_sigmoid * (1.0 + pre_gate * (1.0 - gate_sigmoid))
    ).astype(jnp.bfloat16)
    pre_up_grad = (hidden_grad * activated).astype(jnp.bfloat16)
    over_rows = (((0,), (0,)), ((), ()))
    down_grad = lax.dot_general(
        rows_dy, scaled_hidden, over_rows, preferred_element_type=jnp.float32
    )
    gate_wgrad = lax.dot_general(
        rows_x, pre_gate_grad, over_rows, preferred_element_type=jnp.float32
    )
    up_wgrad = lax.dot_general(rows_x, pre_up_grad, over_rows, preferred_element_type=jnp.float32)
    over_hidden = (((1,), (1,)), ((), ()))
    input_rows = lax.dot_general(
        pre_gate_grad, gate_proj, over_hidden, preferred_element_type=jnp.float32
    )
    input_rows = input_rows + lax.dot_general(
        pre_up_grad, up_proj, over_hidden, preferred_element_type=jnp.float32
    )
    return (input_rows.astype(jnp.bfloat16), gate_grad, gate_wgrad, up_wgrad, down_grad)


def local(tokens, cotangent, routes, gates, w_gate, w_up, w_down):
    tokens_dev, top_count = routes.shape
    width = tokens.shape[1]
    groups = lax.axis_size("node")
    members = lax.axis_size("local")
    experts = groups * members
    capacity = min(
        tokens_dev,
        max(3 * tokens_dev * top_count // (2 * experts), tokens_dev * top_count // experts),
    )
    slots = experts * capacity
    pad = 128
    hit = routes[:, :, None] == jnp.arange(experts, dtype=jnp.int32)[None, None, :]
    named = jnp.any(hit, axis=1)
    earlier = (
        jnp.arange(tokens_dev)[:, None] > jnp.arange(tokens_dev)[None, :]
    ).astype(jnp.bfloat16)
    rank = jnp.dot(earlier, named.astype(jnp.bfloat16), preferred_element_type=jnp.float32)
    rank = rank.astype(jnp.int32)
    choose = named.T[:, None, :] & (
        rank.T[:, None, :] == jnp.arange(capacity, dtype=jnp.int32)[None, :, None]
    )
    choose_b = choose.astype(jnp.bfloat16)
    send_x = jnp.einsum(
        "ert,td->erd", choose_b, tokens, preferred_element_type=jnp.float32
    ).astype(jnp.bfloat16)
    send_dy = jnp.einsum(
        "ert,td->erd", choose_b, cotangent, preferred_element_type=jnp.float32
    ).astype(jnp.bfloat16)
    gate_te = jnp.sum(jnp.where(hit, gates[:, :, None], jnp.zeros((), gates.dtype)), axis=1)
    send_gate = jnp.sum(
        jnp.where(choose, gate_te.T[:, None, :], jnp.zeros((), gates.dtype)), axis=2
    )
    gate_block = jnp.zeros((experts, capacity, pad), jnp.bfloat16).at[:, :, 0].set(send_gate)
    send = jnp.concatenate([send_x, send_dy, gate_block], axis=2)
    full_weights = (
        lax.all_gather(w_gate, "dp", axis=1, tiled=True),
        lax.all_gather(w_up, "dp", axis=1, tiled=True),
        lax.all_gather(w_down, "dp", axis=1, tiled=True),
    )
    gate_proj = full_weights[0][0]
    up_proj = full_weights[1][0]
    down_proj = full_weights[2][0]
    recv = lax.all_to_all(send, ("node", "local"), split_axis=0, concat_axis=0, tiled=True)
    flat = recv.reshape(slots, 2 * width + pad)
    results = expert_rows(
        flat[:, :width],
        flat[:, width : 2 * width],
        flat[:, 2 * width],
        gate_proj,
        up_proj,
        down_proj,
    )
    grad_block = jnp.zeros((slots, pad), jnp.bfloat16).at[:, 0].set(results[1])
    back = jnp.concatenate([results[0], grad_block], axis=1).reshape(
        experts, capacity, width + pad
    )
    home = lax.all_to_all(back, ("node", "local"), split_axis=0, concat_axis=0, tiled=True)
    input_grad = jnp.einsum(
        "ert,erd->td", choose_b, home[:, :, :width], preferred_element_type=jnp.float32
    ).astype(jnp.bfloat16)
    home_gate = home[:, :, width]
    gate_et = jnp.sum(
        jnp.where(choose, home_gate[:, :, None], jnp.zeros((), jnp.bfloat16)), axis=1
    )
    gate_grad = jnp.sum(
        jnp.where(hit, gate_et.T[:, None, :], jnp.zeros((), jnp.bfloat16)), axis=2
    )
    summed = (
        lax.psum_scatter(results[2], "dp", scatter_dimension=0, tiled=True),
        lax.psum_scatter(results[3], "dp", scatter_dimension=0, tiled=True),
        lax.psum_scatter(results[4], "dp", scatter_dimension=0, tiled=True),
    )
    return (input_grad, gate_grad, summed[0][None], summed[1][None], summed[2][None])


def solution(mesh):
    placed = (
        P(("dp", "node", "local"), None),
        P(("dp", "node", "local"), None),
        P(("dp", "node", "local"), None),
        P(("dp", "node", "local"), None),
        P(("node", "local"), "dp", None),
        P(("node", "local"), "dp", None),
        P(("node", "local"), "dp", None),
    )
    return jax.shard_map(
        local,
        mesh=mesh,
        in_specs=placed,
        out_specs=(
            P(("dp", "node", "local"), None),
            P(("dp", "node", "local"), None),
            P(("node", "local"), "dp", None),
            P(("node", "local"), "dp", None),
            P(("node", "local"), "dp", None),
        ),
        check_vma=False,
    )
```

time: 731 us -> 564 us (0.77)
  waiting for transfers between devices: 232 us -> 430 us
  blocking collectives: 150 us -> 0 us
  local copies, waits for them, and re-layouts: 157 us -> 7.52 us
  other arithmetic: 67.8 us -> 12.8 us
  starting transfers between devices: 40.5 us -> 25.7 us
  matrix products: 57.5 us -> 69.4 us
    all_to_all x4 -> x2, waiting for transfers between devices: 229 us -> 427 us  [the longest x1 295 us: local(): lax.all_to_all(send, ('node', 'local'), split_axis=0, concat_axis=0, tile...]
    all_to_all x1 -> x0, blocking collectives: 150 us -> none  [local(): lax.all_to_all(send_dy.reshape(experts, capacity, width), ('node', 'local...]
    gather x10 -> x0, local copies, waits for them, and re-layouts: 111 us -> none  [the longest x1 16.4 us: local(): jnp.concatenate([results[0], jnp.zeros((1, width), jnp.bfloat16)])]
    add x6 -> x0, other arithmetic: 30.5 us -> none  [the longest x3 22.4 us: one_tile(): down_acc + results[4]]
    concatenate x3 -> x0, local copies, waits for them, and re-layouts: 19.9 us -> none  [the longest x1 6.65 us: local(): jnp.concatenate([results[0], jnp.zeros((1, width), jnp.bfloat16)])]
    another operation x5 -> x2, other arithmetic: 18.5 us -> 1.29 us
    all_to_all x4 -> x2, starting transfers between devices: 40.3 us -> 24.9 us  [the longest x1 13.4 us: local(): lax.all_to_all(send, ('node', 'local'), split_axis=0, concat_axis=0, tile...]
    dot_general x0 -> x4, matrix products: none -> 11.6 us  [the longest x1 7.86 us: local(): jnp.einsum('ert,erd->td', choose_b, home[:, :, :width], preferred_element...]
  transfers between devices with their start and end apart: 10 -> 8, of which waited for: 2 -> 2; matrix products, arithmetic and copies ran while one was open for 20% -> 11% of each run, Pallas kernels for 0% -> 0%
where the time goes in v1:
time: 564 us; the launch traced here: 559 us
  waiting for transfers between devices  430 us (76%)
  matrix products  69.4 us (12%)
  starting transfers between devices  25.7 us (5%)
  between operations  14.5 us (3%)
  other arithmetic  12.8 us (2%)
  local copies, waits for them, and re-layouts  7.52 us (1%)
    all_to_all x1, waiting for transfers between devices, local(): lax.all_to_all(send, ('node', 'local'), split_axis=0, concat_axis=0, tile...  295 us
    all_to_all x1, waiting for transfers between devices, local(): lax.all_to_all(back, ('node', 'local'), split_axis=0, concat_axis=0, tile...  132 us
    all_to_all x1, starting transfers between devices, local(): lax.all_to_all(send, ('node', 'local'), split_axis=0, concat_axis=0, tile...  13.4 us
    all_to_all x1, starting transfers between devices, local(): lax.all_to_all(back, ('node', 'local'), split_axis=0, concat_axis=0, tile...  11.4 us
  transfers between devices with their start and end apart: 8, of which 2 were waited for; matrix products, arithmetic and copies ran while one was open for 11% of the time, Pallas kernels for 0%

profile of v1, /device:TPU:1, one launch (start us, length us, event | category | flops | bytes accessed | tf_op | source)
XLA Modules:
  0.0 559.4 jit_solution(4049484042283345044)
XLA Ops:
  7.2 0.0 copy-start
  7.2 0.8 fusion.40
  8.0 0.7 fusion.41
  8.7 0.1 convolution_convert_fusion.2
  8.8 0.0 copy-start.6
  8.8 0.1 fusion.33
  9.0 0.3 select_reduce_fusion.1
  9.3 0.2 copy-done.6
  9.5 0.3 copy.37
  9.8 0.0 copy-done
  9.8 0.0 copy-start.8
  9.8 1.8 convolution_convert_fusion
  11.6 0.0 copy-done.8
  11.6 1.8 convolution_convert_fusion.1
  13.4 5.4 fusion.2
  18.8 13.4 %all-to-all-start = ((bf16[64,24,4224]{2,1,0:T(8,128)(2,1)}), bf16[64,24,4224]{2,1,0:T(8,128)(2,1)}, u32[]{:S(2)}, u32[]{:S(2)}) async-start(bf16[64,24,4224]{2,1,0:T(8,128)(2,1)} %fusion.2), calls=%async_computation | async-start | bytes 25952256 | tf_op jit(solution)/shard_map/all_to_all | solution.py:83
  32.2 0.0 all-gather.4.cloned.1.call-start
  32.3 0.7 all-gather.4.cloned.1.call-update
  33.0 0.0 all-gather.6.cloned.1.call-start
  33.0 0.7 all-gather.6.cloned.1.call-update
  33.7 0.0 all-gather.8.cloned.1.call-start
  33.8 0.7 all-gather.8.cloned.1.call-update
  34.5 0.2 reduce-scatter.8.cloned.1.call-start
  34.7 295.0 %all-to-all-done = bf16[64,24,4224]{2,1,0:T(8,128)(2,1)} async-done(((bf16[64,24,4224]{2,1,0:T(8,128)(2,1)}), bf16[64,24,4224]{2,1,0:T(8,128)(2,1)}, u32[]{:S(2)}, u32[]{:S(2)}) %all-to-all-start) | async-done | bytes 12976160 | tf_op jit(solution)/shard_map/all_to_all | solution.py:83
  329.7 1.0 slice.53
  330.7 0.2 copy.42
  331.0 0.0 all-gather.4.cloned.1.call-done
  331.0 7.3 %fusion.8 = f32[1536,384]{0,1:T(8,128)} fusion(bf16[1536,4224]{1,0:T(8,128)(2,1)} %bitcast.5, bf16[1,2048,384]{2,1,0:T(8,128)(2,1)} %all-gather.4.cloned.1.call-done), kind=kOutput, calls=%fused_computation.11 | convolution fusion | flops 2415919104 | bytes 10223616 | tf_op jit(solution)/shard_map/dot_general | solution.py:13
  338.2 0.0 all-gather.6.cloned.1.call-done
  338.2 7.3 %fusion.16 = f32[1536,384]{0,1:T(8,128)} fusion(bf16[1536,4224]{1,0:T(8,128)(2,1)} %bitcast.5, bf16[1,2048,384]{2,1,0:T(8,128)(2,1)} %all-gather.6.cloned.1.call-done), kind=kOutput, calls=%fused_computation.21 | convolution fusion | flops 2415919104 | bytes 10223616 | tf_op jit(solution)/shard_map/dot_general | solution.py:9
  345.5 0.0 all-gather.8.cloned.1.call-done
  345.5 0.0 copy-start.10
  345.5 9.7 %multiply_convert_fusion.2 = (bf16[1536,384]{0,1:T(8,128)(2,1)S(1)}, bf16[1536]{0:T(1024)(128)(2,1)S(1)}, bf16[1536,384]{0,1:T(8,128)(2,1)}, f32[1536,384]{0,1:T(8,128)S(1)}) fusion(f32[1536,384]{0,1:T(8,128)} %fusion.16, f32[1536,384]{0,1:T(8,128)} %fusion.8, f32[1536]{0:T(1024)S(1)} %convert_reduce_fusion, ...), kind=kOutput, calls=%fused_computation.28 | convolution fusion | flops 2425944576 | bytes 17310720 | tf_op jit(solution)/shard_map/dot_general | solution.py:8
  355.2 0.0 copy-done.10
  355.2 8.7 %fusion.6 = f32[2048,384]{1,0:T(8,128)} fusion(bf16[1536,4224]{1,0:T(8,128)(2,1)} %bitcast.5, f32[1536]{0:T(1024)S(1)} %convert_reduce_fusion, f32[1536,384]{0,1:T(8,128)S(1)} %copy-done.10, f32[1536,384]{0,1:T(8,128)S(1)} %get-tuple-element.32), kind=kOutput, calls=%fused_computation.9 | convolution fusion | flops 2420047872 | bytes 14161920 | tf_op jit(solution)/shard_map/dot_general | solution.py:23
  364.0 0.0 reduce-scatter.8.cloned.1.call-update
  364.0 0.6 compare_reduce_fusion
  364.6 0.7 convert_select_fusion
  365.3 0.3 reshape.101
  365.6 0.0 copy-done.3
  365.6 0.0 copy-done.2
  365.6 3.5 fusion.25
  369.1 5.4 add_convert_fusion
  374.5 3.2 fusion.3
  377.7 11.4 %all-to-all-start.1 = ((bf16[64,24,2176]{2,1,0:T(8,128)(2,1)}), bf16[64,24,2176]{2,1,0:T(8,128)(2,1)}, u32[]{:S(2)}, u32[]{:S(2)}) async-start(bf16[64,24,2176]{2,1,0:T(8,128)(2,1)} %bitcast.40), calls=%async_computation.1 | async-start | bytes 13369344 | tf_op jit(solution)/shard_map/all_to_all | solution.py:97
  389.2 0.0 reduce-scatter.6.cloned.1.call-start
  389.2 0.0 copy-done.5
  389.2 8.0 %fusion.10 = f32[2048,384]{1,0:T(8,128)} fusion(bf16[1536,384]{0,1:T(8,128)(2,1)S(1)} %copy-done.5, bf16[1536,4224]{1,0:T(8,128)(2,1)} %bitcast.5), kind=kOutput, calls=%fused_computation.15 | convolution fusion | flops 2415919104 | bytes 10616832 | tf_op jit(solution)/shard_map/dot_general | solution.py:29
  397.2 0.0 reduce-scatter.6.cloned.1.call-update
  397.2 0.4 reduce-scatter.4.cloned.1.call-start
  397.7 0.8 copy-done.4
  398.5 8.0 %fusion.12 = f32[2048,384]{1,0:T(8,128)} fusion(bf16[1536,384]{0,1:T(8,128)(2,1)S(1)} %copy-done.4, bf16[1536,4224]{1,0:T(8,128)(2,1)} %bitcast.5), kind=kOutput, calls=%fused_computation.17 | convolution fusion | flops 2415919104 | bytes 10616832 | tf_op jit(solution)/shard_map/dot_general | solution.py:26
  406.5 0.0 reduce-scatter.4.cloned.1.call-update
  406.5 132.3 %all-to-all-done.1 = bf16[64,24,2176]{2,1,0:T(8,128)(2,1)} async-done(((bf16[64,24,2176]{2,1,0:T(8,128)(2,1)}), bf16[64,24,2176]{2,1,0:T(8,128)(2,1)}, u32[]{:S(2)}, u32[]{:S(2)}) %all-to-all-start.1) | async-done | bytes 6684704 | tf_op jit(solution)/shard_map/all_to_all | solution.py:97
  538.8 1.0 slice.57
  539.9 0.3 copy.44
  540.2 3.4 slice.56
  543.6 0.0 copy-done.7
  543.6 0.3 select_reduce_fusion
  543.9 0.0 copy-done.9
  543.9 0.0 copy-start.1
  543.9 0.6 fusion.42
  544.5 7.9 %fusion.21 = bf16[128,2048]{1,0:T(8,128)(2,1)} fusion(bf16[64,24,2048]{2,1,0:T(8,128)(2,1)S(1)} %slice.56, s32[64,128]{1,0:T(8,128)S(1)} %copy-done.7, pred[64,128]{1,0:T(8,128)(4,1)S(1)} %bitcast.44), kind=kOutput, calls=%fused_computation.24 | convolution fusion | flops 805961728 | bytes 6856704 | tf_op jit(solution)/shard_map/ert,erd->td/dot_general | solution.py:98
  552.4 0.0 copy-done.1
  (10 shorter events, 0.0 us)
Async XLA Ops:
  7.2 2.6 copy-start
  8.8 0.6 copy-start.6
  9.8 1.8 copy-start.8
  18.8 310.9 %all-to-all-start = ((bf16[64,24,4224]{2,1,0:T(8,128)(2,1)}), bf16[64,24,4224]{2,1,0:T(8,128)(2,1)}, u32[]{:S(2)}, u32[]{:S(2)}) async-start(bf16[64,24,4224]{2,1,0:T(8,128)(2,1)} %fusion.2), calls=%async_computation | async-start | bytes 25952256 | tf_op jit(solution)/shard_map/all_to_all | solution.py:83
  32.2 298.7 %all-gather.4.cloned.1.call-start = ((), (), s32[]{:S(2)}) async-start(), calls=%async_computation.5 | async-start | bytes 1966080 | tf_op jit(solution)/shard_map/all_gather | solution.py:78
  33.0 305.3 %all-gather.6.cloned.1.call-start = ((), (), s32[]{:S(2)}) async-start(), calls=%async_computation.6 | async-start | bytes 1966080 | tf_op jit(solution)/shard_map/all_gather | solution.py:77
  33.7 311.8 %all-gather.8.cloned.1.call-start = ((), (), s32[]{:S(2)}) async-start(), calls=%async_computation.7 | async-start | bytes 1966080 | tf_op jit(solution)/shard_map/all_gather | solution.py:76
  34.5 517.9 %reduce-scatter.8.cloned.1.call-start = ((), (), s32[]{:S(2)}) async-start(), calls=%async_computation.10 | async-start | bytes 3932160 | tf_op jit(solution)/shard_map/reduce_scatter | solution.py:111
  345.5 9.7 %copy-start.10 = (f32[1536,384]{0,1:T(8,128)S(1)}, f32[1536,384]{0,1:T(8,128)}, u32[]{:S(2)}) copy-start(f32[1536,384]{0,1:T(8,128)} %fusion.16) | copy-start | bytes 7077892
  355.2 10.3 %copy-start.3 = (bf16[1536,384]{0,1:T(8,128)(2,1)}, bf16[1536,384]{0,1:T(8,128)(2,1)S(1)}, u32[]{:S(2)}) copy-start(bf16[1536,384]{0,1:T(8,128)(2,1)S(1)} %get-tuple-element.29) | copy-start | bytes 3538948
  364.0 1.6 copy-start.2
  377.7 11.5 %copy-start.5 = (bf16[1536,384]{0,1:T(8,128)(2,1)S(1)}, bf16[1536,384]{0,1:T(8,128)(2,1)}, u32[]{:S(2)}) copy-start(bf16[1536,384]{0,1:T(8,128)(2,1)} %get-tuple-element.31) | copy-start | bytes 3538948
  377.7 161.1 %all-to-all-start.1 = ((bf16[64,24,2176]{2,1,0:T(8,128)(2,1)}), bf16[64,24,2176]{2,1,0:T(8,128)(2,1)}, u32[]{:S(2)}, u32[]{:S(2)}) async-start(bf16[64,24,2176]{2,1,0:T(8,128)(2,1)} %bitcast.40), calls=%async_computation.1 | async-start | bytes 13369344 | tf_op jit(solution)/shard_map/all_to_all | solution.py:97
  389.2 163.2 %reduce-scatter.6.cloned.1.call-start = ((), (), s32[]{:S(2)}) async-start(), calls=%async_computation.9 | async-start | bytes 3932160 | tf_op jit(solution)/shard_map/reduce_scatter | solution.py:110
  397.2 1.3 copy-start.4
  397.2 155.2 %reduce-scatter.4.cloned.1.call-start = ((), (), s32[]{:S(2)}) async-start(), calls=%async_computation.8 | async-start | bytes 3932160 | tf_op jit(solution)/shard_map/reduce_scatter | solution.py:109
  540.2 3.4 copy-start.7
  540.2 3.7 copy-start.9
  543.9 8.5 %copy-start.1 = (bf16[128,2048]{1,0:T(8,128)(2,1)S(1)}, bf16[128,2048]{1,0:T(8,128)(2,1)}, u32[]{:S(2)}) copy-start(bf16[128,2048]{1,0:T(8,128)(2,1)} %param.12) | copy-start | bytes 1572868
Sparse Core Ops, SparseCore 0:
  34.9 29.7 all-gather.3
  66.5 29.1 all-gather.5
  97.5 29.1 all-gather.7
  364.1 42.4 reduce-scatter.7
  409.6 40.5 reduce-scatter.5
  453.2 40.5 reduce-scatter.3

commit v2 on v1

v2 whole, which is shorter than its diff:
```python
import jax
import jax.numpy as jnp
from jax import lax
from jax.sharding import PartitionSpec as P


def expert_rows(rows_x, rows_dy, rows_gate, gate_proj, up_proj, down_proj):
    pre_gate = jnp.dot(rows_x, gate_proj, preferred_element_type=jnp.float32)
    pre_up = jnp.dot(rows_x, up_proj, preferred_element_type=jnp.float32)
    gate_sigmoid = jax.nn.sigmoid(pre_gate)
    activated = pre_gate * gate_sigmoid
    hidden = activated * pre_up
    upstream = jnp.dot(rows_dy, down_proj, preferred_element_type=jnp.float32)
    gate_grad = jnp.sum(upstream * hidden, axis=1).astype(jnp.bfloat16)
    weight = rows_gate.astype(jnp.float32)[:, None]
    scaled_hidden = (weight * hidden).astype(jnp.bfloat16)
    hidden_grad = weight * upstream
    pre_gate_grad = (
        hidden_grad * pre_up * gate_sigmoid * (1.0 + pre_gate * (1.0 - gate_sigmoid))
    ).astype(jnp.bfloat16)
    pre_up_grad = (hidden_grad * activated).astype(jnp.bfloat16)
    over_rows = (((0,), (0,)), ((), ()))
    down_grad = lax.dot_general(
        rows_dy, scaled_hidden, over_rows, preferred_element_type=jnp.float32
    )
    gate_wgrad = lax.dot_general(
        rows_x, pre_gate_grad, over_rows, preferred_element_type=jnp.float32
    )
    up_wgrad = lax.dot_general(rows_x, pre_up_grad, over_rows, preferred_element_type=jnp.float32)
    over_hidden = (((1,), (1,)), ((), ()))
    input_rows = lax.dot_general(
        pre_gate_grad, gate_proj, over_hidden, preferred_element_type=jnp.float32
    )
    input_rows = input_rows + lax.dot_general(
        pre_up_grad, up_proj, over_hidden, preferred_element_type=jnp.float32
    )
    return (input_rows.astype(jnp.bfloat16), gate_grad, gate_wgrad, up_wgrad, down_grad)


def local(tokens, cotangent, routes, gates, w_gate, w_up, w_down):
    tokens_dev, top_count = routes.shape
    width = tokens.shape[1]
    hidden_units = w_gate.shape[2]
    cores = lax.axis_size("node")
    planes = lax.axis_size("lz")
    rows_of = lax.axis_size("ly")
    experts = cores * planes * rows_of
    capacity = min(
        tokens_dev,
        max(3 * tokens_dev * top_count // (2 * experts), tokens_dev * top_count // experts),
    )
    near = cores * rows_of
    slots = near * planes * capacity
    pad = 128
    meta = (
        jnp.zeros((tokens_dev, pad), jnp.bfloat16)
        .at[:, :top_count]
        .set(gates)
        .at[:, top_count : 2 * top_count]
        .set(routes.astype(jnp.bfloat16))
    )
    pack = jnp.concatenate([tokens, cotangent, meta], axis=1)
    gathered = lax.all_gather(pack, "lz", axis=0, tiled=False)
    seen_gates = gathered[:, :, 2 * width : 2 * width + top_count]
    seen_routes = gathered[:, :, 2 * width + top_count : 2 * width + 2 * top_count].astype(
        jnp.int32
    )
    plane = lax.axis_index("lz")
    near_ids = jnp.arange(near, dtype=jnp.int32)
    near_experts = (near_ids // rows_of) * (planes * rows_of) + plane * rows_of + near_ids % rows_of
    hit = seen_routes[..., None] == near_experts
    named = jnp.any(hit, axis=2)
    earlier = (
        jnp.arange(tokens_dev)[:, None] > jnp.arange(tokens_dev)[None, :]
    ).astype(jnp.bfloat16)
    rank = jnp.einsum(
        "ts,zsj->jzt", earlier, named.astype(jnp.bfloat16), preferred_element_type=jnp.float32
    ).astype(jnp.int32)
    choose = jnp.transpose(named, (2, 0, 1))[:, :, None, :] & (
        rank[:, :, None, :] == jnp.arange(capacity, dtype=jnp.int32)[None, None, :, None]
    )
    choose_b = choose.astype(jnp.bfloat16)
    send_rows = jnp.einsum(
        "jzrt,ztd->jzrd",
        choose_b,
        gathered[:, :, : 2 * width],
        preferred_element_type=jnp.float32,
    ).astype(jnp.bfloat16)
    gate_tj = jnp.sum(
        jnp.where(hit, seen_gates[..., None], jnp.zeros((), jnp.bfloat16)), axis=2
    )
    send_gate = jnp.sum(
        jnp.where(
            choose, jnp.transpose(gate_tj, (2, 0, 1))[:, :, None, :], jnp.zeros((), jnp.bfloat16)
        ),
        axis=3,
    )
    gate_block = (
        jnp.zeros((near, planes, capacity, pad), jnp.bfloat16).at[..., 0].set(send_gate)
    )
    send = jnp.concatenate([send_rows, gate_block], axis=3)
    all_weights = lax.all_gather(
        jnp.concatenate([w_gate, w_up, w_down], axis=2), "dp", axis=1, tiled=True
    )[0]
    gate_proj = all_weights[:, :hidden_units]
    up_proj = all_weights[:, hidden_units : 2 * hidden_units]
    down_proj = all_weights[:, 2 * hidden_units :]
    recv = lax.all_to_all(send, ("node", "ly"), split_axis=0, concat_axis=0, tiled=True)
    flat = recv.reshape(slots, 2 * width + pad)
    results = expert_rows(
        flat[:, :width],
        flat[:, width : 2 * width],
        flat[:, 2 * width],
        gate_proj,
        up_proj,
        down_proj,
    )
    grad_block = jnp.zeros((slots, pad), jnp.bfloat16).at[:, 0].set(results[1])
    back = jnp.concatenate([results[0], grad_block], axis=1).reshape(
        near, planes, capacity, width + pad
    )
    home = lax.all_to_all(back, ("node", "ly"), split_axis=0, concat_axis=0, tiled=True)
    partial = jnp.einsum(
        "jzrt,jzrd->ztd", choose_b, home[..., :width], preferred_element_type=jnp.float32
    )
    gate_jzt = jnp.sum(
        jnp.where(choose, home[..., width][..., None], jnp.zeros((), jnp.bfloat16)), axis=2
    )
    pick_gate = jnp.sum(
        jnp.where(
            hit, jnp.transpose(gate_jzt, (1, 2, 0))[:, :, None, :], jnp.zeros((), jnp.bfloat16)
        ),
        axis=3,
    )
    gate_cols = (
        jnp.zeros((planes, tokens_dev, pad), jnp.float32)
        .at[..., :top_count]
        .set(pick_gate.astype(jnp.float32))
    )
    reduced = lax.psum_scatter(
        jnp.concatenate([partial, gate_cols], axis=2), "lz", scatter_dimension=0, tiled=True
    )[0]
    input_grad = reduced[:, :width].astype(jnp.bfloat16)
    gate_grad = reduced[:, width : width + top_count].astype(jnp.bfloat16)
    summed = lax.psum_scatter(
        jnp.concatenate([results[2], results[3], results[4]], axis=1),
        "dp",
        scatter_dimension=0,
        tiled=True,
    )
    return (
        input_grad,
        gate_grad,
        summed[None, :, :hidden_units],
        summed[None, :, hidden_units : 2 * hidden_units],
        summed[None, :, 2 * hidden_units :],
    )


def solution(mesh):
    local_size = mesh.shape["local"]
    rows_of = 4 if local_size % 4 == 0 else 1
    split = jax.sharding.Mesh(
        mesh.devices.reshape(
            mesh.shape["dp"], mesh.shape["node"], local_size // rows_of, rows_of
        ),
        ("dp", "node", "lz", "ly"),
    )
    rows = P(("dp", "node", "lz", "ly"), None)
    expert = P(("node", "lz", "ly"), "dp", None)
    return jax.shard_map(
        local,
        mesh=split,
        in_specs=(rows, rows, rows, rows, expert, expert, expert),
        out_specs=(rows, rows, expert, expert, expert),
        check_vma=False,
    )
```

time: 564 us -> 546 us (0.968)
  waiting for transfers between devices: 430 us -> 334 us
  blocking collectives: 0 us -> 78.6 us
  starting transfers between devices: 25.7 us -> 6.63 us
  other arithmetic: 12.8 us -> 30.6 us
  local copies, waits for them, and re-layouts: 7.52 us -> 19.3 us
  matrix products: 69.4 us -> 60.4 us
    all_to_all x2 -> x1, waiting for transfers between devices: 427 us -> 87.3 us  [local(): lax.all_to_all(send, ('node', 'ly'), split_axis=0, concat_axis=0, tiled=T...]
    all_gather x3 -> x2, waiting for transfers between devices: 0.02 us -> 155 us  [the longest x1 101 us: local(): gathered = lax.all_gather(pack, 'lz', axis=0, tiled=False)]
    reduce_scatter x3 -> x2, waiting for transfers between devices: 0.01 us -> 91.6 us  [the longest x1 91.6 us: local(): lax.psum_scatter(jnp.concatenate([partial, gate_cols], axis=2), 'lz', sca...]
    all_to_all x0 -> x1, blocking collectives: none -> 78.6 us  [local(): lax.all_to_all(back, ('node', 'ly'), split_axis=0, concat_axis=0, tiled=T...]
    all_to_all x2 -> x1, starting transfers between devices: 24.9 us -> 6.1 us  [local(): lax.all_to_all(send, ('node', 'ly'), split_axis=0, concat_axis=0, tiled=T...]
    concatenate x1 -> x5, other arithmetic: 5.4 us -> 21.7 us  [the longest x1 7.82 us: local(): jnp.concatenate([results[2], results[3], results[4]], axis=1)]
    unnamed x24 -> x22, local copies, waits for them, and re-layouts: 1.52 us -> 7.82 us
    dot_general x4 -> x3, matrix products: 11.6 us -> 13.6 us  [the longest x1 9.82 us: local(): jnp.einsum('jzrt,ztd->jzrd', choose_b, gathered[:, :, :2 * width], prefer...]
  transfers between devices with their start and end apart: 8 -> 5, of which waited for: 2 -> 4; matrix products, arithmetic and copies ran while one was open for 11% -> 5% of each run, Pallas kernels for 0% -> 0%
where the time goes in v2:
time: 546 us; the launch traced here: 545 us
  waiting for transfers between devices  334 us (61%)
  blocking collectives  78.6 us (14%)
  matrix products  60.4 us (11%)
  other arithmetic  30.6 us (6%)
  local copies, waits for them, and re-layouts  19.3 us (4%)
  between operations  15.9 us (3%)
  starting transfers between devices  6.63 us (1%)
    all_gather x1, waiting for transfers between devices, local(): gathered = lax.all_gather(pack, 'lz', axis=0, tiled=False)  101 us
    reduce_scatter x1, waiting for transfers between devices, local(): lax.psum_scatter(jnp.concatenate([partial, gate_cols], axis=2), 'lz', sca...  91.6 us
    all_to_all x1, waiting for transfers between devices, local(): lax.all_to_all(send, ('node', 'ly'), split_axis=0, concat_axis=0, tiled=T...  87.3 us
    all_to_all x1, blocking collectives, local(): lax.all_to_all(back, ('node', 'ly'), split_axis=0, concat_axis=0, tiled=T...  78.6 us
    all_gather x1, waiting for transfers between devices, local(): lax.all_gather(jnp.concatenate([w_gate, w_up, w_down], axis=2), 'dp', axi...  54.2 us
  transfers between devices with their start and end apart: 5, of which 4 were waited for; matrix products, arithmetic and copies ran while one was open for 5% of the time, Pallas kernels for 0%

profile of v2, /device:TPU:1, one launch (start us, length us, event | category | flops | bytes accessed | tf_op | source)
XLA Modules:
  0.0 545.1 jit_solution(16453981119396134751)
XLA Ops:
  8.0 0.0 all-gather.6.cloned.1.call-start
  8.0 0.6 compare_reduce_fusion.3
  8.7 0.6 compare_reduce_fusion.2
  9.3 0.8 copy.71
  10.1 0.7 convert_element_type.55
  10.8 0.1 copy.72
  10.9 0.7 broadcast_select_fusion.1
  11.6 0.7 broadcast_select_fusion
  12.3 0.4 scatter.21
  12.7 2.3 pad_maximum_fusion.3
  15.0 0.0 all-gather.6.cloned.1.call-update
  15.0 100.5 %all-gather.6.cloned.1.call-done = bf16[1024,4224]{1,0:T(8,128)(2,1)} async-done(((bf16[128,4224]{1,0:T(8,128)(2,1)}), bf16[1024,4224]{1,0:T(8,128)(2,1)}) %all-gather.6.cloned.1.call-update) | async-done | bytes 8650768 | tf_op jit(solution)/shard_map/all_gather | solution.py:63
  115.5 1.2 fusion.50
  116.8 0.1 copy.91
  116.9 0.1 compare_reduce_fusion
  117.0 0.1 fusion.29
  117.2 0.1 copy.74
  117.3 0.1 fusion.42
  117.4 9.8 %convert_bitcast_fusion = bf16[8,8,24,4096]{3,2,0,1:T(8,128)(2,1)} fusion(bf16[8,128,4224]{2,1,0:T(8,128)(2,1)} %bitcast.53, s32[8,8,128]{2,0,1:T(8,128)S(1)} %fusion.29, pred[8,8,128]{2,0,1:T(8,128)(4,1)S(1)} %bitcast.44), kind=kOutput, calls=%fused_computation.6 | convolution fusion | flops 1617297408 | bytes 21012480 | tf_op jit(solution)/shard_map/jzrt,ztd->jzrd/dot_general | solution.py:83
  127.2 0.3 fusion.36
  127.6 0.5 copy.76
  128.0 6.2 %fusion.2 = bf16[8,8,24,4224]{3,2,0,1:T(8,128)(2,1)S(1)} fusion(bf16[8,8,24,1]{3,2,0,1:T(8,128)(2,1)S(1)} %copy.76, bf16[8,8,24,4096]{3,2,0,1:T(8,128)(2,1)} %convert_bitcast_fusion), kind=kLoop, calls=%fused_computation.4 | loop fusion | flops 38928384 | bytes 25562112 | tf_op jit(solution)/shard_map/concatenate | solution.py:101
  134.3 5.5 %copy.77 = bf16[8,8,24,4224]{3,2,1,0:T(8,128)(2,1)} copy(bf16[8,8,24,4224]{3,2,0,1:T(8,128)(2,1)S(1)} %fusion.2) | data formatting | bytes 25952256 | tf_op jit(solution)/shard_map/concatenate | solution.py:101
  139.8 6.1 %all-to-all-start = ((bf16[8,8,24,4224]{3,2,1,0:T(8,128)(2,1)}), bf16[8,8,24,4224]{3,2,1,0:T(8,128)(2,1)}, u32[]{:S(2)}, u32[]{:S(2)}) async-start(bf16[8,8,24,4224]{3,2,1,0:T(8,128)(2,1)} %copy.77), calls=%async_computation | async-start | bytes 25952256 | tf_op jit(solution)/shard_map/all_to_all | solution.py:108
  145.9 1.1 pad_maximum_fusion.2
  147.0 0.0 all-gather.4.cloned.1.call-update
  147.1 0.2 reduce-scatter.5.cloned.1.call-start
  147.3 54.2 %all-gather.4.cloned.1.call-done = bf16[1,2048,1152]{2,1,0:T(8,128)(2,1)} async-done(((bf16[1,512,1152]{2,1,0:T(8,128)(2,1)}), bf16[1,2048,1152]{2,1,0:T(8,128)(2,1)}) %all-gather.4.cloned.1.call-update) | async-done | bytes 4718608 | tf_op jit(solution)/shard_map/all_gather | solution.py:102
  201.5 87.3 %all-to-all-done = bf16[8,8,24,4224]{3,2,1,0:T(8,128)(2,1)} async-done(((bf16[8,8,24,4224]{3,2,1,0:T(8,128)(2,1)}), bf16[8,8,24,4224]{3,2,1,0:T(8,128)(2,1)}, u32[]{:S(2)}, u32[]{:S(2)}) %all-to-all-start) | async-done | bytes 12976160 | tf_op jit(solution)/shard_map/all_to_all | solution.py:108
  288.8 5.4 fusion.19
  294.2 4.9 fusion.8
  299.0 1.2 convert_reduce_fusion
  300.2 6.0 %multiply_convert_fusion.2 = (bf16[1536,384]{0,1:T(8,128)(2,1)S(1)}, bf16[1536]{0:T(1024)(128)(2,1)S(1)}, bf16[1536,384]{0,1:T(8,128)(2,1)S(1)}, f32[1536,384]{0,1:T(8,128)S(1)}) fusion(f32[1536,384]{0,1:T(8,128)S(1)} %fusion.19, f32[1536,384]{0,1:T(8,128)S(1)} %fusion.8, f32[1536]{0:T(1024)S(1)} %convert_reduce_fusion, ...), kind=kOutput, calls=%fused_computation.29 | convolution fusion | flops 2425944576 | bytes 17312768 | tf_op jit(solution)/shard_map/dot_general | solution.py:8
  306.2 5.9 %fusion.6 = f32[2048,384]{0,1:T(8,128)S(1)} fusion(bf16[1536,4224]{1,0:T(8,128)(2,1)} %bitcast.9, f32[1536]{0:T(1024)S(1)} %convert_reduce_fusion, f32[1536,384]{0,1:T(8,128)S(1)} %fusion.19, f32[1536,384]{0,1:T(8,128)S(1)} %get-tuple-element.103), kind=kOutput, calls=%fused_computation.13 | convolution fusion | flops 2420047872 | bytes 14161920 | tf_op jit(solution)/shard_map/dot_general | solution.py:23
  312.2 7.2 %fusion.13 = f32[2048,384]{0,1:T(8,128)} fusion(bf16[1536,384]{0,1:T(8,128)(2,1)S(1)} %get-tuple-element.97, bf16[1536,4224]{1,0:T(8,128)(2,1)} %bitcast.9), kind=kOutput, calls=%fused_computation.18 | convolution fusion | flops 2415919104 | bytes 10616832 | tf_op jit(solution)/shard_map/dot_general | solution.py:26
  319.3 7.1 %fusion.15 = f32[2048,384]{0,1:T(8,128)} fusion(bf16[1536,384]{0,1:T(8,128)(2,1)S(1)} %get-tuple-element.99, bf16[1536,4224]{1,0:T(8,128)(2,1)} %bitcast.9), kind=kOutput, calls=%fused_computation.20 | convolution fusion | flops 2415919104 | bytes 10616832 | tf_op jit(solution)/shard_map/dot_general | solution.py:29
  326.5 7.8 %pad_maximum_fusion = f32[2048,1152]{0,1:T(8,128)} fusion(f32[2048,384]{0,1:T(8,128)S(1)} %fusion.6, f32[2048,384]{0,1:T(8,128)} %fusion.15, f32[2048,384]{0,1:T(8,128)} %fusion.13), kind=kLoop, calls=%fused_computation.7 | loop fusion | flops 4718592 | bytes 18874368 | tf_op jit(solution)/shard_map/concatenate | solution.py:146
  334.3 0.0 reduce-scatter.5.cloned.1.call-update
  334.3 0.3 reduce-scatter.3.cloned.1.call-start
  334.6 0.6 compare_reduce_fusion.1
  335.3 0.7 convert_select_fusion
  335.9 0.3 reshape.207
  336.2 4.9 fusion.23
  341.1 5.4 add_convert_fusion
  346.5 0.6 fusion.3
  347.1 78.6 %all_to_all.10 = bf16[8,8,24,2176]{3,2,1,0:T(8,128)(2,1)S(1)} all-to-all(bf16[8,8,24,2176]{3,2,1,0:T(8,128)(2,1)S(1)} %bitcast.38), channel_id=1, replica_groups=mesh['dp'=4,'node'=2,'lz'=8,'ly'=4] {'node','ly'}, dimensions={0} | all-to-all | bytes 13369344 | tf_op jit(solution)/shard_map/all_to_all | solution.py:122
  425.7 2.8 copy-done
  428.5 0.1 slice.168
  428.6 0.5 copy.94
  429.0 0.4 fusion.37
  429.4 0.2 fusion.43
  429.6 0.2 copy.82
  429.8 3.7 fusion.10
  433.5 4.3 pad_maximum_fusion.1
  437.8 0.0 reduce-scatter.3.cloned.1.call-update
  437.8 0.0 reduce-scatter.5.cloned.1.call-done
  437.8 1.8 slice_bitcast_fusion.2
  439.7 1.1 copy.84
  440.8 1.1 copy.85
  442.0 1.1 copy.86
  443.1 91.6 %reduce-scatter.3.cloned.1.call-done = f32[1,128,2176]{2,1,0:T(8,128)} async-done(((f32[8,128,2176]{2,1,0:T(8,128)}), f32[1,128,2176]{2,1,0:T(8,128)}) %reduce-scatter.3.cloned.1.call-update) | async-done | bytes 1114128 | tf_op jit(solution)/shard_map/reduce_scatter | solution.py:140
  534.7 1.3 convert_bitcast_fusion.1
  536.0 0.8 slice.169
  536.9 0.7 copy.83
  (21 shorter events, 0.1 us)
Async XLA Ops:
  8.0 107.5 %all-gather.6.cloned.1.call-start = ((), (), s32[]{:S(2)}) async-start(), calls=%async_computation.7 | async-start | bytes 9732096 | tf_op jit(solution)/shard_map/all_gather | solution.py:63
  139.8 6.1 %copy-start.5 = (bf16[1,512,384]{2,1,0:T(8,128)(2,1)S(1)}, bf16[1,512,384]{2,1,0:T(8,128)(2,1)}, u32[]{:S(2)}) copy-start(bf16[1,512,384]{2,1,0:T(8,128)(2,1)} %param.23) | copy-start | bytes 1179652
  139.8 6.1 %copy-start.6 = (bf16[1,512,384]{2,1,0:T(8,128)(2,1)S(1)}, bf16[1,512,384]{2,1,0:T(8,128)(2,1)}, u32[]{:S(2)}) copy-start(bf16[1,512,384]{2,1,0:T(8,128)(2,1)} %param.22) | copy-start | bytes 1179652
  139.8 6.1 %copy-start.7 = (bf16[1,512,384]{2,1,0:T(8,128)(2,1)S(1)}, bf16[1,512,384]{2,1,0:T(8,128)(2,1)}, u32[]{:S(2)}) copy-start(bf16[1,512,384]{2,1,0:T(8,128)(2,1)} %param.21) | copy-start | bytes 1179652
  139.8 149.0 %all-to-all-start = ((bf16[8,8,24,4224]{3,2,1,0:T(8,128)(2,1)}), bf16[8,8,24,4224]{3,2,1,0:T(8,128)(2,1)}, u32[]{:S(2)}, u32[]{:S(2)}) async-start(bf16[8,8,24,4224]{3,2,1,0:T(8,128)(2,1)} %copy.77), calls=%async_computation | async-start | bytes 25952256 | tf_op jit(solution)/shard_map/all_to_all | solution.py:108
  145.9 55.6 %all-gather.4.cloned.1.call-start = ((), (), s32[]{:S(2)}) async-start(), calls=%async_computation.4 | async-start | bytes 5898240 | tf_op jit(solution)/shard_map/all_gather | solution.py:102
  147.1 290.8 %reduce-scatter.5.cloned.1.call-start = ((), (), s32[]{:S(2)}) async-start(), calls=%async_computation.6 | async-start | bytes 11796480 | tf_op jit(solution)/shard_map/reduce_scatter | solution.py:145
  288.8 5.4 copy-start.1
  306.2 6.0 %copy-start.3 = (bf16[1536,384]{0,1:T(8,128)(2,1)}, bf16[1536,384]{0,1:T(8,128)(2,1)S(1)}, u32[]{:S(2)}) copy-start(bf16[1536,384]{0,1:T(8,128)(2,1)S(1)} %get-tuple-element.97) | copy-start | bytes 3538948
  306.2 13.1 %copy-start.2 = (bf16[1536,384]{0,1:T(8,128)(2,1)}, bf16[1536,384]{0,1:T(8,128)(2,1)S(1)}, u32[]{:S(2)}) copy-start(bf16[1536,384]{0,1:T(8,128)(2,1)S(1)} %get-tuple-element.99) | copy-start | bytes 3538948
  334.3 1.9 copy-start.4
  334.3 200.4 %reduce-scatter.3.cloned.1.call-start = ((), (), s32[]{:S(2)}) async-start(), calls=%async_computation.5 | async-start | bytes 10027008 | tf_op jit(solution)/shard_map/reduce_scatter | solution.py:140
  425.7 2.8 copy-start
Sparse Core Ops, SparseCore 0:
  15.1 100.3 all-gather.5
Sparse Core Ops, SparseCore 1:
  148.1 53.3 all-gather.3
  334.4 88.4 reduce-scatter.4
  437.9 96.8 reduce-scatter.2

commit v3 on v2

v3 whole, which is shorter than its diff:
```python
import jax
import jax.numpy as jnp
from jax import lax
from jax.sharding import PartitionSpec as P


def expert_rows(rows_x, rows_dy, rows_gate, gate_proj, up_proj, down_proj):
    pre_gate = jnp.dot(rows_x, gate_proj, preferred_element_type=jnp.float32)
    pre_up = jnp.dot(rows_x, up_proj, preferred_element_type=jnp.float32)
    gate_sigmoid = jax.nn.sigmoid(pre_gate)
    activated = pre_gate * gate_sigmoid
    hidden = activated * pre_up
    upstream = jnp.dot(rows_dy, down_proj, preferred_element_type=jnp.float32)
    gate_grad = jnp.sum(upstream * hidden, axis=1).astype(jnp.bfloat16)
    weight = rows_gate.astype(jnp.float32)[:, None]
    scaled_hidden = (weight * hidden).astype(jnp.bfloat16)
    hidden_grad = weight * upstream
    pre_gate_grad = (
        hidden_grad * pre_up * gate_sigmoid * (1.0 + pre_gate * (1.0 - gate_sigmoid))
    ).astype(jnp.bfloat16)
    pre_up_grad = (hidden_grad * activated).astype(jnp.bfloat16)
    over_hidden = (((1,), (1,)), ((), ()))
    input_rows = lax.dot_general(
        pre_gate_grad, gate_proj, over_hidden, preferred_element_type=jnp.float32
    )
    input_rows = input_rows + lax.dot_general(
        pre_up_grad, up_proj, over_hidden, preferred_element_type=jnp.float32
    )
    return input_rows.astype(jnp.bfloat16), gate_grad, pre_gate_grad, pre_up_grad, scaled_hidden


def weight_grads(rows_x, rows_dy, pre_gate_grad, pre_up_grad, scaled_hidden):
    over_rows = (((0,), (0,)), ((), ()))
    down_grad = lax.dot_general(
        rows_dy, scaled_hidden, over_rows, preferred_element_type=jnp.float32
    )
    gate_wgrad = lax.dot_general(
        rows_x, pre_gate_grad, over_rows, preferred_element_type=jnp.float32
    )
    up_wgrad = lax.dot_general(rows_x, pre_up_grad, over_rows, preferred_element_type=jnp.float32)
    return gate_wgrad, up_wgrad, down_grad


def local(tokens, cotangent, routes, gates, w_gate, w_up, w_down):
    tokens_dev, top_count = routes.shape
    width = tokens.shape[1]
    hidden_units = w_gate.shape[2]
    cores = lax.axis_size("node")
    planes = lax.axis_size("lz")
    rows_of = lax.axis_size("ly")
    experts = cores * planes * rows_of
    capacity = min(
        tokens_dev,
        max(3 * tokens_dev * top_count // (2 * experts), tokens_dev * top_count // experts),
    )
    near = cores * rows_of
    pad = 128
    meta = (
        jnp.zeros((tokens_dev, pad), jnp.bfloat16)
        .at[:, :top_count]
        .set(gates)
        .at[:, top_count : 2 * top_count]
        .set(routes.astype(jnp.bfloat16))
    )
    pack = jnp.concatenate([tokens, cotangent, meta], axis=1)
    all_weights = lax.all_gather(
        jnp.concatenate([w_gate, w_up, w_down], axis=2), "dp", axis=1, tiled=True
    )[0]
    gate_proj = all_weights[:, :hidden_units]
    up_proj = all_weights[:, hidden_units : 2 * hidden_units]
    down_proj = all_weights[:, 2 * hidden_units :]
    plane = lax.axis_index("lz")
    near_ids = jnp.arange(near, dtype=jnp.int32)
    near_experts = (near_ids // rows_of) * (planes * rows_of) + plane * rows_of + near_ids % rows_of
    earlier = (
        jnp.arange(tokens_dev)[:, None] > jnp.arange(tokens_dev)[None, :]
    ).astype(jnp.bfloat16)
    to_right = [(i, (i + 1) % planes) for i in range(planes)]
    to_left = [(i, (i - 1) % planes) for i in range(planes)]
    rounds = [([0], [pack])]
    right, left = pack, pack
    for step in range(1, (planes - 1) // 2 + 1):
        right = lax.ppermute(right, "lz", to_right)
        left = lax.ppermute(left, "lz", to_left)
        rounds.append(([-step, step], [right, left]))
    if planes % 2 == 0 and planes > 1:
        right = lax.ppermute(right, "lz", to_right)
        rounds.append(([planes // 2], [right]))
    partial_of = {}
    kept = []
    for offsets, packs in rounds:
        count = len(offsets)
        seen = jnp.stack(packs)
        seen_gates = seen[:, :, 2 * width : 2 * width + top_count]
        seen_routes = seen[:, :, 2 * width + top_count : 2 * width + 2 * top_count].astype(
            jnp.int32
        )
        hit = seen_routes[..., None] == near_experts
        named = jnp.any(hit, axis=2)
        rank = jnp.einsum(
            "ts,zsj->jzt",
            earlier,
            named.astype(jnp.bfloat16),
            preferred_element_type=jnp.float32,
        ).astype(jnp.int32)
        choose = jnp.transpose(named, (2, 0, 1))[:, :, None, :] & (
            rank[:, :, None, :] == jnp.arange(capacity, dtype=jnp.int32)[None, None, :, None]
        )
        choose_b = choose.astype(jnp.bfloat16)
        send_rows = jnp.einsum(
            "jzrt,ztd->jzrd",
            choose_b,
            seen[:, :, : 2 * width],
            preferred_element_type=jnp.float32,
        ).astype(jnp.bfloat16)
        gate_tj = jnp.sum(
            jnp.where(hit, seen_gates[..., None], jnp.zeros((), jnp.bfloat16)), axis=2
        )
        send_gate = jnp.sum(
            jnp.where(
                choose,
                jnp.transpose(gate_tj, (2, 0, 1))[:, :, None, :],
                jnp.zeros((), jnp.bfloat16),
            ),
            axis=3,
        )
        gate_block = (
            jnp.zeros((near, count, capacity, pad), jnp.bfloat16).at[..., 0].set(send_gate)
        )
        send = jnp.concatenate([send_rows, gate_block], axis=3)
        recv = lax.all_to_all(send, ("node", "ly"), split_axis=0, concat_axis=0, tiled=True)
        flat = recv.reshape(near * count * capacity, 2 * width + pad)
        rows_x = flat[:, :width]
        rows_dy = flat[:, width : 2 * width]
        results = expert_rows(
            rows_x, rows_dy, flat[:, 2 * width], gate_proj, up_proj, down_proj
        )
        kept.append((rows_x, rows_dy) + results[2:])
        grad_block = (
            jnp.zeros((near * count * capacity, pad), jnp.bfloat16).at[:, 0].set(results[1])
        )
        back = jnp.concatenate([results[0], grad_block], axis=1).reshape(
            near, count, capacity, width + pad
        )
        home = lax.all_to_all(back, ("node", "ly"), split_axis=0, concat_axis=0, tiled=True)
        partial = jnp.einsum(
            "jzrt,jzrd->ztd", choose_b, home[..., :width], preferred_element_type=jnp.float32
        )
        gate_jzt = jnp.sum(
            jnp.where(choose, home[..., width][..., None], jnp.zeros((), jnp.bfloat16)),
            axis=2,
        )
        pick_gate = jnp.sum(
            jnp.where(
                hit,
                jnp.transpose(gate_jzt, (1, 2, 0))[:, :, None, :],
                jnp.zeros((), jnp.bfloat16),
            ),
            axis=3,
        )
        gate_cols = (
            jnp.zeros((count, tokens_dev, pad), jnp.float32)
            .at[..., :top_count]
            .set(pick_gate.astype(jnp.float32))
        )
        joined = jnp.concatenate([partial, gate_cols], axis=2)
        for index, offset in enumerate(offsets):
            partial_of[offset % planes] = joined[index]
    stacked = jnp.stack([partial_of[m] for m in range(planes)])
    ordered = jnp.roll(stacked, plane, axis=0)
    reduced = lax.psum_scatter(ordered, "lz", scatter_dimension=0, tiled=True)[0]
    input_grad = reduced[:, :width].astype(jnp.bfloat16)
    gate_grad = reduced[:, width : width + top_count].astype(jnp.bfloat16)
    all_rows = [jnp.concatenate(parts, axis=0) for parts in zip(*kept)]
    grads = weight_grads(*all_rows)
    summed = lax.psum_scatter(
        jnp.concatenate(grads, axis=1), "dp", scatter_dimension=0, tiled=True
    )
    return (
        input_grad,
        gate_grad,
        summed[None, :, :hidden_units],
        summed[None, :, hidden_units : 2 * hidden_units],
        summed[None, :, 2 * hidden_units :],
    )


def solution(mesh):
    local_size = mesh.shape["local"]
    rows_of = 4 if local_size % 4 == 0 else 1
    split = jax.sharding.Mesh(
        mesh.devices.reshape(
            mesh.shape["dp"], mesh.shape["node"], local_size // rows_of, rows_of
        ),
        ("dp", "node", "lz", "ly"),
    )
    rows = P(("dp", "node", "lz", "ly"), None)
    expert = P(("node", "lz", "ly"), "dp", None)
    return jax.shard_map(
        local,
        mesh=split,
        in_specs=(rows, rows, rows, rows, expert, expert, expert),
        out_specs=(rows, rows, expert, expert, expert),
        check_vma=False,
    )
```

time: 546 us -> 636 us (1.16); the launches traced: 545 us -> 623 us
  blocking collectives: 78.6 us -> 0 us
  starting transfers between devices: 6.63 us -> 57 us
  waiting for transfers between devices: 334 us -> 368 us
  local copies, waits for them, and re-layouts: 19.3 us -> 46.9 us
  other arithmetic: 30.6 us -> 55.9 us
  matrix products: 60.4 us -> 80.7 us
    all_gather x1 -> x0, waiting for transfers between devices: 101 us -> none  [local(): gathered = lax.all_gather(pack, 'lz', axis=0, tiled=False)]
    ppermute x0 -> x7, waiting for transfers between devices: none -> 92 us  [the longest x4 92 us: local(): right = lax.ppermute(right, 'lz', to_right)]
    all_to_all x1 -> x0, blocking collectives: 78.6 us -> none  [local(): lax.all_to_all(back, ('node', 'ly'), split_axis=0, concat_axis=0, tiled=T...]
    all_to_all x0 -> x5, waiting for transfers between devices: none -> 54.4 us  [local(): lax.all_to_all(back, ('node', 'ly'), split_axis=0, concat_axis=0, tiled=T...]
    all_gather x1, waiting for transfers between devices: 54.2 us -> 0.01 us  [local(): lax.all_gather(jnp.concatenate([w_gate, w_up, w_down], axis=2), 'dp', axi...]
    all_to_all x1 -> x5, waiting for transfers between devices: 87.3 us -> 129 us  [local(): lax.all_to_all(send, ('node', 'ly'), split_axis=0, concat_axis=0, tiled=T...]
    all_to_all x0 -> x5, starting transfers between devices: none -> 20.6 us  [local(): lax.all_to_all(back, ('node', 'ly'), split_axis=0, concat_axis=0, tiled=T...]
    all_to_all x1 -> x5, starting transfers between devices: 6.1 us -> 25.4 us  [local(): lax.all_to_all(send, ('node', 'ly'), split_axis=0, concat_axis=0, tiled=T...]
  transfers between devices with their start and end apart: 5 -> 20, of which waited for: 4 -> 15; matrix products, arithmetic and copies ran while one was open for 5% -> 20% of each run, Pallas kernels for 0% -> 0%
where the time goes in v3:
time: 636 us; the launch traced here: 623 us
  waiting for transfers between devices  368 us (58%)
  matrix products  80.7 us (13%)
  starting transfers between devices  57 us (9%)
  other arithmetic  55.9 us (9%)
  local copies, waits for them, and re-layouts  46.9 us (7%)
  between operations  15.3 us (2%)
    all_to_all x5, waiting for transfers between devices, local(): lax.all_to_all(send, ('node', 'ly'), split_axis=0, concat_axis=0, tiled=T...  129 us
    reduce_scatter x1, waiting for transfers between devices, local(): lax.psum_scatter(ordered, 'lz', scatter_dimension=0, tiled=True)[0]  92.1 us
    ppermute x4, waiting for transfers between devices, local(): right = lax.ppermute(right, 'lz', to_right)  92 us
    all_to_all x5, waiting for transfers between devices, local(): lax.all_to_all(back, ('node', 'ly'), split_axis=0, concat_axis=0, tiled=T...  54.4 us
    all_to_all x5, starting transfers between devices, local(): lax.all_to_all(send, ('node', 'ly'), split_axis=0, concat_axis=0, tiled=T...  25.4 us
    unnamed x149, local copies, waits for them, and re-layouts  25 us
    all_to_all x5, starting transfers between devices, local(): lax.all_to_all(back, ('node', 'ly'), split_axis=0, concat_axis=0, tiled=T...  20.6 us
    unnamed x17, other arithmetic  16.3 us
  transfers between devices with their start and end apart: 20, of which 15 were waited for; matrix products, arithmetic and copies ran while one was open for 20% of the time, Pallas kernels for 0%

profile of v3, /device:TPU:1, one launch (start us, length us, event | category | flops | bytes accessed | tf_op | source)
XLA Modules:
  0.0 623.5 jit_solution(18182547965577443301)
XLA Ops:
  12.7 2.5 collective-permute-start
  15.2 27.5 %collective-permute-done = bf16[128,4224]{0,1:T(8,128)(2,1)S(1)} collective-permute-done((bf16[128,4224]{0,1:T(8,128)(2,1)S(1)}, bf16[128,4224]{0,1:T(8,128)(2,1)S(1)}, u32[]{:S(2)}, u32[]{:S(2)}) %collective-permute-start) | collective-permute-done | bytes 1081376 | tf_op jit(solution)/shard_map/ppermute | solution.py:83
  42.8 2.7 collective-permute-start.1
  45.4 22.7 %collective-permute-done.2 = bf16[128,4224]{0,1:T(8,128)(2,1)S(1)} collective-permute-done((bf16[128,4224]{0,1:T(8,128)(2,1)S(1)}, bf16[128,4224]{0,1:T(8,128)(2,1)S(1)}, u32[]{:S(2)}, u32[]{:S(2)}) %collective-permute-start.2) | collective-permute-done | bytes 1081376 | tf_op jit(solution)/shard_map/ppermute | solution.py:83
  68.1 2.7 collective-permute-start.3
  70.8 21.7 %collective-permute-done.4 = bf16[128,4224]{0,1:T(8,128)(2,1)S(1)} collective-permute-done((bf16[128,4224]{0,1:T(8,128)(2,1)S(1)}, bf16[128,4224]{0,1:T(8,128)(2,1)S(1)}, u32[]{:S(2)}, u32[]{:S(2)}) %collective-permute-start.4) | collective-permute-done | bytes 1081376 | tf_op jit(solution)/shard_map/ppermute | solution.py:83
  93.3 2.7 collective-permute-start.5
  96.0 20.1 %collective-permute-done.6 = bf16[128,4224]{0,1:T(8,128)(2,1)} collective-permute-done((bf16[128,4224]{0,1:T(8,128)(2,1)S(1)}, bf16[128,4224]{0,1:T(8,128)(2,1)}, u32[]{:S(2)}, u32[]{:S(2)}) %collective-permute-start.6) | collective-permute-done | bytes 1081376 | tf_op jit(solution)/shard_map/ppermute | solution.py:87
  119.3 8.5 %all-to-all-start = ((bf16[8,1,24,4224]{3,2,1,0:T(8,128)(2,1)}), bf16[8,1,24,4224]{3,2,1,0:T(8,128)(2,1)S(1)}, u32[]{:S(2)}, u32[]{:S(2)}) async-start(bf16[8,1,24,4224]{3,2,1,0:T(8,128)(2,1)} %fusion.33), calls=%async_computation | async-start | bytes 3244032 | tf_op jit(solution)/shard_map/all_to_all | solution.py:131
  132.8 16.1 %all-to-all-done = bf16[8,1,24,4224]{3,2,1,0:T(8,128)(2,1)S(1)} async-done(((bf16[8,1,24,4224]{3,2,1,0:T(8,128)(2,1)}), bf16[8,1,24,4224]{3,2,1,0:T(8,128)(2,1)S(1)}, u32[]{:S(2)}, u32[]{:S(2)}) %all-to-all-start) | async-done | bytes 1622048 | tf_op jit(solution)/shard_map/all_to_all | solution.py:131
  148.9 3.9 all-to-all-start.8
  153.4 2.5 fusion.3
  156.2 1.9 copy.139
  158.1 15.7 %all-to-all-done.8 = bf16[8,1,24,4224]{3,2,1,0:T(8,128)(2,1)S(1)} async-done(((bf16[8,1,24,4224]{3,2,1,0:T(8,128)(2,1)}), bf16[8,1,24,4224]{3,2,1,0:T(8,128)(2,1)S(1)}, u32[]{:S(2)}, u32[]{:S(2)}) %all-to-all-start.8) | async-done | bytes 1622048 | tf_op jit(solution)/shard_map/all_to_all | solution.py:131
  175.1 3.9 all-to-all-start.2
  179.5 2.5 fusion.4
  182.4 1.9 copy.146
  184.2 33.3 %all-to-all-done.2 = bf16[8,2,24,4224]{3,2,1,0:T(8,128)(2,1)S(1)} async-done(((bf16[8,2,24,4224]{3,2,1,0:T(8,128)(2,1)}), bf16[8,2,24,4224]{3,2,1,0:T(8,128)(2,1)S(1)}, u32[]{:S(2)}, u32[]{:S(2)}) %all-to-all-start.2) | async-done | bytes 3244064 | tf_op jit(solution)/shard_map/all_to_all | solution.py:131
  217.6 4.7 all-to-all-start.4
  222.3 2.3 pad_maximum_fusion.1
  225.1 2.5 fusion.5
  227.9 2.0 copy.153
  229.9 31.3 %all-to-all-done.4 = bf16[8,2,24,4224]{3,2,1,0:T(8,128)(2,1)} async-done(((bf16[8,2,24,4224]{3,2,1,0:T(8,128)(2,1)}), bf16[8,2,24,4224]{3,2,1,0:T(8,128)(2,1)}, u32[]{:S(2)}, u32[]{:S(2)}) %all-to-all-start.4) | async-done | bytes 3244064 | tf_op jit(solution)/shard_map/all_to_all | solution.py:131
  261.2 4.4 all-to-all-start.6
  267.8 2.8 slice_dynamic-update-slice_fusion.9
  271.7 32.5 %all-to-all-done.6 = bf16[8,2,24,4224]{3,2,1,0:T(8,128)(2,1)} async-done(((bf16[8,2,24,4224]{3,2,1,0:T(8,128)(2,1)}), bf16[8,2,24,4224]{3,2,1,0:T(8,128)(2,1)}, u32[]{:S(2)}, u32[]{:S(2)}) %all-to-all-start.6) | async-done | bytes 3244064 | tf_op jit(solution)/shard_map/all_to_all | solution.py:131
  305.2 2.2 slice_dynamic-update-slice_fusion.5
  307.4 4.1 slice_dynamic-update-slice_fusion.4
  311.4 4.1 slice_dynamic-update-slice_fusion.3
  316.9 3.0 fusion.39
  320.2 2.6 fusion.47
  322.8 2.6 fusion.41
  325.4 2.6 fusion.51
  336.1 2.2 constant_dynamic-update-slice_fusion.3
  338.3 3.8 constant_dynamic-update-slice_fusion.2
  342.1 3.8 constant_dynamic-update-slice_fusion.1
  346.2 3.0 fusion.213
  349.3 4.5 fusion.214
  353.7 4.5 fusion.215
  358.2 7.9 %pad_maximum_fusion = f32[2048,1152]{0,1:T(8,128)} fusion(f32[2048,384]{0,1:T(8,128)} %fusion.215, f32[2048,384]{0,1:T(8,128)} %fusion.214, f32[2048,384]{0,1:T(8,128)S(1)} %fusion.213), kind=kLoop, calls=%fused_computation | loop fusion | flops 4718592 | bytes 18874368 | tf_op jit(solution)/shard_map/concatenate | solution.py:177
  368.2 2.1 fusion.199
  370.3 2.1 fusion.16
  373.5 4.5 all-to-all-start.1
  379.0 2.1 fusion.187
  381.1 2.2 fusion.17
  384.2 2.4 fusion.193
  387.6 3.5 all-to-all-done.1
  391.1 4.2 all-to-all-start.9
  395.3 2.4 add_convert_fusion.1
  399.0 9.4 %all-to-all-done.9 = bf16[8,1,24,2176]{3,2,1,0:T(8,128)(2,1)} async-done(((bf16[8,1,24,2176]{3,2,1,0:T(8,128)(2,1)}), bf16[8,1,24,2176]{3,2,1,0:T(8,128)(2,1)}, u32[]{:S(2)}, u32[]{:S(2)}) %all-to-all-start.9) | async-done | bytes 835616 | tf_op jit(solution)/shard_map/all_to_all | solution.py:145
  408.4 3.8 all-to-all-start.5
  413.4 2.7 fusion.196
  416.1 2.6 add_convert_fusion.2
  420.0 14.3 %all-to-all-done.5 = bf16[8,2,24,2176]{3,2,1,0:T(8,128)(2,1)S(1)} async-done(((bf16[8,2,24,2176]{3,2,1,0:T(8,128)(2,1)}), bf16[8,2,24,2176]{3,2,1,0:T(8,128)(2,1)S(1)}, u32[]{:S(2)}, u32[]{:S(2)}) %all-to-all-start.5) | async-done | bytes 1671200 | tf_op jit(solution)/shard_map/all_to_all | solution.py:145
  434.3 3.5 all-to-all-start.3
  440.3 2.5 fusion.190
  442.9 2.4 add_convert_fusion
  448.6 10.9 %all-to-all-done.3 = bf16[8,2,24,2176]{3,2,1,0:T(8,128)(2,1)S(1)} async-done(((bf16[8,2,24,2176]{3,2,1,0:T(8,128)(2,1)}), bf16[8,2,24,2176]{3,2,1,0:T(8,128)(2,1)S(1)}, u32[]{:S(2)}, u32[]{:S(2)}) %all-to-all-start.3) | async-done | bytes 1671200 | tf_op jit(solution)/shard_map/all_to_all | solution.py:145
  459.4 4.6 all-to-all-start.7
  469.3 16.5 %all-to-all-done.7 = bf16[8,2,24,2176]{3,2,1,0:T(8,128)(2,1)} async-done(((bf16[8,2,24,2176]{3,2,1,0:T(8,128)(2,1)}), bf16[8,2,24,2176]{3,2,1,0:T(8,128)(2,1)}, u32[]{:S(2)}, u32[]{:S(2)}) %all-to-all-start.7) | async-done | bytes 1671200 | tf_op jit(solution)/shard_map/all_to_all | solution.py:145
  487.9 2.0 convolution_bitcast_fusion.1
  490.5 1.9 convolution_bitcast_fusion
  508.7 7.6 %constant_dynamic-slice_fusion = f32[8,128,2176]{2,1,0:T(8,128)} fusion(f32[16,128,2176]{2,1,0:T(8,128)} %fusion.93, s32[]{:T(128)S(6)} %select_n.183), kind=kLoop, calls=%fused_computation.323 | loop fusion | bytes 17825796 | tf_op jit(solution)/shard_map/jit(_roll_dynamic)/dynamic_slice | solution.py:170
  521.6 92.1 %reduce-scatter.3.cloned.1.call-done = f32[1,128,2176]{2,1,0:T(8,128)} async-done(((f32[8,128,2176]{2,1,0:T(8,128)}), f32[1,128,2176]{2,1,0:T(8,128)}) %reduce-scatter.3.cloned.1.call-update) | async-done | bytes 1114128 | tf_op jit(solution)/shard_map/reduce_scatter | solution.py:171
  (280 shorter events, 79.7 us)
Async XLA Ops:
  7.2 4.7 copy-start.61
  12.7 30.1 %collective-permute-start = (bf16[128,4224]{0,1:T(8,128)(2,1)S(1)}, bf16[128,4224]{0,1:T(8,128)(2,1)S(1)}, u32[]{:S(2)}, u32[]{:S(2)}) collective-permute-start(bf16[128,4224]{0,1:T(8,128)(2,1)S(1)} %get-tuple-element.302), channel_id=1, source_target_pairs={{0,4},{4,8},{8,12},{12,16},{16,20},{20,24},{24,28},{28,0},{1,5},{5... | collective-permute-start | bytes 3244040 | tf_op jit(solution)/shard_map/ppermute | solution.py:83
  42.7 49.8 %copy-start.11 = (bf16[128,4224]{0,1:T(8,128)(2,1)}, bf16[128,4224]{0,1:T(8,128)(2,1)S(1)}, u32[]{:S(2)}) copy-start(bf16[128,4224]{0,1:T(8,128)(2,1)S(1)} %collective-permute-done) | copy-start | bytes 3244036
  42.8 25.3 %collective-permute-start.2 = (bf16[128,4224]{0,1:T(8,128)(2,1)S(1)}, bf16[128,4224]{0,1:T(8,128)(2,1)S(1)}, u32[]{:S(2)}, u32[]{:S(2)}) collective-permute-start(bf16[128,4224]{0,1:T(8,128)(2,1)S(1)} %collective-permute-done), channel_id=1, source_target_pairs={{0,4},{4,8},{8,12},{12,16},{16,20},{20,24},{24,28},{28,0},{1,5},{5... | collective-permute-start | bytes 3244040 | tf_op jit(solution)/shard_map/ppermute | solution.py:83
  42.8 25.3 %collective-permute-start.1 = (bf16[128,4224]{0,1:T(8,128)(2,1)S(1)}, bf16[128,4224]{0,1:T(8,128)(2,1)}, u32[]{:S(2)}, u32[]{:S(2)}) collective-permute-start(bf16[128,4224]{0,1:T(8,128)(2,1)S(1)} %get-tuple-element.302), channel_id=1, source_target_pairs={{0,28},{4,0},{8,4},{12,8},{16,12},{20,16},{24,20},{28,24},{1,29},{... | collective-permute-start | bytes 3244040 | tf_op jit(solution)/shard_map/ppermute | solution.py:84
  68.1 24.4 %copy-start.10 = (bf16[128,4224]{0,1:T(8,128)(2,1)}, bf16[128,4224]{0,1:T(8,128)(2,1)S(1)}, u32[]{:S(2)}) copy-start(bf16[128,4224]{0,1:T(8,128)(2,1)S(1)} %collective-permute-done.2) | copy-start | bytes 3244036
  68.1 24.4 %collective-permute-start.4 = (bf16[128,4224]{0,1:T(8,128)(2,1)S(1)}, bf16[128,4224]{0,1:T(8,128)(2,1)S(1)}, u32[]{:S(2)}, u32[]{:S(2)}) collective-permute-start(bf16[128,4224]{0,1:T(8,128)(2,1)S(1)} %collective-permute-done.2), channel_id=1, source_target_pairs={{0,4},{4,8},{8,12},{12,16},{16,20},{20,24},{24,28},{28,0},{1,5},{5... | collective-permute-start | bytes 3244040 | tf_op jit(solution)/shard_map/ppermute | solution.py:83
  68.1 25.2 %collective-permute-start.3 = (bf16[128,4224]{0,1:T(8,128)(2,1)}, bf16[128,4224]{0,1:T(8,128)(2,1)}, u32[]{:S(2)}, u32[]{:S(2)}) collective-permute-start(bf16[128,4224]{0,1:T(8,128)(2,1)} %collective-permute-done.1), channel_id=1, source_target_pairs={{0,28},{4,0},{8,4},{12,8},{16,12},{20,16},{24,20},{28,24},{1,29},{... | collective-permute-start | bytes 3244040 | tf_op jit(solution)/shard_map/ppermute | solution.py:84
  92.5 35.9 %copy-start.9 = (bf16[128,4224]{0,1:T(8,128)(2,1)}, bf16[128,4224]{0,1:T(8,128)(2,1)S(1)}, u32[]{:S(2)}) copy-start(bf16[128,4224]{0,1:T(8,128)(2,1)S(1)} %collective-permute-done.4) | copy-start | bytes 3244036
  92.5 23.6 %collective-permute-start.6 = (bf16[128,4224]{0,1:T(8,128)(2,1)S(1)}, bf16[128,4224]{0,1:T(8,128)(2,1)}, u32[]{:S(2)}, u32[]{:S(2)}) collective-permute-start(bf16[128,4224]{0,1:T(8,128)(2,1)S(1)} %collective-permute-done.4), channel_id=1, source_target_pairs={{0,4},{4,8},{8,12},{12,16},{16,20},{20,24},{24,28},{28,0},{1,5},{5... | collective-permute-start | bytes 3244040 | tf_op jit(solution)/shard_map/ppermute | solution.py:87
  92.5 60.2 %copy-start.59 = (s32[8]{0:T(128)}, s32[8]{0:T(128)S(1)}, u32[]{:S(2)}) copy-start(s32[8]{0:T(128)S(1)} %fusion.181) | copy-start | bytes 100
  92.6 25.4 %copy-start.49 = (s32[128,8]{0,1:T(8,128)}, s32[128,8]{0,1:T(8,128)S(1)}, u32[]{:S(2)}) copy-start(s32[128,8]{0,1:T(8,128)S(1)} %get-tuple-element.298) | copy-start | bytes 12292
  93.3 35.1 %collective-permute-start.5 = (bf16[128,4224]{0,1:T(8,128)(2,1)}, bf16[128,4224]{0,1:T(8,128)(2,1)}, u32[]{:S(2)}, u32[]{:S(2)}) collective-permute-start(bf16[128,4224]{0,1:T(8,128)(2,1)} %collective-permute-done.3), channel_id=1, source_target_pairs={{0,28},{4,0},{8,4},{12,8},{16,12},{20,16},{24,20},{28,24},{1,29},{... | collective-permute-start | bytes 3244040 | tf_op jit(solution)/shard_map/ppermute | solution.py:84
  116.9 12.7 %copy-start.45 = (pred[128,8]{0,1:T(8,128)(4,1)}, pred[128,8]{0,1:T(8,128)(4,1)S(1)}, u32[]{:S(2)}) copy-start(pred[128,8]{0,1:T(8,128)(4,1)S(1)} %get-tuple-element.238) | copy-start | bytes 3076
  119.3 29.6 %all-to-all-start = ((bf16[8,1,24,4224]{3,2,1,0:T(8,128)(2,1)}), bf16[8,1,24,4224]{3,2,1,0:T(8,128)(2,1)S(1)}, u32[]{:S(2)}, u32[]{:S(2)}) async-start(bf16[8,1,24,4224]{3,2,1,0:T(8,128)(2,1)} %fusion.33), calls=%async_computation | async-start | bytes 3244032 | tf_op jit(solution)/shard_map/all_to_all | solution.py:131
  128.4 24.3 %copy-start.35 = (s32[2,128,8]{1,2,0:T(8,128)}, s32[2,128,8]{1,2,0:T(8,128)S(1)}, u32[]{:S(2)}) copy-start(s32[2,128,8]{1,2,0:T(8,128)S(1)} %get-tuple-element.281) | copy-start | bytes 24580
  129.1 23.6 %copy-start.37 = (s32[2,128,8]{1,2,0:T(8,128)}, s32[2,128,8]{1,2,0:T(8,128)S(1)}, u32[]{:S(2)}) copy-start(s32[2,128,8]{1,2,0:T(8,128)S(1)} %get-tuple-element.283) | copy-start | bytes 24580
  148.9 7.0 %copy-start.4 = (bf16[8,1,24,4224]{3,2,1,0:T(8,128)(2,1)}, bf16[8,1,24,4224]{3,2,1,0:T(8,128)(2,1)S(1)}, u32[]{:S(2)}) copy-start(bf16[8,1,24,4224]{3,2,1,0:T(8,128)(2,1)S(1)} %all-to-all-done) | copy-start | bytes 4866052
  148.9 25.0 %all-to-all-start.8 = ((bf16[8,1,24,4224]{3,2,1,0:T(8,128)(2,1)}), bf16[8,1,24,4224]{3,2,1,0:T(8,128)(2,1)S(1)}, u32[]{:S(2)}, u32[]{:S(2)}) async-start(bf16[8,1,24,4224]{3,2,1,0:T(8,128)(2,1)} %fusion.35), calls=%async_computation.8 | async-start | bytes 3244032 | tf_op jit(solution)/shard_map/all_to_all | solution.py:131
  152.9 26.7 %copy-start.57 = (pred[2,128,8]{1,2,0:T(8,128)(4,1)}, pred[2,128,8]{1,2,0:T(8,128)(4,1)S(1)}, u32[]{:S(2)}) copy-start(pred[2,128,8]{1,2,0:T(8,128)(4,1)S(1)} %get-tuple-element.247) | copy-start | bytes 6148
  152.9 72.2 %copy-start.53 = (pred[2,128,8]{1,2,0:T(8,128)(4,1)}, pred[2,128,8]{1,2,0:T(8,128)(4,1)S(1)}, u32[]{:S(2)}) copy-start(pred[2,128,8]{1,2,0:T(8,128)(4,1)S(1)} %get-tuple-element.246) | copy-start | bytes 6148
  175.1 42.5 %all-to-all-start.2 = ((bf16[8,2,24,4224]{3,2,1,0:T(8,128)(2,1)}), bf16[8,2,24,4224]{3,2,1,0:T(8,128)(2,1)S(1)}, u32[]{:S(2)}, u32[]{:S(2)}) async-start(bf16[8,2,24,4224]{3,2,1,0:T(8,128)(2,1)} %copy.139), calls=%async_computation.2 | async-start | bytes 6488064 | tf_op jit(solution)/shard_map/all_to_all | solution.py:131
  217.6 43.6 %all-to-all-start.4 = ((bf16[8,2,24,4224]{3,2,1,0:T(8,128)(2,1)}), bf16[8,2,24,4224]{3,2,1,0:T(8,128)(2,1)}, u32[]{:S(2)}, u32[]{:S(2)}) async-start(bf16[8,2,24,4224]{3,2,1,0:T(8,128)(2,1)} %copy.146), calls=%async_computation.4 | async-start | bytes 6488064 | tf_op jit(solution)/shard_map/all_to_all | solution.py:131
  222.3 94.6 %all-gather.2.cloned.1.call-start = ((), (), s32[]{:S(2)}) async-start(), calls=%async_computation.12 | async-start | bytes 5898240 | tf_op jit(solution)/shard_map/all_gather | solution.py:66
  261.2 43.0 %all-to-all-start.6 = ((bf16[8,2,24,4224]{3,2,1,0:T(8,128)(2,1)}), bf16[8,2,24,4224]{3,2,1,0:T(8,128)(2,1)}, u32[]{:S(2)}, u32[]{:S(2)}) async-start(bf16[8,2,24,4224]{3,2,1,0:T(8,128)(2,1)} %copy.153), calls=%async_computation.6 | async-start | bytes 6488064 | tf_op jit(solution)/shard_map/all_to_all | solution.py:131
  265.6 250.8 %reduce-scatter.5.cloned.1.call-start = ((), (), s32[]{:S(2)}) async-start(), calls=%async_computation.14 | async-start | bytes 11796480 | tf_op jit(solution)/shard_map/reduce_scatter | solution.py:176
  320.2 22.0 %copy-start.12 = (f32[384,384]{1,0:T(8,128)}, f32[384,384]{1,0:T(8,128)S(1)}, u32[]{:S(2)}) copy-start(f32[384,384]{1,0:T(8,128)S(1)} %fusion.39) | copy-start | bytes 1769476
  322.8 19.4 %copy-start.13 = (f32[384,384]{1,0:T(8,128)}, f32[384,384]{1,0:T(8,128)S(1)}, u32[]{:S(2)}) copy-start(f32[384,384]{1,0:T(8,128)S(1)} %fusion.47) | copy-start | bytes 1769476
  325.4 12.9 %copy-start.19 = (f32[384,384]{1,0:T(8,128)}, f32[384,384]{1,0:T(8,128)S(1)}, u32[]{:S(2)}) copy-start(f32[384,384]{1,0:T(8,128)S(1)} %fusion.41) | copy-start | bytes 1769476
  328.0 10.3 %copy-start.21 = (f32[384,384]{1,0:T(8,128)}, f32[384,384]{1,0:T(8,128)S(1)}, u32[]{:S(2)}) copy-start(f32[384,384]{1,0:T(8,128)S(1)} %fusion.51) | copy-start | bytes 1769476
  329.0 7.1 %copy-start.14 = (f32[384,384]{1,0:T(8,128)}, f32[384,384]{1,0:T(8,128)S(1)}, u32[]{:S(2)}) copy-start(f32[384,384]{1,0:T(8,128)S(1)} %fusion.43) | copy-start | bytes 1769476
  330.7 5.4 copy-start.16
  338.3 7.9 %slice-start.2 = ((s8[6291456]{0:T(1024)(128)(4,1)}), s8[4194304]{0:T(1024)(128)(4,1)S(1)}, s32[]{:S(2)}) async-start(s8[6291456]{0:T(1024)(128)(4,1)} %bitcast.245), calls=%async_computation.17 | async-start | bytes 8388608
  342.1 4.1 slice-start.3
  346.2 7.5 %slice-start.4 = ((s8[6291456]{0:T(1024)(128)(4,1)}), s8[4194304]{0:T(1024)(128)(4,1)S(1)}, s32[]{:S(2)}) async-start(s8[6291456]{0:T(1024)(128)(4,1)} %bitcast.247), calls=%async_computation.19 | async-start | bytes 8388608
  349.2 4.5 slice-start.5
  372.5 5.5 copy-start.20
  372.5 5.5 copy-start.22
  372.5 5.5 copy-start.23
  373.5 17.6 %all-to-all-start.1 = ((bf16[8,1,24,2176]{3,2,1,0:T(8,128)(2,1)}), bf16[8,1,24,2176]{3,2,1,0:T(8,128)(2,1)}, u32[]{:S(2)}, u32[]{:S(2)}) async-start(bf16[8,1,24,2176]{3,2,1,0:T(8,128)(2,1)} %bitcast.20), calls=%async_computation.1 | async-start | bytes 1671168 | tf_op jit(solution)/shard_map/all_to_all | solution.py:145
  386.6 8.7 %copy-start.26 = (bf16[384,384]{1,0:T(8,128)(2,1)S(1)}, bf16[384,384]{1,0:T(8,128)(2,1)}, u32[]{:S(2)}) copy-start(bf16[384,384]{1,0:T(8,128)(2,1)} %get-tuple-element.293) | copy-start | bytes 884740
  391.1 17.3 %all-to-all-start.9 = ((bf16[8,1,24,2176]{3,2,1,0:T(8,128)(2,1)}), bf16[8,1,24,2176]{3,2,1,0:T(8,128)(2,1)}, u32[]{:S(2)}, u32[]{:S(2)}) async-start(bf16[8,1,24,2176]{3,2,1,0:T(8,128)(2,1)} %bitcast.236), calls=%async_computation.9 | async-start | bytes 1671168 | tf_op jit(solution)/shard_map/all_to_all | solution.py:145
  399.0 13.2 %copy-start.15 = (f32[384,384]{1,0:T(8,128)S(1)}, f32[384,384]{1,0:T(8,128)}, u32[]{:S(2)}) copy-start(f32[384,384]{1,0:T(8,128)} %copy-done.14) | copy-start | bytes 1769476
  399.0 13.2 %copy-start.17 = (f32[384,384]{1,0:T(8,128)S(1)}, f32[384,384]{1,0:T(8,128)}, u32[]{:S(2)}) copy-start(f32[384,384]{1,0:T(8,128)} %copy-done.16) | copy-start | bytes 1769476
  399.0 13.2 %copy-start.18 = (f32[384,384]{1,0:T(8,128)S(1)}, f32[384,384]{1,0:T(8,128)}, u32[]{:S(2)}) copy-start(f32[384,384]{1,0:T(8,128)} %get-tuple-element.312) | copy-start | bytes 1769476
  408.4 25.9 %all-to-all-start.5 = ((bf16[8,2,24,2176]{3,2,1,0:T(8,128)(2,1)}), bf16[8,2,24,2176]{3,2,1,0:T(8,128)(2,1)S(1)}, u32[]{:S(2)}, u32[]{:S(2)}) async-start(bf16[8,2,24,2176]{3,2,1,0:T(8,128)(2,1)} %bitcast.54), calls=%async_computation.5 | async-start | bytes 3342336 | tf_op jit(solution)/shard_map/all_to_all | solution.py:145
  434.3 5.2 copy-start.1
  434.3 25.2 %all-to-all-start.3 = ((bf16[8,2,24,2176]{3,2,1,0:T(8,128)(2,1)}), bf16[8,2,24,2176]{3,2,1,0:T(8,128)(2,1)S(1)}, u32[]{:S(2)}, u32[]{:S(2)}) async-start(bf16[8,2,24,2176]{3,2,1,0:T(8,128)(2,1)} %bitcast.225), calls=%async_computation.3 | async-start | bytes 3342336 | tf_op jit(solution)/shard_map/all_to_all | solution.py:145
  446.7 17.3 %copy-start.48 = (pred[128,8]{0,1:T(8,128)(4,1)S(1)}, pred[128,8]{0,1:T(8,128)(4,1)}, u32[]{:S(2)}) copy-start(pred[128,8]{0,1:T(8,128)(4,1)} %copy-done.47) | copy-start | bytes 3076
  446.7 17.4 %copy-start.46 = (pred[128,8]{0,1:T(8,128)(4,1)S(1)}, pred[128,8]{0,1:T(8,128)(4,1)}, u32[]{:S(2)}) copy-start(pred[128,8]{0,1:T(8,128)(4,1)} %copy-done.45) | copy-start | bytes 3076
  446.7 17.6 %copy-start.50 = (s32[128,8]{0,1:T(8,128)S(1)}, s32[128,8]{0,1:T(8,128)}, u32[]{:S(2)}) copy-start(s32[128,8]{0,1:T(8,128)} %copy-done.49) | copy-start | bytes 12292
  446.7 17.6 %copy-start.52 = (s32[128,8]{0,1:T(8,128)S(1)}, s32[128,8]{0,1:T(8,128)}, u32[]{:S(2)}) copy-start(s32[128,8]{0,1:T(8,128)} %copy-done.51) | copy-start | bytes 12292
  446.7 17.6 %copy-start.60 = (s32[8]{0:T(128)S(1)}, s32[8]{0:T(128)}, u32[]{:S(2)}) copy-start(s32[8]{0:T(128)} %copy-done.59) | copy-start | bytes 100
  459.4 5.2 copy-start.2
  459.4 26.3 %all-to-all-start.7 = ((bf16[8,2,24,2176]{3,2,1,0:T(8,128)(2,1)}), bf16[8,2,24,2176]{3,2,1,0:T(8,128)(2,1)}, u32[]{:S(2)}, u32[]{:S(2)}) async-start(bf16[8,2,24,2176]{3,2,1,0:T(8,128)(2,1)} %bitcast.68), calls=%async_computation.7 | async-start | bytes 3342336 | tf_op jit(solution)/shard_map/all_to_all | solution.py:145
  464.0 149.7 %reduce-scatter.3.cloned.1.call-start = ((), (), s32[]{:S(2)}) async-start(), calls=%async_computation.13 | async-start | bytes 10027008 | tf_op jit(solution)/shard_map/reduce_scatter | solution.py:171
  466.2 20.7 %copy-start.40 = (s32[8,2,128]{2,0,1:T(8,128)S(1)}, s32[8,2,128]{2,0,1:T(8,128)}, u32[]{:S(2)}) copy-start(s32[8,2,128]{2,0,1:T(8,128)} %copy-done.39) | copy-start | bytes 24580
  466.2 20.7 %copy-start.56 = (pred[2,128,8]{1,2,0:T(8,128)(4,1)S(1)}, pred[2,128,8]{1,2,0:T(8,128)(4,1)}, u32[]{:S(2)}) copy-start(pred[2,128,8]{1,2,0:T(8,128)(4,1)} %copy-done.55) | copy-start | bytes 6148
  466.2 20.8 %copy-start.42 = (s32[8,2,128]{2,0,1:T(8,128)S(1)}, s32[8,2,128]{2,0,1:T(8,128)}, u32[]{:S(2)}) copy-start(s32[8,2,128]{2,0,1:T(8,128)} %copy-done.41) | copy-start | bytes 24580
  466.2 20.8 %copy-start.58 = (pred[2,128,8]{1,2,0:T(8,128)(4,1)S(1)}, pred[2,128,8]{1,2,0:T(8,128)(4,1)}, u32[]{:S(2)}) copy-start(pred[2,128,8]{1,2,0:T(8,128)(4,1)} %copy-done.57) | copy-start | bytes 6148
  466.2 21.0 %copy-start.44 = (s32[8,2,128]{2,0,1:T(8,128)S(1)}, s32[8,2,128]{2,0,1:T(8,128)}, u32[]{:S(2)}) copy-start(s32[8,2,128]{2,0,1:T(8,128)} %copy-done.43) | copy-start | bytes 24580
  466.2 21.0 %copy-start.54 = (pred[2,128,8]{1,2,0:T(8,128)(4,1)S(1)}, pred[2,128,8]{1,2,0:T(8,128)(4,1)}, u32[]{:S(2)}) copy-start(pred[2,128,8]{1,2,0:T(8,128)(4,1)} %copy-done.53) | copy-start | bytes 6148
  466.2 21.1 %copy-start.36 = (s32[2,128,8]{1,2,0:T(8,128)S(1)}, s32[2,128,8]{1,2,0:T(8,128)}, u32[]{:S(2)}) copy-start(s32[2,128,8]{1,2,0:T(8,128)} %copy-done.35) | copy-start | bytes 24580
  466.2 21.1 %copy-start.38 = (s32[2,128,8]{1,2,0:T(8,128)S(1)}, s32[2,128,8]{1,2,0:T(8,128)}, u32[]{:S(2)}) copy-start(s32[2,128,8]{1,2,0:T(8,128)} %copy-done.37) | copy-start | bytes 24580
  (25 other events, 62.2 us)
Sparse Core Ops, SparseCore 0:
  224.9 53.9 all-gather.1
  366.3 88.9 reduce-scatter.4
  516.5 97.2 reduce-scatter.2

commit v4 on v2

--- a/solution.py
+++ b/solution.py
@@ -52,6 +52,7 @@
     near = cores * rows_of
     slots = near * planes * capacity
     pad = 128
+    half = width // 2
     meta = (
         jnp.zeros((tokens_dev, pad), jnp.bfloat16)
         .at[:, :top_count]
@@ -59,12 +60,10 @@
         .at[:, top_count : 2 * top_count]
         .set(routes.astype(jnp.bfloat16))
     )
-    pack = jnp.concatenate([tokens, cotangent, meta], axis=1)
-    gathered = lax.all_gather(pack, "lz", axis=0, tiled=False)
-    seen_gates = gathered[:, :, 2 * width : 2 * width + top_count]
-    seen_routes = gathered[:, :, 2 * width + top_count : 2 * width + 2 * top_count].astype(
-        jnp.int32
-    )
+    seen_x = lax.all_gather(jnp.concatenate([tokens, meta], axis=1), "lz", axis=0, tiled=False)
+    seen_dy = lax.all_gather(cotangent, "lz", axis=0, tiled=False)
+    seen_gates = seen_x[:, :, width : width + top_count]
+    seen_routes = seen_x[:, :, width + top_count : width + 2 * top_count].astype(jnp.int32)
     plane = lax.axis_index("lz")
     near_ids = jnp.arange(near, dtype=jnp.int32)
     near_experts = (near_ids // rows_of) * (planes * rows_of) + plane * rows_of + near_ids % rows_of
@@ -80,12 +79,6 @@
         rank[:, :, None, :] == jnp.arange(capacity, dtype=jnp.int32)[None, None, :, None]
     )
     choose_b = choose.astype(jnp.bfloat16)
-    send_rows = jnp.einsum(
-        "jzrt,ztd->jzrd",
-        choose_b,
-        gathered[:, :, : 2 * width],
-        preferred_element_type=jnp.float32,
-    ).astype(jnp.bfloat16)
     gate_tj = jnp.sum(
         jnp.where(hit, seen_gates[..., None], jnp.zeros((), jnp.bfloat16)), axis=2
     )
@@ -98,33 +91,42 @@
     gate_block = (
         jnp.zeros((near, planes, capacity, pad), jnp.bfloat16).at[..., 0].set(send_gate)
     )
-    send = jnp.concatenate([send_rows, gate_block], axis=3)
+    send_x = jnp.einsum(
+        "jzrt,ztd->jzrd", choose_b, seen_x[:, :, :width], preferred_element_type=jnp.float32
+    ).astype(jnp.bfloat16)
+    send_x = jnp.concatenate([send_x, gate_block], axis=3)
+    send_dy = jnp.einsum(
+        "jzrt,ztd->jzrd", choose_b, seen_dy, preferred_element_type=jnp.float32
+    ).astype(jnp.bfloat16)
     all_weights = lax.all_gather(
         jnp.concatenate([w_gate, w_up, w_down], axis=2), "dp", axis=1, tiled=True
     )[0]
     gate_proj = all_weights[:, :hidden_units]
     up_proj = all_weights[:, hidden_units : 2 * hidden_units]
     down_proj = all_weights[:, 2 * hidden_units :]
-    recv = lax.all_to_all(send, ("node", "ly"), split_axis=0, concat_axis=0, tiled=True)
-    flat = recv.reshape(slots, 2 * width + pad)
+    recv_x = lax.all_to_all(send_x, ("node", "ly"), split_axis=0, concat_axis=0, tiled=True)
+    recv_dy = lax.all_to_all(send_dy, ("node", "ly"), split_axis=0, concat_axis=0, tiled=True)
+    flat_x = recv_x.reshape(slots, width + pad)
     results = expert_rows(
-        flat[:, :width],
-        flat[:, width : 2 * width],
-        flat[:, 2 * width],
+        flat_x[:, :width],
+        recv_dy.reshape(slots, width),
+        flat_x[:, width],
         gate_proj,
         up_proj,
         down_proj,
     )
     grad_block = jnp.zeros((slots, pad), jnp.bfloat16).at[:, 0].set(results[1])
-    back = jnp.concatenate([results[0], grad_block], axis=1).reshape(
-        near, planes, capacity, width + pad
+    back_lo = jnp.concatenate([results[0][:, :half], grad_block], axis=1).reshape(
+        near, planes, capacity, half + pad
     )
-    home = lax.all_to_all(back, ("node", "ly"), split_axis=0, concat_axis=0, tiled=True)
-    partial = jnp.einsum(
-        "jzrt,jzrd->ztd", choose_b, home[..., :width], preferred_element_type=jnp.float32
+    back_hi = results[0][:, half:].reshape(near, planes, capacity, width - half)
+    home_lo = lax.all_to_all(back_lo, ("node", "ly"), split_axis=0, concat_axis=0, tiled=True)
+    home_hi = lax.all_to_all(back_hi, ("node", "ly"), split_axis=0, concat_axis=0, tiled=True)
+    partial_lo = jnp.einsum(
+        "jzrt,jzrd->ztd", choose_b, home_lo[..., :half], preferred_element_type=jnp.float32
     )
     gate_jzt = jnp.sum(
-        jnp.where(choose, home[..., width][..., None], jnp.zeros((), jnp.bfloat16)), axis=2
+        jnp.where(choose, home_lo[..., half][..., None], jnp.zeros((), jnp.bfloat16)), axis=2
     )
     pick_gate = jnp.sum(
         jnp.where(
@@ -137,11 +139,17 @@
         .at[..., :top_count]
         .set(pick_gate.astype(jnp.float32))
     )
-    reduced = lax.psum_scatter(
-        jnp.concatenate([partial, gate_cols], axis=2), "lz", scatter_dimension=0, tiled=True
+    reduced_lo = lax.psum_scatter(
+        jnp.concatenate([partial_lo, gate_cols], axis=2), "lz", scatter_dimension=0, tiled=True
     )[0]
-    input_grad = reduced[:, :width].astype(jnp.bfloat16)
-    gate_grad = reduced[:, width : width + top_count].astype(jnp.bfloat16)
+    partial_hi = jnp.einsum(
+        "jzrt,jzrd->ztd", choose_b, home_hi, preferred_element_type=jnp.float32
+    )
+    reduced_hi = lax.psum_scatter(partial_hi, "lz", scatter_dimension=0, tiled=True)[0]
+    input_grad = jnp.concatenate(
+        [reduced_lo[:, :half], reduced_hi], axis=1
+    ).astype(jnp.bfloat16)
+    gate_grad = reduced_lo[:, half : half + top_count].astype(jnp.bfloat16)
     summed = lax.psum_scatter(
         jnp.concatenate([results[2], results[3], results[4]], axis=1),
         "dp",

time: 546 us -> 532 us (0.974)
  waiting for transfers between devices: 334 us -> 304 us
  blocking collectives: 78.6 us -> 85.9 us
    reduce_scatter x1, waiting for transfers between devices: 0.03 us -> 90 us  [local(): lax.psum_scatter(jnp.concatenate([results[2], results[3], results[4]], ax...]
    reduce_scatter x1 -> x2, waiting for transfers between devices: 91.6 us -> 28.5 us  [the longest x1 28.4 us: local(): lax.psum_scatter(jnp.concatenate([partial_lo, gate_cols], axis=2), 'lz',...]
    all_gather x1, waiting for transfers between devices: 54.2 us -> 12.5 us  [local(): lax.all_gather(jnp.concatenate([w_gate, w_up, w_down], axis=2), 'dp', axi...]
    all_to_all x1 -> x2, waiting for transfers between devices: 87.3 us -> 73.9 us  [the longest x1 43.9 us: local(): lax.all_to_all(send_dy, ('node', 'ly'), split_axis=0, concat_axis=0, tile...]
    all_to_all x1 -> x2, blocking collectives: 78.6 us -> 85.9 us  [the longest x1 45.3 us: local(): lax.all_to_all(back_lo, ('node', 'ly'), split_axis=0, concat_axis=0, tile...]
    concatenate x4 -> x5, other arithmetic: 13.4 us -> 6.23 us  [the longest x1 2.5 us: local(): jnp.concatenate([partial_lo, gate_cols], axis=2)]
    all_gather x1 -> x2, waiting for transfers between devices: 101 us -> 97.8 us  [the longest x1 60.5 us: local(): lax.all_gather(jnp.concatenate([tokens, meta], axis=1), 'lz', axis=0, til...]
    dot_general x2 -> x4, matrix products: 13.5 us -> 12.2 us  [the longest x1 3.96 us: local(): jnp.einsum('jzrt,ztd->jzrd', choose_b, seen_x[:, :, :width], preferred_el...]
  transfers between devices with their start and end apart: 5 -> 8, of which waited for: 4 -> 7; matrix products, arithmetic and copies ran while one was open for 5% -> 15% of each run, Pallas kernels for 0% -> 0%
where the time goes in v4:
time: 532 us; the launch traced here: 531 us
  waiting for transfers between devices  304 us (57%)
  blocking collectives  85.9 us (16%)
  matrix products  65.3 us (12%)
  other arithmetic  27.7 us (5%)
  local copies, waits for them, and re-layouts  23.3 us (4%)
  between operations  14.4 us (3%)
  starting transfers between devices  10.4 us (2%)
    reduce_scatter x1, waiting for transfers between devices, local(): lax.psum_scatter(jnp.concatenate([results[2], results[3], results[4]], ax...  90 us
    all_gather x1, waiting for transfers between devices, local(): lax.all_gather(jnp.concatenate([tokens, meta], axis=1), 'lz', axis=0, til...  60.5 us
    all_to_all x1, blocking collectives, local(): lax.all_to_all(back_lo, ('node', 'ly'), split_axis=0, concat_axis=0, tile...  45.3 us
    all_to_all x1, waiting for transfers between devices, local(): lax.all_to_all(send_dy, ('node', 'ly'), split_axis=0, concat_axis=0, tile...  43.9 us
    all_to_all x1, blocking collectives, local(): lax.all_to_all(back_hi, ('node', 'ly'), split_axis=0, concat_axis=0, tile...  40.7 us
    all_gather x1, waiting for transfers between devices, local(): seen_dy = lax.all_gather(cotangent, 'lz', axis=0, tiled=False)  37.4 us
    all_to_all x1, waiting for transfers between devices, local(): lax.all_to_all(send_x, ('node', 'ly'), split_axis=0, concat_axis=0, tiled...  30 us
    reduce_scatter x1, waiting for transfers between devices, local(): lax.psum_scatter(jnp.concatenate([partial_lo, gate_cols], axis=2), 'lz',...  28.4 us
  transfers between devices with their start and end apart: 8, of which 7 were waited for; matrix products, arithmetic and copies ran while one was open for 15% of the time, Pallas kernels for 0%

profile of v4, /device:TPU:1, one launch (start us, length us, event | category | flops | bytes accessed | tf_op | source)
XLA Modules:
  0.0 530.5 jit_solution(14317885065794748154)
XLA Ops:
  7.2 0.6 compare_reduce_fusion.3
  7.9 0.6 compare_reduce_fusion.2
  8.5 0.7 convert_element_type.61
  9.2 0.1 copy.81
  9.3 0.8 copy.80
  10.1 0.7 broadcast_select_fusion
  10.8 0.7 broadcast_select_fusion.1
  11.4 0.4 scatter.21
  11.9 1.9 pad_maximum_fusion.3
  13.8 0.7 all-gather.10.cloned.1.call-update
  14.6 60.5 %all-gather.8.cloned.1.call-done = bf16[1024,2176]{1,0:T(8,128)(2,1)} async-done(((bf16[128,2176]{1,0:T(8,128)(2,1)}), bf16[1024,2176]{1,0:T(8,128)(2,1)}) %all-gather.8.cloned.1.call-update) | async-done | bytes 4456464 | tf_op jit(solution)/shard_map/all_gather | solution.py:63
  75.0 1.2 fusion.60
  76.6 0.5 copy-done.4
  77.2 0.1 fusion.32
  77.3 0.3 fusion.41
  77.7 0.5 copy.85
  78.1 4.0 convert_bitcast_fusion.1
  82.1 0.6 fusion.2
  82.8 3.4 copy.86
  86.1 5.5 %all-to-all-start = ((bf16[8,8,24,2176]{3,2,1,0:T(8,128)(2,1)}), bf16[8,8,24,2176]{3,2,1,0:T(8,128)(2,1)}, u32[]{:S(2)}, u32[]{:S(2)}) async-start(bf16[8,8,24,2176]{3,2,1,0:T(8,128)(2,1)} %copy.86), calls=%async_computation | async-start | bytes 13369344 | tf_op jit(solution)/shard_map/all_to_all | solution.py:107
  91.7 1.2 pad_maximum_fusion.2
  92.9 37.4 %all-gather.10.cloned.1.call-done = bf16[1024,2048]{1,0:T(8,128)(2,1)} async-done(((bf16[128,2048]{1,0:T(8,128)(2,1)}), bf16[1024,2048]{1,0:T(8,128)(2,1)}) %all-gather.10.cloned.1.call-update) | async-done | bytes 4194320 | tf_op jit(solution)/shard_map/all_gather | solution.py:64
  130.2 4.0 convert_bitcast_fusion
  134.2 3.2 copy.87
  137.4 30.0 %all-to-all-done = bf16[8,8,24,2176]{3,2,1,0:T(8,128)(2,1)} async-done(((bf16[8,8,24,2176]{3,2,1,0:T(8,128)(2,1)}), bf16[8,8,24,2176]{3,2,1,0:T(8,128)(2,1)}, u32[]{:S(2)}, u32[]{:S(2)}) %all-to-all-start) | async-done | bytes 6684704 | tf_op jit(solution)/shard_map/all_to_all | solution.py:107
  167.4 4.7 all-to-all-start.1
  172.1 1.2 convert_reduce_fusion
  173.3 12.5 %all-gather.6.cloned.1.call-done = bf16[1,2048,1152]{2,1,0:T(8,128)(2,1)} async-done(((bf16[1,512,1152]{2,1,0:T(8,128)(2,1)}), bf16[1,2048,1152]{2,1,0:T(8,128)(2,1)}) %all-gather.6.cloned.1.call-update) | async-done | bytes 4718608 | tf_op jit(solution)/shard_map/all_gather | solution.py:101
  185.8 5.4 %fusion.7 = f32[1536,384]{0,1:T(8,128)S(1)} fusion(bf16[1536,2176]{1,0:T(8,128)(2,1)} %bitcast.9, bf16[2048,1152]{1,0:T(8,128)(2,1)} %bitcast.58), kind=kOutput, calls=%fused_computation.15 | convolution fusion | flops 2415919104 | bytes 10223616 | tf_op jit(solution)/shard_map/dot_general | solution.py:8
  191.3 8.2 %fusion.9 = f32[1536,384]{0,1:T(8,128)} fusion(bf16[1536,2176]{1,0:T(8,128)(2,1)} %bitcast.9, bf16[2048,1152]{1,0:T(8,128)(2,1)} %bitcast.59), kind=kOutput, calls=%fused_computation.17 | convolution fusion | flops 2415919104 | bytes 10223616 | tf_op jit(solution)/shard_map/dot_general | solution.py:9
  199.5 43.9 %all-to-all-done.1 = bf16[8,8,24,2048]{3,2,1,0:T(8,128)(2,1)} async-done(((bf16[8,8,24,2048]{3,2,1,0:T(8,128)(2,1)}), bf16[8,8,24,2048]{3,2,1,0:T(8,128)(2,1)}, u32[]{:S(2)}, u32[]{:S(2)}) %all-to-all-start.1) | async-done | bytes 6291488 | tf_op jit(solution)/shard_map/all_to_all | solution.py:108
  243.4 8.8 %multiply_reduce_fusion = (bf16[1536]{0:T(1024)(128)(2,1)S(1)}, bf16[1536,384]{0,1:T(8,128)(2,1)S(1)}, bf16[1536,384]{0,1:T(8,128)(2,1)}) fusion(f32[1536,384]{0,1:T(8,128)} %fusion.9, f32[1536,384]{0,1:T(8,128)S(1)} %fusion.7, f32[1536]{0:T(1024)S(1)} %convert_reduce_fusion, bf16[1536,2048]{1,0:T(8,128)(2,1)} %bitcast.14, bf16[2048,1152]{1,0:T(8,128)(2,1)} %bitcast.60), kind=kOutput, calls=%fused_computation.25 | convolution fusion | flops 2425944576 | bytes 14951424 | tf_op jit(solution)/shard_map/dot_general | solution.py:13
  252.2 5.4 %fusion.25 = f32[1536,2048]{1,0:T(8,128)S(1)} fusion(bf16[1536,384]{0,1:T(8,128)(2,1)S(1)} %get-tuple-element.96, bf16[2048,1152]{1,0:T(8,128)(2,1)} %bitcast.61), kind=kOutput, calls=%fused_computation.34 | convolution fusion | flops 2415919104 | bytes 15335424 | tf_op jit(solution)/shard_map/dot_general | solution.py:31
  257.5 5.6 %add_convert_fusion = bf16[1536,2048]{1,0:T(8,128)(2,1)S(1)} fusion(f32[1536,2048]{1,0:T(8,128)S(1)} %fusion.25, bf16[1536,384]{0,1:T(8,128)(2,1)} %get-tuple-element.99, bf16[2048,1152]{1,0:T(8,128)(2,1)} %bitcast.62), kind=kOutput, calls=%fused_computation.2 | convolution fusion | flops 2422210560 | bytes 21626880 | tf_op jit(solution)/shard_map/dot_general | solution.py:34
  263.2 2.3 fusion.59
  265.5 40.7 %all_to_all.20 = bf16[8,8,24,1024]{3,2,1,0:T(8,128)(2,1)S(1)} all-to-all(bf16[8,8,24,1024]{3,2,1,0:T(8,128)(2,1)S(1)} %bitcast.56), channel_id=1, replica_groups=mesh['dp'=4,'node'=2,'lz'=8,'ly'=4] {'node','ly'}, dimensions={0} | all-to-all | bytes 6291456 | tf_op jit(solution)/shard_map/all_to_all | solution.py:124
  306.2 2.7 fusion.17
  309.0 0.6 compare_reduce_fusion.1
  309.6 0.9 convert_select_fusion
  310.5 0.3 reshape.218
  310.8 0.4 fusion.11
  311.2 45.3 %all_to_all.21 = bf16[8,8,24,1152]{3,2,1,0:T(8,128)(2,1)S(1)} all-to-all(bf16[8,8,24,1152]{3,2,1,0:T(8,128)(2,1)S(1)} %bitcast.55), channel_id=1, replica_groups=mesh['dp'=4,'node'=2,'lz'=8,'ly'=4] {'node','ly'}, dimensions={0} | all-to-all | bytes 7077888 | tf_op jit(solution)/shard_map/all_to_all | solution.py:123
  356.5 0.8 slice.172
  357.3 2.0 copy.107
  359.3 1.2 fusion.42
  360.5 1.5 fusion.52
  362.0 1.6 copy.92
  363.6 1.0 pad_convert_fusion
  364.6 1.5 fusion.20
  366.1 2.5 pad_maximum_fusion.1
  368.7 5.1 fusion.3
  373.9 7.2 %fusion.5 = f32[2048,384]{0,1:T(8,128)} fusion(bf16[1536,384]{0,1:T(8,128)(2,1)S(1)} %copy-done.2, bf16[1536,2176]{1,0:T(8,128)(2,1)} %bitcast.9), kind=kOutput, calls=%fused_computation.13 | convolution fusion | flops 2415919104 | bytes 10616832 | tf_op jit(solution)/shard_map/dot_general | solution.py:29
  381.0 7.3 %fusion.30 = f32[2048,384]{0,1:T(8,128)} fusion(bf16[1536,2048]{1,0:T(8,128)(2,1)} %bitcast.14, f32[1536]{0:T(1024)S(1)} %convert_reduce_fusion, f32[1536,384]{0,1:T(8,128)S(1)} %copy-done.11, f32[1536,384]{0,1:T(8,128)S(1)} %copy-done.10), kind=kOutput, calls=%fused_computation.39 | convolution fusion | flops 2420047872 | bytes 14161920 | tf_op jit(solution)/shard_map/dot_general | solution.py:23
  388.3 7.9 %pad_maximum_fusion = f32[2048,1152]{0,1:T(8,128)} fusion(f32[2048,384]{0,1:T(8,128)} %fusion.30, f32[2048,384]{0,1:T(8,128)} %fusion.5, f32[2048,384]{0,1:T(8,128)S(1)} %fusion.3), kind=kLoop, calls=%fused_computation.3 | loop fusion | flops 4718592 | bytes 18874368 | tf_op jit(solution)/shard_map/concatenate | solution.py:154
  396.2 1.1 convert_bitcast_fusion.3
  397.3 28.4 %reduce-scatter.4.cloned.1.call-done = f32[1,128,1152]{2,1,0:T(8,128)} async-done(((f32[8,128,1152]{2,1,0:T(8,128)}), f32[1,128,1152]{2,1,0:T(8,128)}) %reduce-scatter.4.cloned.1.call-update) | async-done | bytes 589840 | tf_op jit(solution)/shard_map/reduce_scatter | solution.py:142
  425.8 1.1 convert_bitcast_fusion.2
  426.9 0.7 copy.94
  427.6 0.8 pad_maximum_fusion.4
  428.4 90.0 %reduce-scatter.8.cloned.1.call-done = f32[512,1152]{0,1:T(8,128)} async-done(((f32[2048,1152]{0,1:T(8,128)}), f32[512,1152]{0,1:T(8,128)}) %reduce-scatter.8.cloned.1.call-update) | async-done | bytes 2359312 | tf_op jit(solution)/shard_map/reduce_scatter | solution.py:153
  518.4 1.8 slice_bitcast_fusion.2
  520.2 1.1 copy.97
  521.4 1.1 copy.96
  522.5 1.1 copy.95
  (44 shorter events, 0.8 us)
Async XLA Ops:
  7.2 67.8 %all-gather.8.cloned.1.call-start = ((), (), s32[]{:S(2)}) async-start(), calls=%async_computation.11 | async-start | bytes 5013504 | tf_op jit(solution)/shard_map/all_gather | solution.py:63
  13.8 116.5 %all-gather.10.cloned.1.call-start = ((), (), s32[]{:S(2)}) async-start(), calls=%async_computation.12 | async-start | bytes 4718592 | tf_op jit(solution)/shard_map/all_gather | solution.py:64
  14.5 67.6 %copy-start.8 = (s32[8]{0:T(128)}, s32[8]{0:T(128)S(1)}, u32[]{:S(2)}) copy-start(s32[8]{0:T(128)S(1)} %fusion.55) | copy-start | bytes 100
  76.4 0.6 copy-start.4
  77.3 228.9 %copy-start.1 = (s32[8,8,128]{2,0,1:T(8,128)}, s32[8,8,128]{2,0,1:T(8,128)S(1)}, u32[]{:S(2)}) copy-start(s32[8,8,128]{2,0,1:T(8,128)S(1)} %fusion.32) | copy-start | bytes 98308
  86.1 5.5 %copy-start.5 = (bf16[1,512,384]{2,1,0:T(8,128)(2,1)S(1)}, bf16[1,512,384]{2,1,0:T(8,128)(2,1)}, u32[]{:S(2)}) copy-start(bf16[1,512,384]{2,1,0:T(8,128)(2,1)} %param.23) | copy-start | bytes 1179652
  86.1 5.5 %copy-start.6 = (bf16[1,512,384]{2,1,0:T(8,128)(2,1)S(1)}, bf16[1,512,384]{2,1,0:T(8,128)(2,1)}, u32[]{:S(2)}) copy-start(bf16[1,512,384]{2,1,0:T(8,128)(2,1)} %param.22) | copy-start | bytes 1179652
  86.1 5.5 %copy-start.7 = (bf16[1,512,384]{2,1,0:T(8,128)(2,1)S(1)}, bf16[1,512,384]{2,1,0:T(8,128)(2,1)}, u32[]{:S(2)}) copy-start(bf16[1,512,384]{2,1,0:T(8,128)(2,1)} %param.21) | copy-start | bytes 1179652
  86.1 81.3 %all-to-all-start = ((bf16[8,8,24,2176]{3,2,1,0:T(8,128)(2,1)}), bf16[8,8,24,2176]{3,2,1,0:T(8,128)(2,1)}, u32[]{:S(2)}, u32[]{:S(2)}) async-start(bf16[8,8,24,2176]{3,2,1,0:T(8,128)(2,1)} %copy.86), calls=%async_computation | async-start | bytes 13369344 | tf_op jit(solution)/shard_map/all_to_all | solution.py:107
  91.6 94.2 %all-gather.6.cloned.1.call-start = ((), (), s32[]{:S(2)}) async-start(), calls=%async_computation.7 | async-start | bytes 5898240 | tf_op jit(solution)/shard_map/all_gather | solution.py:101
  167.4 76.0 %all-to-all-start.1 = ((bf16[8,8,24,2048]{3,2,1,0:T(8,128)(2,1)}), bf16[8,8,24,2048]{3,2,1,0:T(8,128)(2,1)}, u32[]{:S(2)}, u32[]{:S(2)}) async-start(bf16[8,8,24,2048]{3,2,1,0:T(8,128)(2,1)} %copy.87), calls=%async_computation.1 | async-start | bytes 12582912 | tf_op jit(solution)/shard_map/all_to_all | solution.py:108
  172.1 224.1 %reduce-scatter.6.cloned.1.call-start = ((), (), s32[]{:S(2)}) async-start(), calls=%async_computation.9 | async-start | bytes 4718592 | tf_op jit(solution)/shard_map/reduce_scatter | solution.py:148
  191.3 52.1 %copy-start.9 = (f32[1536,384]{0,1:T(8,128)}, f32[1536,384]{0,1:T(8,128)S(1)}, u32[]{:S(2)}) copy-start(f32[1536,384]{0,1:T(8,128)S(1)} %fusion.7) | copy-start | bytes 7077892
  252.2 5.4 %copy-start.3 = (bf16[1536,384]{0,1:T(8,128)(2,1)}, bf16[1536,384]{0,1:T(8,128)(2,1)S(1)}, u32[]{:S(2)}) copy-start(bf16[1536,384]{0,1:T(8,128)(2,1)S(1)} %get-tuple-element.96) | copy-start | bytes 3538948
  308.9 1.9 copy-start
  309.0 116.8 %reduce-scatter.4.cloned.1.call-start = ((), (), s32[]{:S(2)}) async-start(), calls=%async_computation.8 | async-start | bytes 5308416 | tf_op jit(solution)/shard_map/reduce_scatter | solution.py:142
  368.6 149.8 %reduce-scatter.8.cloned.1.call-start = ((), (), s32[]{:S(2)}) async-start(), calls=%async_computation.10 | async-start | bytes 11796480 | tf_op jit(solution)/shard_map/reduce_scatter | solution.py:153
  368.7 5.2 copy-start.2
  373.8 7.2 %copy-start.10 = (f32[1536,384]{0,1:T(8,128)S(1)}, f32[1536,384]{0,1:T(8,128)}, u32[]{:S(2)}) copy-start(f32[1536,384]{0,1:T(8,128)} %copy-done.9) | copy-start | bytes 7077892
  373.8 7.2 %copy-start.11 = (f32[1536,384]{0,1:T(8,128)S(1)}, f32[1536,384]{0,1:T(8,128)}, u32[]{:S(2)}) copy-start(f32[1536,384]{0,1:T(8,128)} %fusion.9) | copy-start | bytes 7077892
Sparse Core Ops, SparseCore 0:
  13.9 61.0 all-gather.7
  76.8 53.4 all-gather.9
  132.1 53.7 all-gather.5
  309.1 52.4 reduce-scatter.5
  368.7 56.9 reduce-scatter.3
  428.2 90.1 reduce-scatter.7

commit v5 on v4

--- a/solution.py
+++ b/solution.py
@@ -139,6 +139,13 @@
         .at[..., :top_count]
         .set(pick_gate.astype(jnp.float32))
     )
+    summed = lax.psum_scatter(
+        jnp.concatenate([results[2], results[3], results[4]], axis=1),
+        "dp",
+        scatter_dimension=0,
+        tiled=True,
+    )
+    summed, partial_lo, gate_cols = lax.optimization_barrier((summed, partial_lo, gate_cols))
     reduced_lo = lax.psum_scatter(
         jnp.concatenate([partial_lo, gate_cols], axis=2), "lz", scatter_dimension=0, tiled=True
     )[0]
@@ -150,12 +157,6 @@
         [reduced_lo[:, :half], reduced_hi], axis=1
     ).astype(jnp.bfloat16)
     gate_grad = reduced_lo[:, half : half + top_count].astype(jnp.bfloat16)
-    summed = lax.psum_scatter(
-        jnp.concatenate([results[2], results[3], results[4]], axis=1),
-        "dp",
-        scatter_dimension=0,
-        tiled=True,
-    )
     return (
         input_grad,
         gate_grad,

time: 532 us -> 499 us (0.938)
  waiting for transfers between devices: 304 us -> 264 us
    reduce_scatter x1, waiting for transfers between devices: 90 us -> 0.01 us  [local(): lax.psum_scatter(jnp.concatenate([results[2], results[3], results[4]], ax...]
    reduce_scatter x1, waiting for transfers between devices: 28.4 us -> 55 us  [local(): lax.psum_scatter(jnp.concatenate([partial_lo, gate_cols], axis=2), 'lz',...]
    reduce_scatter x1, waiting for transfers between devices: 0.02 us -> 24.4 us  [local(): lax.psum_scatter(partial_hi, 'lz', scatter_dimension=0, tiled=True)[0]]
where the time goes in v5:
time: 499 us; the launch traced here: 497 us
  waiting for transfers between devices  264 us (53%)
  blocking collectives  85.6 us (17%)
  matrix products  67 us (13%)
  other arithmetic  30.9 us (6%)
  local copies, waits for them, and re-layouts  24.5 us (5%)
  between operations  14.4 us (3%)
  starting transfers between devices  10.6 us (2%)
    all_gather x1, waiting for transfers between devices, local(): lax.all_gather(jnp.concatenate([tokens, meta], axis=1), 'lz', axis=0, til...  60.5 us
    reduce_scatter x1, waiting for transfers between devices, local(): lax.psum_scatter(jnp.concatenate([partial_lo, gate_cols], axis=2), 'lz',...  55 us
    all_to_all x1, blocking collectives, local(): lax.all_to_all(back_lo, ('node', 'ly'), split_axis=0, concat_axis=0, tile...  44.6 us
    all_to_all x1, waiting for transfers between devices, local(): lax.all_to_all(send_dy, ('node', 'ly'), split_axis=0, concat_axis=0, tile...  44.2 us
    all_to_all x1, blocking collectives, local(): lax.all_to_all(back_hi, ('node', 'ly'), split_axis=0, concat_axis=0, tile...  41.1 us
    all_gather x1, waiting for transfers between devices, local(): seen_dy = lax.all_gather(cotangent, 'lz', axis=0, tiled=False)  37.4 us
    all_to_all x1, waiting for transfers between devices, local(): lax.all_to_all(send_x, ('node', 'ly'), split_axis=0, concat_axis=0, tiled...  30 us
    reduce_scatter x1, waiting for transfers between devices, local(): lax.psum_scatter(partial_hi, 'lz', scatter_dimension=0, tiled=True)[0]  24.4 us
  transfers between devices with their start and end apart: 8, of which 7 were waited for; matrix products, arithmetic and copies ran while one was open for 15% of the time, Pallas kernels for 0%

profile of v5, /device:TPU:1, one launch (start us, length us, event | category | flops | bytes accessed | tf_op | source)
XLA Modules:
  0.0 497.4 jit_solution(2130428037776248625)
XLA Ops:
  7.2 0.6 compare_reduce_fusion.3
  7.9 0.6 compare_reduce_fusion.2
  8.5 0.7 convert_element_type.61
  9.3 0.8 copy.80
  10.1 0.7 broadcast_select_fusion
  10.8 0.7 broadcast_select_fusion.1
  11.4 0.4 scatter.21
  11.9 1.9 pad_maximum_fusion.3
  13.8 0.7 all-gather.10.cloned.1.call-update
  14.5 60.5 %all-gather.8.cloned.1.call-done = bf16[1024,2176]{1,0:T(8,128)(2,1)} async-done(((bf16[128,2176]{1,0:T(8,128)(2,1)}), bf16[1024,2176]{1,0:T(8,128)(2,1)}) %all-gather.8.cloned.1.call-update) | async-done | bytes 4456464 | tf_op jit(solution)/shard_map/all_gather | solution.py:63
  75.0 1.2 fusion.60
  76.6 0.5 copy-done.5
  77.3 0.3 fusion.41
  77.7 0.5 copy.85
  78.1 4.0 convert_bitcast_fusion.1
  82.1 0.6 fusion.2
  82.8 3.4 copy.86
  86.1 5.5 %all-to-all-start = ((bf16[8,8,24,2176]{3,2,1,0:T(8,128)(2,1)}), bf16[8,8,24,2176]{3,2,1,0:T(8,128)(2,1)}, u32[]{:S(2)}, u32[]{:S(2)}) async-start(bf16[8,8,24,2176]{3,2,1,0:T(8,128)(2,1)} %copy.86), calls=%async_computation | async-start | bytes 13369344 | tf_op jit(solution)/shard_map/all_to_all | solution.py:107
  91.6 1.2 pad_maximum_fusion.2
  92.9 37.4 %all-gather.10.cloned.1.call-done = bf16[1024,2048]{1,0:T(8,128)(2,1)} async-done(((bf16[128,2048]{1,0:T(8,128)(2,1)}), bf16[1024,2048]{1,0:T(8,128)(2,1)}) %all-gather.10.cloned.1.call-update) | async-done | bytes 4194320 | tf_op jit(solution)/shard_map/all_gather | solution.py:64
  130.2 4.0 convert_bitcast_fusion
  134.2 3.2 copy.87
  137.4 30.0 %all-to-all-done = bf16[8,8,24,2176]{3,2,1,0:T(8,128)(2,1)} async-done(((bf16[8,8,24,2176]{3,2,1,0:T(8,128)(2,1)}), bf16[8,8,24,2176]{3,2,1,0:T(8,128)(2,1)}, u32[]{:S(2)}, u32[]{:S(2)}) %all-to-all-start) | async-done | bytes 6684704 | tf_op jit(solution)/shard_map/all_to_all | solution.py:107
  167.4 4.7 all-to-all-start.1
  172.1 0.2 reduce-scatter.4.cloned.1.call-start
  172.3 1.2 convert_reduce_fusion
  173.5 12.4 %all-gather.6.cloned.1.call-done = bf16[1,2048,1152]{2,1,0:T(8,128)(2,1)} async-done(((bf16[1,512,1152]{2,1,0:T(8,128)(2,1)}), bf16[1,2048,1152]{2,1,0:T(8,128)(2,1)}) %all-gather.6.cloned.1.call-update) | async-done | bytes 4718608 | tf_op jit(solution)/shard_map/all_gather | solution.py:101
  185.8 5.2 %fusion.7 = f32[1536,384]{0,1:T(8,128)S(1)} fusion(bf16[1536,2176]{1,0:T(8,128)(2,1)} %bitcast.9, bf16[2048,1152]{1,0:T(8,128)(2,1)} %bitcast.58), kind=kOutput, calls=%fused_computation.15 | convolution fusion | flops 2415919104 | bytes 10223616 | tf_op jit(solution)/shard_map/dot_general | solution.py:8
  191.1 8.1 %fusion.9 = f32[1536,384]{0,1:T(8,128)} fusion(bf16[1536,2176]{1,0:T(8,128)(2,1)} %bitcast.9, bf16[2048,1152]{1,0:T(8,128)(2,1)} %bitcast.59), kind=kOutput, calls=%fused_computation.17 | convolution fusion | flops 2415919104 | bytes 10223616 | tf_op jit(solution)/shard_map/dot_general | solution.py:9
  199.2 44.2 %all-to-all-done.1 = bf16[8,8,24,2048]{3,2,1,0:T(8,128)(2,1)} async-done(((bf16[8,8,24,2048]{3,2,1,0:T(8,128)(2,1)}), bf16[8,8,24,2048]{3,2,1,0:T(8,128)(2,1)}, u32[]{:S(2)}, u32[]{:S(2)}) %all-to-all-start.1) | async-done | bytes 6291488 | tf_op jit(solution)/shard_map/all_to_all | solution.py:108
  243.4 7.9 %multiply_reduce_fusion = (bf16[1536]{0:T(1024)(128)(2,1)S(1)}, bf16[1536,384]{0,1:T(8,128)(2,1)S(1)}, bf16[1536,384]{0,1:T(8,128)(2,1)S(1)}) fusion(f32[1536,384]{0,1:T(8,128)} %fusion.9, f32[1536,384]{0,1:T(8,128)S(1)} %fusion.7, f32[1536]{0:T(1024)S(1)} %convert_reduce_fusion, bf16[1536,2048]{1,0:T(8,128)(2,1)} %bitcast.14, bf16[2048,1152]{1,0:T(8,128)(2,1)} %bitcast.60), kind=kOutput, calls=%fused_computation.24 | convolution fusion | flops 2425944576 | bytes 14951424 | tf_op jit(solution)/shard_map/dot_general | solution.py:13
  251.3 6.8 %fusion.30 = f32[2048,384]{0,1:T(8,128)S(1)} fusion(bf16[1536,2048]{1,0:T(8,128)(2,1)} %bitcast.14, f32[1536]{0:T(1024)S(1)} %convert_reduce_fusion, f32[1536,384]{0,1:T(8,128)S(1)} %copy-done.10, f32[1536,384]{0,1:T(8,128)} %copy-done.9), kind=kOutput, calls=%fused_computation.39 | convolution fusion | flops 2420047872 | bytes 14161920 | tf_op jit(solution)/shard_map/dot_general | solution.py:23
  258.1 7.2 %fusion.3 = f32[2048,384]{0,1:T(8,128)} fusion(bf16[1536,384]{0,1:T(8,128)(2,1)S(1)} %get-tuple-element.102, bf16[1536,2176]{1,0:T(8,128)(2,1)} %bitcast.9), kind=kOutput, calls=%fused_computation.11 | convolution fusion | flops 2415919104 | bytes 10616832 | tf_op jit(solution)/shard_map/dot_general | solution.py:26
  265.3 7.1 %fusion.5 = f32[2048,384]{0,1:T(8,128)} fusion(bf16[1536,384]{0,1:T(8,128)(2,1)S(1)} %get-tuple-element.105, bf16[1536,2176]{1,0:T(8,128)(2,1)} %bitcast.9), kind=kOutput, calls=%fused_computation.13 | convolution fusion | flops 2415919104 | bytes 10616832 | tf_op jit(solution)/shard_map/dot_general | solution.py:29
  272.4 7.8 %pad_maximum_fusion = f32[2048,1152]{0,1:T(8,128)} fusion(f32[2048,384]{0,1:T(8,128)S(1)} %fusion.30, f32[2048,384]{0,1:T(8,128)} %fusion.5, f32[2048,384]{0,1:T(8,128)} %fusion.3), kind=kLoop, calls=%fused_computation.3 | loop fusion | flops 4718592 | bytes 18874368 | tf_op jit(solution)/shard_map/concatenate | solution.py:143
  280.3 1.2 copy-done.4
  281.5 4.9 fusion.25
  286.4 5.4 %add_convert_fusion = bf16[1536,2048]{1,0:T(8,128)(2,1)S(1)} fusion(f32[1536,2048]{1,0:T(8,128)S(1)} %fusion.25, bf16[1536,384]{0,1:T(8,128)(2,1)} %copy-done.2, bf16[2048,1152]{1,0:T(8,128)(2,1)} %bitcast.62), kind=kOutput, calls=%fused_computation.2 | convolution fusion | flops 2422210560 | bytes 21626880 | tf_op jit(solution)/shard_map/dot_general | solution.py:34
  291.9 2.4 fusion.59
  294.2 41.1 %all_to_all.20 = bf16[8,8,24,1024]{3,2,1,0:T(8,128)(2,1)S(1)} all-to-all(bf16[8,8,24,1024]{3,2,1,0:T(8,128)(2,1)S(1)} %bitcast.56), channel_id=1, replica_groups=mesh['dp'=4,'node'=2,'lz'=8,'ly'=4] {'node','ly'}, dimensions={0} | all-to-all | bytes 6291456 | tf_op jit(solution)/shard_map/all_to_all | solution.py:124
  335.3 2.8 fusion.17
  338.2 0.6 compare_reduce_fusion.1
  338.8 0.9 convert_select_fusion
  339.7 0.3 reshape.218
  340.0 0.4 fusion.11
  340.3 44.6 %all_to_all.21 = bf16[8,8,24,1152]{3,2,1,0:T(8,128)(2,1)S(1)} all-to-all(bf16[8,8,24,1152]{3,2,1,0:T(8,128)(2,1)S(1)} %bitcast.55), channel_id=1, replica_groups=mesh['dp'=4,'node'=2,'lz'=8,'ly'=4] {'node','ly'}, dimensions={0} | all-to-all | bytes 7077888 | tf_op jit(solution)/shard_map/all_to_all | solution.py:123
  384.9 0.8 slice.172
  385.7 2.0 copy.107
  387.8 1.2 fusion.42
  388.9 1.5 fusion.52
  390.5 1.6 copy.92
  392.0 1.8 pad_convert_fusion
  393.8 3.5 fusion.20
  397.3 5.0 pad_maximum_fusion.1
  402.2 24.4 %reduce-scatter.8.cloned.1.call-done = f32[1,128,1024]{2,1,0:T(8,128)} async-done(((f32[8,128,1024]{2,1,0:T(8,128)}), f32[1,128,1024]{2,1,0:T(8,128)}) %reduce-scatter.8.cloned.1.call-update) | async-done | bytes 524304 | tf_op jit(solution)/shard_map/reduce_scatter | solution.py:155
  426.6 1.1 convert_bitcast_fusion.3
  427.7 1.8 slice_bitcast_fusion.2
  429.5 1.1 copy.97
  430.6 1.1 copy.96
  431.8 1.1 copy.95
  432.9 55.0 %reduce-scatter.6.cloned.1.call-done = f32[1,128,1152]{2,1,0:T(8,128)} async-done(((f32[8,128,1152]{2,1,0:T(8,128)}), f32[1,128,1152]{2,1,0:T(8,128)}) %reduce-scatter.6.cloned.1.call-update) | async-done | bytes 589840 | tf_op jit(solution)/shard_map/reduce_scatter | solution.py:149
  487.9 1.1 convert_bitcast_fusion.2
  489.1 0.7 copy.94
  489.7 0.8 pad_maximum_fusion.4
  (42 shorter events, 1.1 us)
Async XLA Ops:
  7.2 67.8 %all-gather.8.cloned.1.call-start = ((), (), s32[]{:S(2)}) async-start(), calls=%async_computation.11 | async-start | bytes 5013504 | tf_op jit(solution)/shard_map/all_gather | solution.py:63
  13.8 116.5 %all-gather.10.cloned.1.call-start = ((), (), s32[]{:S(2)}) async-start(), calls=%async_computation.12 | async-start | bytes 4718592 | tf_op jit(solution)/shard_map/all_gather | solution.py:64
  76.4 0.6 copy-start.5
  77.3 258.0 %copy-start.1 = (s32[8,8,128]{2,0,1:T(8,128)}, s32[8,8,128]{2,0,1:T(8,128)S(1)}, u32[]{:S(2)}) copy-start(s32[8,8,128]{2,0,1:T(8,128)S(1)} %fusion.32) | copy-start | bytes 98308
  86.1 5.5 %copy-start.6 = (bf16[1,512,384]{2,1,0:T(8,128)(2,1)S(1)}, bf16[1,512,384]{2,1,0:T(8,128)(2,1)}, u32[]{:S(2)}) copy-start(bf16[1,512,384]{2,1,0:T(8,128)(2,1)} %param.23) | copy-start | bytes 1179652
  86.1 5.5 %copy-start.7 = (bf16[1,512,384]{2,1,0:T(8,128)(2,1)S(1)}, bf16[1,512,384]{2,1,0:T(8,128)(2,1)}, u32[]{:S(2)}) copy-start(bf16[1,512,384]{2,1,0:T(8,128)(2,1)} %param.22) | copy-start | bytes 1179652
  86.1 5.5 %copy-start.8 = (bf16[1,512,384]{2,1,0:T(8,128)(2,1)S(1)}, bf16[1,512,384]{2,1,0:T(8,128)(2,1)}, u32[]{:S(2)}) copy-start(bf16[1,512,384]{2,1,0:T(8,128)(2,1)} %param.21) | copy-start | bytes 1179652
  86.1 81.3 %all-to-all-start = ((bf16[8,8,24,2176]{3,2,1,0:T(8,128)(2,1)}), bf16[8,8,24,2176]{3,2,1,0:T(8,128)(2,1)}, u32[]{:S(2)}, u32[]{:S(2)}) async-start(bf16[8,8,24,2176]{3,2,1,0:T(8,128)(2,1)} %copy.86), calls=%async_computation | async-start | bytes 13369344 | tf_op jit(solution)/shard_map/all_to_all | solution.py:107
  91.6 94.2 %all-gather.6.cloned.1.call-start = ((), (), s32[]{:S(2)}) async-start(), calls=%async_computation.7 | async-start | bytes 5898240 | tf_op jit(solution)/shard_map/all_gather | solution.py:101
  167.4 76.0 %all-to-all-start.1 = ((bf16[8,8,24,2048]{3,2,1,0:T(8,128)(2,1)}), bf16[8,8,24,2048]{3,2,1,0:T(8,128)(2,1)}, u32[]{:S(2)}, u32[]{:S(2)}) async-start(bf16[8,8,24,2048]{3,2,1,0:T(8,128)(2,1)} %copy.87), calls=%async_computation.1 | async-start | bytes 12582912 | tf_op jit(solution)/shard_map/all_to_all | solution.py:108
  172.1 225.2 %reduce-scatter.4.cloned.1.call-start = ((), (), s32[]{:S(2)}) async-start(), calls=%async_computation.8 | async-start | bytes 11796480 | tf_op jit(solution)/shard_map/reduce_scatter | solution.py:142
  191.1 52.3 %copy-start.9 = (f32[1536,384]{0,1:T(8,128)}, f32[1536,384]{0,1:T(8,128)S(1)}, u32[]{:S(2)}) copy-start(f32[1536,384]{0,1:T(8,128)S(1)} %fusion.7) | copy-start | bytes 7077892
  243.4 7.9 %copy-start.10 = (f32[1536,384]{0,1:T(8,128)S(1)}, f32[1536,384]{0,1:T(8,128)}, u32[]{:S(2)}) copy-start(f32[1536,384]{0,1:T(8,128)} %fusion.9) | copy-start | bytes 7077892
  251.3 6.9 %copy-start.3 = (bf16[1536,384]{0,1:T(8,128)(2,1)}, bf16[1536,384]{0,1:T(8,128)(2,1)S(1)}, u32[]{:S(2)}) copy-start(bf16[1536,384]{0,1:T(8,128)(2,1)S(1)} %get-tuple-element.102) | copy-start | bytes 3538948
  251.3 14.1 %copy-start.2 = (bf16[1536,384]{0,1:T(8,128)(2,1)}, bf16[1536,384]{0,1:T(8,128)(2,1)S(1)}, u32[]{:S(2)}) copy-start(bf16[1536,384]{0,1:T(8,128)(2,1)S(1)} %get-tuple-element.105) | copy-start | bytes 3538948
  280.3 1.3 copy-start.4
  280.3 146.3 %reduce-scatter.8.cloned.1.call-start = ((), (), s32[]{:S(2)}) async-start(), calls=%async_computation.10 | async-start | bytes 4718592 | tf_op jit(solution)/shard_map/reduce_scatter | solution.py:155
  338.1 1.9 copy-start
  338.1 149.8 %reduce-scatter.6.cloned.1.call-start = ((), (), s32[]{:S(2)}) async-start(), calls=%async_computation.9 | async-start | bytes 5308416 | tf_op jit(solution)/shard_map/reduce_scatter | solution.py:149
Sparse Core Ops, SparseCore 0:
  13.9 61.0 all-gather.7
  76.8 53.4 all-gather.9
  132.1 53.7 all-gather.5
  280.4 88.6 reduce-scatter.3
  371.5 55.0 reduce-scatter.7
  429.0 58.8 reduce-scatter.5

commit v6 on v5

--- a/solution.py
+++ b/solution.py
@@ -94,10 +94,14 @@
     send_x = jnp.einsum(
         "jzrt,ztd->jzrd", choose_b, seen_x[:, :, :width], preferred_element_type=jnp.float32
     ).astype(jnp.bfloat16)
-    send_x = jnp.concatenate([send_x, gate_block], axis=3)
-    send_dy = jnp.einsum(
-        "jzrt,ztd->jzrd", choose_b, seen_dy, preferred_element_type=jnp.float32
-    ).astype(jnp.bfloat16)
+    send_x = jnp.concatenate([send_x, gate_block], axis=3).reshape(
+        near, planes * capacity, width + pad
+    )
+    send_dy = (
+        jnp.einsum("jzrt,ztd->jzrd", choose_b, seen_dy, preferred_element_type=jnp.float32)
+        .astype(jnp.bfloat16)
+        .reshape(near, planes * capacity, width)
+    )
     all_weights = lax.all_gather(
         jnp.concatenate([w_gate, w_up, w_down], axis=2), "dp", axis=1, tiled=True
     )[0]
@@ -117,11 +121,15 @@
     )
     grad_block = jnp.zeros((slots, pad), jnp.bfloat16).at[:, 0].set(results[1])
     back_lo = jnp.concatenate([results[0][:, :half], grad_block], axis=1).reshape(
-        near, planes, capacity, half + pad
+        near, planes * capacity, half + pad
     )
-    back_hi = results[0][:, half:].reshape(near, planes, capacity, width - half)
-    home_lo = lax.all_to_all(back_lo, ("node", "ly"), split_axis=0, concat_axis=0, tiled=True)
-    home_hi = lax.all_to_all(back_hi, ("node", "ly"), split_axis=0, concat_axis=0, tiled=True)
+    back_hi = results[0][:, half:].reshape(near, planes * capacity, width - half)
+    home_lo = lax.all_to_all(
+        back_lo, ("node", "ly"), split_axis=0, concat_axis=0, tiled=True
+    ).reshape(near, planes, capacity, half + pad)
+    home_hi = lax.all_to_all(
+        back_hi, ("node", "ly"), split_axis=0, concat_axis=0, tiled=True
+    ).reshape(near, planes, capacity, width - half)
     partial_lo = jnp.einsum(
         "jzrt,jzrd->ztd", choose_b, home_lo[..., :half], preferred_element_type=jnp.float32
     )

time: 499 us -> 499 us (level)
  no operation moved by 1% of the time
where the time goes in v6:
time: 499 us; the launch traced here: 497 us
  waiting for transfers between devices  264 us (53%)
  blocking collectives  85.6 us (17%)
  matrix products  67 us (13%)
  other arithmetic  29.7 us (6%)
  local copies, waits for them, and re-layouts  25.7 us (5%)
  between operations  14.4 us (3%)
  starting transfers between devices  10.6 us (2%)
    all_gather x1, waiting for transfers between devices, local(): lax.all_gather(jnp.concatenate([tokens, meta], axis=1), 'lz', axis=0, til...  60.5 us
    reduce_scatter x1, waiting for transfers between devices, local(): lax.psum_scatter(jnp.concatenate([partial_lo, gate_cols], axis=2), 'lz',...  55 us
    all_to_all x1, blocking collectives, local(): lax.all_to_all(back_lo, ('node', 'ly'), split_axis=0, concat_axis=0, tile...  44.6 us
    all_to_all x1, waiting for transfers between devices, local(): lax.all_to_all(send_dy, ('node', 'ly'), split_axis=0, concat_axis=0, tile...  44.2 us
    all_to_all x1, blocking collectives, local(): lax.all_to_all(back_hi, ('node', 'ly'), split_axis=0, concat_axis=0, tile...  41 us
    all_gather x1, waiting for transfers between devices, local(): seen_dy = lax.all_gather(cotangent, 'lz', axis=0, tiled=False)  37.4 us
    all_to_all x1, waiting for transfers between devices, local(): lax.all_to_all(send_x, ('node', 'ly'), split_axis=0, concat_axis=0, tiled...  30 us
    reduce_scatter x1, waiting for transfers between devices, local(): lax.psum_scatter(partial_hi, 'lz', scatter_dimension=0, tiled=True)[0]  24.4 us
  transfers between devices with their start and end apart: 8, of which 7 were waited for; matrix products, arithmetic and copies ran while one was open for 15% of the time, Pallas kernels for 0%

profile of v6, /device:TPU:1, one launch (start us, length us, event | category | flops | bytes accessed | tf_op | source)
XLA Modules:
  0.0 497.4 jit_solution(5101339825587483676)
XLA Ops:
  7.2 0.6 compare_reduce_fusion.3
  7.9 0.6 compare_reduce_fusion.2
  8.5 0.7 convert_element_type.61
  9.3 0.8 copy.78
  10.1 0.7 broadcast_select_fusion
  10.8 0.7 broadcast_select_fusion.1
  11.4 0.4 scatter.21
  11.9 1.9 pad_maximum_fusion.3
  13.8 0.7 all-gather.10.cloned.1.call-update
  14.5 60.5 %all-gather.8.cloned.1.call-done = bf16[1024,2176]{1,0:T(8,128)(2,1)} async-done(((bf16[128,2176]{1,0:T(8,128)(2,1)}), bf16[1024,2176]{1,0:T(8,128)(2,1)}) %all-gather.8.cloned.1.call-update) | async-done | bytes 4456464 | tf_op jit(solution)/shard_map/all_gather | solution.py:63
  75.0 1.2 fusion.60
  76.6 0.5 copy-done.5
  77.3 0.3 fusion.41
  77.7 0.5 copy.83
  78.1 4.0 convert_bitcast_fusion.1
  82.1 0.6 fusion.2
  82.8 3.4 copy.84
  86.1 5.5 %all-to-all-start = ((bf16[8,192,2176]{2,1,0:T(8,128)(2,1)}), bf16[8,192,2176]{2,1,0:T(8,128)(2,1)}, u32[]{:S(2)}, u32[]{:S(2)}) async-start(bf16[8,192,2176]{2,1,0:T(8,128)(2,1)} %bitcast.58), calls=%async_computation | async-start | bytes 13369344 | tf_op jit(solution)/shard_map/all_to_all | solution.py:111
  91.6 1.2 pad_maximum_fusion.2
  92.9 37.4 %all-gather.10.cloned.1.call-done = bf16[1024,2048]{1,0:T(8,128)(2,1)} async-done(((bf16[128,2048]{1,0:T(8,128)(2,1)}), bf16[1024,2048]{1,0:T(8,128)(2,1)}) %all-gather.10.cloned.1.call-update) | async-done | bytes 4194320 | tf_op jit(solution)/shard_map/all_gather | solution.py:64
  130.2 4.0 convert_bitcast_fusion
  134.2 3.2 copy.86
  137.4 30.0 %all-to-all-done = bf16[8,192,2176]{2,1,0:T(8,128)(2,1)} async-done(((bf16[8,192,2176]{2,1,0:T(8,128)(2,1)}), bf16[8,192,2176]{2,1,0:T(8,128)(2,1)}, u32[]{:S(2)}, u32[]{:S(2)}) %all-to-all-start) | async-done | bytes 6684704 | tf_op jit(solution)/shard_map/all_to_all | solution.py:111
  167.4 4.7 all-to-all-start.1
  172.1 0.2 reduce-scatter.4.cloned.1.call-start
  172.3 1.0 slice.165
  173.6 12.3 %all-gather.6.cloned.1.call-done = bf16[1,2048,1152]{2,1,0:T(8,128)(2,1)} async-done(((bf16[1,512,1152]{2,1,0:T(8,128)(2,1)}), bf16[1,2048,1152]{2,1,0:T(8,128)(2,1)}) %all-gather.6.cloned.1.call-update) | async-done | bytes 4718608 | tf_op jit(solution)/shard_map/all_gather | solution.py:105
  185.8 5.2 %fusion.7 = f32[1536,384]{0,1:T(8,128)S(1)} fusion(bf16[1536,2176]{1,0:T(8,128)(2,1)} %bitcast.10, bf16[2048,1152]{1,0:T(8,128)(2,1)} %bitcast.66), kind=kOutput, calls=%fused_computation.15 | convolution fusion | flops 2415919104 | bytes 10223616 | tf_op jit(solution)/shard_map/dot_general | solution.py:8
  191.1 8.1 %fusion.9 = f32[1536,384]{0,1:T(8,128)} fusion(bf16[1536,2176]{1,0:T(8,128)(2,1)} %bitcast.10, bf16[2048,1152]{1,0:T(8,128)(2,1)} %bitcast.67), kind=kOutput, calls=%fused_computation.17 | convolution fusion | flops 2415919104 | bytes 10223616 | tf_op jit(solution)/shard_map/dot_general | solution.py:9
  199.2 44.2 %all-to-all-done.1 = bf16[8,192,2048]{2,1,0:T(8,128)(2,1)} async-done(((bf16[8,192,2048]{2,1,0:T(8,128)(2,1)}), bf16[8,192,2048]{2,1,0:T(8,128)(2,1)}, u32[]{:S(2)}, u32[]{:S(2)}) %all-to-all-start.1) | async-done | bytes 6291488 | tf_op jit(solution)/shard_map/all_to_all | solution.py:112
  243.4 7.9 %multiply_reduce_fusion = (bf16[1536]{0:T(1024)(128)(2,1)S(1)}, bf16[1536,384]{0,1:T(8,128)(2,1)S(1)}, bf16[1536,384]{0,1:T(8,128)(2,1)S(1)}) fusion(f32[1536,384]{0,1:T(8,128)} %fusion.9, f32[1536,384]{0,1:T(8,128)S(1)} %fusion.7, f32[1536]{0:T(1024)S(1)} %convert_reduce_fusion, bf16[1536,2048]{1,0:T(8,128)(2,1)} %bitcast.16, bf16[2048,1152]{1,0:T(8,128)(2,1)} %bitcast.68), kind=kOutput, calls=%fused_computation.24 | convolution fusion | flops 2425944576 | bytes 14951424 | tf_op jit(solution)/shard_map/dot_general | solution.py:13
  251.3 6.8 %fusion.30 = f32[2048,384]{0,1:T(8,128)S(1)} fusion(bf16[1536,2048]{1,0:T(8,128)(2,1)} %bitcast.16, f32[1536]{0:T(1024)S(1)} %convert_reduce_fusion, f32[1536,384]{0,1:T(8,128)S(1)} %copy-done.10, f32[1536,384]{0,1:T(8,128)} %copy-done.9), kind=kOutput, calls=%fused_computation.39 | convolution fusion | flops 2420047872 | bytes 14161920 | tf_op jit(solution)/shard_map/dot_general | solution.py:23
  258.1 7.2 %fusion.3 = f32[2048,384]{0,1:T(8,128)} fusion(bf16[1536,384]{0,1:T(8,128)(2,1)S(1)} %get-tuple-element.102, bf16[1536,2176]{1,0:T(8,128)(2,1)} %bitcast.10), kind=kOutput, calls=%fused_computation.11 | convolution fusion | flops 2415919104 | bytes 10616832 | tf_op jit(solution)/shard_map/dot_general | solution.py:26
  265.3 7.1 %fusion.5 = f32[2048,384]{0,1:T(8,128)} fusion(bf16[1536,384]{0,1:T(8,128)(2,1)S(1)} %get-tuple-element.105, bf16[1536,2176]{1,0:T(8,128)(2,1)} %bitcast.10), kind=kOutput, calls=%fused_computation.13 | convolution fusion | flops 2415919104 | bytes 10616832 | tf_op jit(solution)/shard_map/dot_general | solution.py:29
  272.5 7.8 %pad_maximum_fusion = f32[2048,1152]{0,1:T(8,128)} fusion(f32[2048,384]{0,1:T(8,128)S(1)} %fusion.30, f32[2048,384]{0,1:T(8,128)} %fusion.5, f32[2048,384]{0,1:T(8,128)} %fusion.3), kind=kLoop, calls=%fused_computation.3 | loop fusion | flops 4718592 | bytes 18874368 | tf_op jit(solution)/shard_map/concatenate | solution.py:151
  280.4 1.2 copy-done.4
  281.6 4.9 fusion.25
  286.5 5.4 %add_convert_fusion = bf16[1536,2048]{1,0:T(8,128)(2,1)S(1)} fusion(f32[1536,2048]{1,0:T(8,128)S(1)} %fusion.25, bf16[1536,384]{0,1:T(8,128)(2,1)} %copy-done.2, bf16[2048,1152]{1,0:T(8,128)(2,1)} %bitcast.70), kind=kOutput, calls=%fused_computation.2 | convolution fusion | flops 2422210560 | bytes 21626880 | tf_op jit(solution)/shard_map/dot_general | solution.py:34
  291.9 2.4 fusion.59
  294.2 41.0 %all_to_all.20 = bf16[8,192,1024]{2,1,0:T(8,128)(2,1)S(1)} all-to-all(bf16[8,192,1024]{2,1,0:T(8,128)(2,1)S(1)} %bitcast.64), channel_id=1, replica_groups=mesh['dp'=4,'node'=2,'lz'=8,'ly'=4] {'node','ly'}, dimensions={0} | all-to-all | bytes 6291456 | tf_op jit(solution)/shard_map/all_to_all | solution.py:130
  335.3 2.8 fusion.17
  338.2 0.6 compare_reduce_fusion.1
  338.8 0.9 convert_select_fusion
  339.7 0.3 reshape.234
  340.0 0.4 fusion.11
  340.4 44.6 %all_to_all.21 = bf16[8,192,1152]{2,1,0:T(8,128)(2,1)S(1)} all-to-all(bf16[8,192,1152]{2,1,0:T(8,128)(2,1)S(1)} %bitcast.62), channel_id=1, replica_groups=mesh['dp'=4,'node'=2,'lz'=8,'ly'=4] {'node','ly'}, dimensions={0} | all-to-all | bytes 7077888 | tf_op jit(solution)/shard_map/all_to_all | solution.py:127
  384.9 0.8 slice.172
  385.7 2.0 copy.102
  387.8 1.2 fusion.42
  389.0 1.5 fusion.52
  390.5 1.6 copy.90
  392.0 1.8 pad_convert_fusion
  393.8 3.5 fusion.20
  397.3 5.0 pad_maximum_fusion.1
  402.2 24.4 %reduce-scatter.8.cloned.1.call-done = f32[1,128,1024]{2,1,0:T(8,128)} async-done(((f32[8,128,1024]{2,1,0:T(8,128)}), f32[1,128,1024]{2,1,0:T(8,128)}) %reduce-scatter.8.cloned.1.call-update) | async-done | bytes 524304 | tf_op jit(solution)/shard_map/reduce_scatter | solution.py:163
  426.6 1.1 convert_bitcast_fusion.3
  427.7 1.8 slice_bitcast_fusion.2
  429.5 1.1 copy.95
  430.7 1.1 copy.94
  431.8 1.1 copy.93
  433.0 55.0 %reduce-scatter.6.cloned.1.call-done = f32[1,128,1152]{2,1,0:T(8,128)} async-done(((f32[8,128,1152]{2,1,0:T(8,128)}), f32[1,128,1152]{2,1,0:T(8,128)}) %reduce-scatter.6.cloned.1.call-update) | async-done | bytes 589840 | tf_op jit(solution)/shard_map/reduce_scatter | solution.py:157
  488.0 1.1 convert_bitcast_fusion.2
  489.1 0.7 copy.92
  489.8 0.8 pad_maximum_fusion.4
  (44 shorter events, 1.3 us)
Async XLA Ops:
  7.2 67.8 %all-gather.8.cloned.1.call-start = ((), (), s32[]{:S(2)}) async-start(), calls=%async_computation.11 | async-start | bytes 5013504 | tf_op jit(solution)/shard_map/all_gather | solution.py:63
  13.8 116.5 %all-gather.10.cloned.1.call-start = ((), (), s32[]{:S(2)}) async-start(), calls=%async_computation.12 | async-start | bytes 4718592 | tf_op jit(solution)/shard_map/all_gather | solution.py:64
  76.4 0.6 copy-start.5
  77.3 258.0 %copy-start.1 = (s32[8,8,128]{2,0,1:T(8,128)}, s32[8,8,128]{2,0,1:T(8,128)S(1)}, u32[]{:S(2)}) copy-start(s32[8,8,128]{2,0,1:T(8,128)S(1)} %fusion.32) | copy-start | bytes 98308
  86.1 5.5 %copy-start.6 = (bf16[1,512,384]{2,1,0:T(8,128)(2,1)S(1)}, bf16[1,512,384]{2,1,0:T(8,128)(2,1)}, u32[]{:S(2)}) copy-start(bf16[1,512,384]{2,1,0:T(8,128)(2,1)} %param.23) | copy-start | bytes 1179652
  86.1 5.5 %copy-start.7 = (bf16[1,512,384]{2,1,0:T(8,128)(2,1)S(1)}, bf16[1,512,384]{2,1,0:T(8,128)(2,1)}, u32[]{:S(2)}) copy-start(bf16[1,512,384]{2,1,0:T(8,128)(2,1)} %param.22) | copy-start | bytes 1179652
  86.1 5.5 %copy-start.8 = (bf16[1,512,384]{2,1,0:T(8,128)(2,1)S(1)}, bf16[1,512,384]{2,1,0:T(8,128)(2,1)}, u32[]{:S(2)}) copy-start(bf16[1,512,384]{2,1,0:T(8,128)(2,1)} %param.21) | copy-start | bytes 1179652
  86.1 81.3 %all-to-all-start = ((bf16[8,192,2176]{2,1,0:T(8,128)(2,1)}), bf16[8,192,2176]{2,1,0:T(8,128)(2,1)}, u32[]{:S(2)}, u32[]{:S(2)}) async-start(bf16[8,192,2176]{2,1,0:T(8,128)(2,1)} %bitcast.58), calls=%async_computation | async-start | bytes 13369344 | tf_op jit(solution)/shard_map/all_to_all | solution.py:111
  91.6 94.2 %all-gather.6.cloned.1.call-start = ((), (), s32[]{:S(2)}) async-start(), calls=%async_computation.7 | async-start | bytes 5898240 | tf_op jit(solution)/shard_map/all_gather | solution.py:105
  167.4 76.0 %all-to-all-start.1 = ((bf16[8,192,2048]{2,1,0:T(8,128)(2,1)}), bf16[8,192,2048]{2,1,0:T(8,128)(2,1)}, u32[]{:S(2)}, u32[]{:S(2)}) async-start(bf16[8,192,2048]{2,1,0:T(8,128)(2,1)} %bitcast.59), calls=%async_computation.1 | async-start | bytes 12582912 | tf_op jit(solution)/shard_map/all_to_all | solution.py:112
  172.1 225.2 %reduce-scatter.4.cloned.1.call-start = ((), (), s32[]{:S(2)}) async-start(), calls=%async_computation.8 | async-start | bytes 11796480 | tf_op jit(solution)/shard_map/reduce_scatter | solution.py:150
  191.1 52.3 %copy-start.9 = (f32[1536,384]{0,1:T(8,128)}, f32[1536,384]{0,1:T(8,128)S(1)}, u32[]{:S(2)}) copy-start(f32[1536,384]{0,1:T(8,128)S(1)} %fusion.7) | copy-start | bytes 7077892
  243.4 7.9 %copy-start.10 = (f32[1536,384]{0,1:T(8,128)S(1)}, f32[1536,384]{0,1:T(8,128)}, u32[]{:S(2)}) copy-start(f32[1536,384]{0,1:T(8,128)} %fusion.9) | copy-start | bytes 7077892
  251.3 6.9 %copy-start.3 = (bf16[1536,384]{0,1:T(8,128)(2,1)}, bf16[1536,384]{0,1:T(8,128)(2,1)S(1)}, u32[]{:S(2)}) copy-start(bf16[1536,384]{0,1:T(8,128)(2,1)S(1)} %get-tuple-element.102) | copy-start | bytes 3538948
  251.3 14.0 %copy-start.2 = (bf16[1536,384]{0,1:T(8,128)(2,1)}, bf16[1536,384]{0,1:T(8,128)(2,1)S(1)}, u32[]{:S(2)}) copy-start(bf16[1536,384]{0,1:T(8,128)(2,1)S(1)} %get-tuple-element.105) | copy-start | bytes 3538948
  280.3 1.3 copy-start.4
  280.3 146.3 %reduce-scatter.8.cloned.1.call-start = ((), (), s32[]{:S(2)}) async-start(), calls=%async_computation.10 | async-start | bytes 4718592 | tf_op jit(solution)/shard_map/reduce_scatter | solution.py:163
  338.1 1.9 copy-start
  338.1 149.8 %reduce-scatter.6.cloned.1.call-start = ((), (), s32[]{:S(2)}) async-start(), calls=%async_computation.9 | async-start | bytes 5308416 | tf_op jit(solution)/shard_map/reduce_scatter | solution.py:157
Sparse Core Ops, SparseCore 0:
  13.9 61.0 all-gather.7
  76.8 53.4 all-gather.9
  132.1 53.7 all-gather.5
  280.4 88.6 reduce-scatter.3
  371.5 55.0 reduce-scatter.7
  429.0 58.8 reduce-scatter.5

commit v7 on v6

--- a/solution.py
+++ b/solution.py
@@ -35,6 +35,27 @@
         pre_up_grad, up_proj, over_hidden, preferred_element_type=jnp.float32
     )
     return (input_rows.astype(jnp.bfloat16), gate_grad, gate_wgrad, up_wgrad, down_grad)
+
+
+def ring_sum_scatter(full):
+    ring = lax.axis_size("dp")
+    rank = lax.axis_index("dp")
+    rows = full.shape[0] // ring
+    split = full.shape[1] // 2
+    to_right = [(i, (i + 1) % ring) for i in range(ring)]
+    to_left = [(i, (i - 1) % ring) for i in range(ring)]
+
+    def block(index, lo, hi):
+        start = ((index % ring + ring) % ring) * rows
+        return lax.dynamic_slice(full, (start, lo), (rows, hi - lo))
+
+    width = full.shape[1]
+    right = block(rank - 1, 0, split)
+    left = block(rank + 1, split, width)
+    for step in range(2, ring + 1):
+        right = lax.ppermute(right, "dp", to_right) + block(rank - step, 0, split)
+        left = lax.ppermute(left, "dp", to_left) + block(rank + step, split, width)
+    return jnp.concatenate([right, left], axis=1)
 
 
 def local(tokens, cotangent, routes, gates, w_gate, w_up, w_down):
@@ -147,13 +168,6 @@
         .at[..., :top_count]
         .set(pick_gate.astype(jnp.float32))
     )
-    summed = lax.psum_scatter(
-        jnp.concatenate([results[2], results[3], results[4]], axis=1),
-        "dp",
-        scatter_dimension=0,
-        tiled=True,
-    )
-    summed, partial_lo, gate_cols = lax.optimization_barrier((summed, partial_lo, gate_cols))
     reduced_lo = lax.psum_scatter(
         jnp.concatenate([partial_lo, gate_cols], axis=2), "lz", scatter_dimension=0, tiled=True
     )[0]
@@ -165,6 +179,7 @@
         [reduced_lo[:, :half], reduced_hi], axis=1
     ).astype(jnp.bfloat16)
     gate_grad = reduced_lo[:, half : half + top_count].astype(jnp.bfloat16)
+    summed = ring_sum_scatter(jnp.concatenate([results[2], results[3], results[4]], axis=1))
     return (
         input_grad,
         gate_grad,

time: 499 us -> 516 us (1.034); the launches traced: 497 us -> 507 us
  starting transfers between devices: 10.6 us -> 16.1 us
    ppermute x0 -> x6, waiting for transfers between devices: none -> 80.5 us  [the longest x3 74.4 us: ring_sum_scatter(): left = lax.ppermute(left, 'dp', to_left) + block(rank + step, split, width)]
    reduce_scatter x1, waiting for transfers between devices: 55 us -> 0.02 us  [local(): lax.psum_scatter(jnp.concatenate([partial_lo, gate_cols], axis=2), 'lz',...]
    reduce_scatter x1, waiting for transfers between devices: 24.4 us -> 0.01 us  [local(): lax.psum_scatter(partial_hi, 'lz', scatter_dimension=0, tiled=True)[0]]
    add x0 -> x3, other arithmetic: none -> 8.63 us  [ring_sum_scatter(): left = lax.ppermute(left, 'dp', to_left) + block(rank + step, split, width)]
    ppermute x0 -> x6, starting transfers between devices: none -> 5.72 us  [the longest x3 2.97 us: ring_sum_scatter(): left = lax.ppermute(left, 'dp', to_left) + block(rank + step, split, width)]
  transfers between devices with their start and end apart: 8 -> 13, of which waited for: 7 -> 11; matrix products, arithmetic and copies ran while one was open for 15% -> 18% of each run, Pallas kernels for 0% -> 0%
where the time goes in v7:
time: 516 us; the launch traced here: 507 us
  waiting for transfers between devices  265 us (51%)
  blocking collectives  85.9 us (17%)
  matrix products  65.4 us (13%)
  other arithmetic  34.7 us (7%)
  local copies, waits for them, and re-layouts  25.3 us (5%)
  starting transfers between devices  16.1 us (3%)
  between operations  14.7 us (3%)
    ppermute x3, waiting for transfers between devices, ring_sum_scatter(): left = lax.ppermute(left, 'dp', to_left) + block(rank + step, split, width)  74.4 us
    all_gather x1, waiting for transfers between devices, local(): lax.all_gather(jnp.concatenate([tokens, meta], axis=1), 'lz', axis=0, til...  60.5 us
    all_to_all x1, blocking collectives, local(): lax.all_to_all(back_lo, ('node', 'ly'), split_axis=0, concat_axis=0, tile...  45.3 us
    all_to_all x1, waiting for transfers between devices, local(): lax.all_to_all(send_dy, ('node', 'ly'), split_axis=0, concat_axis=0, tile...  43.9 us
    all_to_all x1, blocking collectives, local(): lax.all_to_all(back_hi, ('node', 'ly'), split_axis=0, concat_axis=0, tile...  40.7 us
    all_gather x1, waiting for transfers between devices, local(): seen_dy = lax.all_gather(cotangent, 'lz', axis=0, tiled=False)  37.3 us
    all_to_all x1, waiting for transfers between devices, local(): lax.all_to_all(send_x, ('node', 'ly'), split_axis=0, concat_axis=0, tiled...  30 us
    all_gather x1, waiting for transfers between devices, local(): lax.all_gather(jnp.concatenate([w_gate, w_up, w_down], axis=2), 'dp', axi...  12.4 us
  transfers between devices with their start and end apart: 13, of which 11 were waited for; matrix products, arithmetic and copies ran while one was open for 18% of the time, Pallas kernels for 0%

profile of v7, /device:TPU:1, one launch (start us, length us, event | category | flops | bytes accessed | tf_op | source)
XLA Modules:
  0.0 507.5 jit_solution(6280797074014300413)
XLA Ops:
  8.5 0.7 convert_element_type.61
  9.3 0.8 copy.78
  10.1 0.7 broadcast_select_fusion
  10.8 0.7 broadcast_select_fusion.1
  11.9 1.9 pad_maximum_fusion.4
  13.8 0.7 all-gather.10.cloned.1.call-update
  14.6 60.5 %all-gather.8.cloned.1.call-done = bf16[1024,2176]{1,0:T(8,128)(2,1)} async-done(((bf16[128,2176]{1,0:T(8,128)(2,1)}), bf16[1024,2176]{1,0:T(8,128)(2,1)}) %all-gather.8.cloned.1.call-update) | async-done | bytes 4456464 | tf_op jit(solution)/shard_map/all_gather | solution.py:84
  75.0 1.2 fusion.61
  78.1 4.0 convert_bitcast_fusion.1
  82.1 0.6 fusion.2
  82.8 3.4 copy.84
  86.1 5.5 %all-to-all-start = ((bf16[8,192,2176]{2,1,0:T(8,128)(2,1)}), bf16[8,192,2176]{2,1,0:T(8,128)(2,1)}, u32[]{:S(2)}, u32[]{:S(2)}) async-start(bf16[8,192,2176]{2,1,0:T(8,128)(2,1)} %bitcast.58), calls=%async_computation | async-start | bytes 13369344 | tf_op jit(solution)/shard_map/all_to_all | solution.py:132
  91.7 1.2 pad_maximum_fusion.2
  92.9 37.3 %all-gather.10.cloned.1.call-done = bf16[1024,2048]{1,0:T(8,128)(2,1)} async-done(((bf16[128,2048]{1,0:T(8,128)(2,1)}), bf16[1024,2048]{1,0:T(8,128)(2,1)}) %all-gather.10.cloned.1.call-update) | async-done | bytes 4194320 | tf_op jit(solution)/shard_map/all_gather | solution.py:85
  130.2 4.0 convert_bitcast_fusion
  134.2 3.2 copy.86
  137.4 30.0 %all-to-all-done = bf16[8,192,2176]{2,1,0:T(8,128)(2,1)} async-done(((bf16[8,192,2176]{2,1,0:T(8,128)(2,1)}), bf16[8,192,2176]{2,1,0:T(8,128)(2,1)}, u32[]{:S(2)}, u32[]{:S(2)}) %all-to-all-start) | async-done | bytes 6684704 | tf_op jit(solution)/shard_map/all_to_all | solution.py:132
  167.4 4.7 all-to-all-start.1
  172.2 1.0 slice.165
  173.4 12.4 %all-gather.6.cloned.1.call-done = bf16[1,2048,1152]{2,1,0:T(8,128)(2,1)} async-done(((bf16[1,512,1152]{2,1,0:T(8,128)(2,1)}), bf16[1,2048,1152]{2,1,0:T(8,128)(2,1)}) %all-gather.6.cloned.1.call-update) | async-done | bytes 4718608 | tf_op jit(solution)/shard_map/all_gather | solution.py:126
  185.8 5.4 %fusion.7 = f32[1536,384]{0,1:T(8,128)S(1)} fusion(bf16[1536,2176]{1,0:T(8,128)(2,1)} %bitcast.10, bf16[2048,1152]{1,0:T(8,128)(2,1)} %bitcast.66), kind=kOutput, calls=%fused_computation.15 | convolution fusion | flops 2415919104 | bytes 10223616 | tf_op jit(solution)/shard_map/dot_general | solution.py:8
  191.3 8.2 %fusion.9 = f32[1536,384]{0,1:T(8,128)} fusion(bf16[1536,2176]{1,0:T(8,128)(2,1)} %bitcast.10, bf16[2048,1152]{1,0:T(8,128)(2,1)} %bitcast.67), kind=kOutput, calls=%fused_computation.17 | convolution fusion | flops 2415919104 | bytes 10223616 | tf_op jit(solution)/shard_map/dot_general | solution.py:9
  199.5 43.9 %all-to-all-done.1 = bf16[8,192,2048]{2,1,0:T(8,128)(2,1)} async-done(((bf16[8,192,2048]{2,1,0:T(8,128)(2,1)}), bf16[8,192,2048]{2,1,0:T(8,128)(2,1)}, u32[]{:S(2)}, u32[]{:S(2)}) %all-to-all-start.1) | async-done | bytes 6291488 | tf_op jit(solution)/shard_map/all_to_all | solution.py:133
  243.4 8.8 %multiply_reduce_fusion = (bf16[1536]{0:T(1024)(128)(2,1)S(1)}, bf16[1536,384]{0,1:T(8,128)(2,1)S(1)}, bf16[1536,384]{0,1:T(8,128)(2,1)}) fusion(f32[1536,384]{0,1:T(8,128)} %fusion.9, f32[1536,384]{0,1:T(8,128)S(1)} %fusion.7, f32[1536]{0:T(1024)S(1)} %convert_reduce_fusion, bf16[1536,2048]{1,0:T(8,128)(2,1)} %bitcast.16, bf16[2048,1152]{1,0:T(8,128)(2,1)} %bitcast.68), kind=kOutput, calls=%fused_computation.25 | convolution fusion | flops 2425944576 | bytes 14951424 | tf_op jit(solution)/shard_map/dot_general | solution.py:13
  252.2 5.4 %fusion.25 = f32[1536,2048]{1,0:T(8,128)S(1)} fusion(bf16[1536,384]{0,1:T(8,128)(2,1)S(1)} %get-tuple-element.104, bf16[2048,1152]{1,0:T(8,128)(2,1)} %bitcast.69), kind=kOutput, calls=%fused_computation.34 | convolution fusion | flops 2415919104 | bytes 15335424 | tf_op jit(solution)/shard_map/dot_general | solution.py:31
  257.6 5.6 %add_convert_fusion = bf16[1536,2048]{1,0:T(8,128)(2,1)S(1)} fusion(f32[1536,2048]{1,0:T(8,128)S(1)} %fusion.25, bf16[1536,384]{0,1:T(8,128)(2,1)} %get-tuple-element.107, bf16[2048,1152]{1,0:T(8,128)(2,1)} %bitcast.70), kind=kOutput, calls=%fused_computation.2 | convolution fusion | flops 2422210560 | bytes 21626880 | tf_op jit(solution)/shard_map/dot_general | solution.py:34
  263.3 2.3 fusion.60
  265.6 40.7 %all_to_all.20 = bf16[8,192,1024]{2,1,0:T(8,128)(2,1)S(1)} all-to-all(bf16[8,192,1024]{2,1,0:T(8,128)(2,1)S(1)} %bitcast.64), channel_id=1, replica_groups=mesh['dp'=4,'node'=2,'lz'=8,'ly'=4] {'node','ly'}, dimensions={0} | all-to-all | bytes 6291456 | tf_op jit(solution)/shard_map/all_to_all | solution.py:151
  306.3 2.7 fusion.17
  309.1 0.8 convert_select_fusion
  310.2 0.7 copy-done
  311.3 45.3 %all_to_all.21 = bf16[8,192,1152]{2,1,0:T(8,128)(2,1)S(1)} all-to-all(bf16[8,192,1152]{2,1,0:T(8,128)(2,1)S(1)} %bitcast.62), channel_id=1, replica_groups=mesh['dp'=4,'node'=2,'lz'=8,'ly'=4] {'node','ly'}, dimensions={0} | all-to-all | bytes 7077888 | tf_op jit(solution)/shard_map/all_to_all | solution.py:148
  356.6 0.8 slice.172
  357.4 2.0 copy.102
  359.4 1.2 fusion.43
  360.6 1.5 fusion.53
  362.1 1.6 copy.90
  363.7 1.0 pad_convert_fusion
  364.7 1.5 fusion.20
  366.2 2.5 pad_maximum_fusion.1
  368.8 5.1 %fusion.3 = f32[2048,384]{0,1:T(8,128)S(1)} fusion(bf16[1536,384]{0,1:T(8,128)(2,1)} %copy-done.3, bf16[1536,2176]{1,0:T(8,128)(2,1)} %bitcast.10), kind=kOutput, calls=%fused_computation.11 | convolution fusion | flops 2415919104 | bytes 10616832 | tf_op jit(solution)/shard_map/dot_general | solution.py:26
  374.0 7.2 %fusion.5 = f32[2048,384]{0,1:T(8,128)} fusion(bf16[1536,384]{0,1:T(8,128)(2,1)S(1)} %copy-done.2, bf16[1536,2176]{1,0:T(8,128)(2,1)} %bitcast.10), kind=kOutput, calls=%fused_computation.13 | convolution fusion | flops 2415919104 | bytes 10616832 | tf_op jit(solution)/shard_map/dot_general | solution.py:29
  381.2 7.3 %fusion.30 = f32[2048,384]{0,1:T(8,128)} fusion(bf16[1536,2048]{1,0:T(8,128)(2,1)} %bitcast.16, f32[1536]{0:T(1024)S(1)} %convert_reduce_fusion, f32[1536,384]{0,1:T(8,128)S(1)} %copy-done.11, f32[1536,384]{0,1:T(8,128)S(1)} %copy-done.10), kind=kOutput, calls=%fused_computation.39 | convolution fusion | flops 2420047872 | bytes 14161920 | tf_op jit(solution)/shard_map/dot_general | solution.py:23
  388.4 7.9 %pad_maximum_fusion = f32[2048,1152]{0,1:T(8,128)} fusion(f32[2048,384]{0,1:T(8,128)} %fusion.30, f32[2048,384]{0,1:T(8,128)} %fusion.5, f32[2048,384]{0,1:T(8,128)S(1)} %fusion.3), kind=kLoop, calls=%fused_computation.3 | loop fusion | flops 4718592 | bytes 18874368 | tf_op jit(solution)/shard_map/concatenate | solution.py:182
  396.4 1.9 constant_dynamic-slice_fusion
  398.2 2.5 collective-permute-start.3
  401.0 25.1 %collective-permute-done.3 = f32[512,576]{0,1:T(8,128)S(1)} collective-permute-done((f32[512,576]{0,1:T(8,128)S(1)}, f32[512,576]{0,1:T(8,128)S(1)}, u32[]{:S(2)}, u32[]{:S(2)}) %collective-permute-start.3) | collective-permute-done | bytes 1179680 | tf_op jit(solution)/shard_map/ppermute | solution.py:57
  426.1 3.4 collective-permute-done
  429.5 3.6 dynamic-slice_add_fusion.2
  433.1 1.5 collective-permute-start.1
  434.5 25.2 %collective-permute-done.4 = f32[512,576]{0,1:T(8,128)S(1)} collective-permute-done((f32[512,576]{0,1:T(8,128)}, f32[512,576]{0,1:T(8,128)S(1)}, u32[]{:S(2)}, u32[]{:S(2)}) %collective-permute-start.4) | collective-permute-done | bytes 1179680 | tf_op jit(solution)/shard_map/ppermute | solution.py:57
  459.8 1.0 collective-permute-done.1
  460.8 2.5 dynamic-slice_add_fusion.1
  463.8 1.0 collective-permute-start.2
  464.8 24.1 %collective-permute-done.5 = f32[512,576]{0,1:T(8,128)S(1)} collective-permute-done((f32[512,576]{0,1:T(8,128)S(1)}, f32[512,576]{0,1:T(8,128)S(1)}, u32[]{:S(2)}, u32[]{:S(2)}) %collective-permute-start.5) | collective-permute-done | bytes 1179680 | tf_op jit(solution)/shard_map/ppermute | solution.py:57
  488.9 1.7 collective-permute-done.2
  490.6 2.5 dynamic-slice_add_fusion
  493.3 1.1 copy.95
  494.5 1.1 copy.94
  495.6 1.1 copy.93
  496.8 1.1 convert_bitcast_fusion.3
  497.9 1.1 convert_bitcast_fusion.2
  499.0 0.7 copy.92
  499.7 0.8 pad_maximum_fusion.5
  (58 shorter events, 5.8 us)
Async XLA Ops:
  7.2 67.8 %all-gather.8.cloned.1.call-start = ((), (), s32[]{:S(2)}) async-start(), calls=%async_computation.9 | async-start | bytes 5013504 | tf_op jit(solution)/shard_map/all_gather | solution.py:84
  13.8 116.5 %all-gather.10.cloned.1.call-start = ((), (), s32[]{:S(2)}) async-start(), calls=%async_computation.10 | async-start | bytes 4718592 | tf_op jit(solution)/shard_map/all_gather | solution.py:85
  14.5 67.6 %copy-start.8 = (s32[8]{0:T(128)}, s32[8]{0:T(128)S(1)}, u32[]{:S(2)}) copy-start(s32[8]{0:T(128)S(1)} %fusion.56) | copy-start | bytes 100
  76.4 0.6 copy-start.4
  77.3 229.0 %copy-start.1 = (s32[8,8,128]{2,0,1:T(8,128)}, s32[8,8,128]{2,0,1:T(8,128)S(1)}, u32[]{:S(2)}) copy-start(s32[8,8,128]{2,0,1:T(8,128)S(1)} %fusion.32) | copy-start | bytes 98308
  86.1 5.5 %copy-start.5 = (bf16[1,512,384]{2,1,0:T(8,128)(2,1)S(1)}, bf16[1,512,384]{2,1,0:T(8,128)(2,1)}, u32[]{:S(2)}) copy-start(bf16[1,512,384]{2,1,0:T(8,128)(2,1)} %param.23) | copy-start | bytes 1179652
  86.1 5.5 %copy-start.6 = (bf16[1,512,384]{2,1,0:T(8,128)(2,1)S(1)}, bf16[1,512,384]{2,1,0:T(8,128)(2,1)}, u32[]{:S(2)}) copy-start(bf16[1,512,384]{2,1,0:T(8,128)(2,1)} %param.22) | copy-start | bytes 1179652
  86.1 5.5 %copy-start.7 = (bf16[1,512,384]{2,1,0:T(8,128)(2,1)S(1)}, bf16[1,512,384]{2,1,0:T(8,128)(2,1)}, u32[]{:S(2)}) copy-start(bf16[1,512,384]{2,1,0:T(8,128)(2,1)} %param.21) | copy-start | bytes 1179652
  86.1 81.3 %all-to-all-start = ((bf16[8,192,2176]{2,1,0:T(8,128)(2,1)}), bf16[8,192,2176]{2,1,0:T(8,128)(2,1)}, u32[]{:S(2)}, u32[]{:S(2)}) async-start(bf16[8,192,2176]{2,1,0:T(8,128)(2,1)} %bitcast.58), calls=%async_computation | async-start | bytes 13369344 | tf_op jit(solution)/shard_map/all_to_all | solution.py:132
  91.7 94.2 %all-gather.6.cloned.1.call-start = ((), (), s32[]{:S(2)}) async-start(), calls=%async_computation.6 | async-start | bytes 5898240 | tf_op jit(solution)/shard_map/all_gather | solution.py:126
  167.4 76.0 %all-to-all-start.1 = ((bf16[8,192,2048]{2,1,0:T(8,128)(2,1)}), bf16[8,192,2048]{2,1,0:T(8,128)(2,1)}, u32[]{:S(2)}, u32[]{:S(2)}) async-start(bf16[8,192,2048]{2,1,0:T(8,128)(2,1)} %bitcast.59), calls=%async_computation.1 | async-start | bytes 12582912 | tf_op jit(solution)/shard_map/all_to_all | solution.py:133
  172.1 324.6 %reduce-scatter.5.cloned.1.call-start = ((), (), s32[]{:S(2)}) async-start(), calls=%async_computation.8 | async-start | bytes 4718592 | tf_op jit(solution)/shard_map/reduce_scatter | solution.py:177
  191.3 52.2 %copy-start.9 = (f32[1536,384]{0,1:T(8,128)}, f32[1536,384]{0,1:T(8,128)S(1)}, u32[]{:S(2)}) copy-start(f32[1536,384]{0,1:T(8,128)S(1)} %fusion.7) | copy-start | bytes 7077892
  252.2 5.4 %copy-start.3 = (bf16[1536,384]{0,1:T(8,128)(2,1)}, bf16[1536,384]{0,1:T(8,128)(2,1)S(1)}, u32[]{:S(2)}) copy-start(bf16[1536,384]{0,1:T(8,128)(2,1)S(1)} %get-tuple-element.104) | copy-start | bytes 3538948
  309.0 1.9 copy-start
  309.0 188.8 %reduce-scatter.3.cloned.1.call-start = ((), (), s32[]{:S(2)}) async-start(), calls=%async_computation.7 | async-start | bytes 5308416 | tf_op jit(solution)/shard_map/reduce_scatter | solution.py:171
  368.8 5.2 %copy-start.2 = (bf16[1536,384]{0,1:T(8,128)(2,1)S(1)}, bf16[1536,384]{0,1:T(8,128)(2,1)}, u32[]{:S(2)}) copy-start(bf16[1536,384]{0,1:T(8,128)(2,1)} %get-tuple-element.107) | copy-start | bytes 3538948
  373.9 7.2 %copy-start.10 = (f32[1536,384]{0,1:T(8,128)S(1)}, f32[1536,384]{0,1:T(8,128)}, u32[]{:S(2)}) copy-start(f32[1536,384]{0,1:T(8,128)} %copy-done.9) | copy-start | bytes 7077892
  374.0 7.2 %copy-start.11 = (f32[1536,384]{0,1:T(8,128)S(1)}, f32[1536,384]{0,1:T(8,128)}, u32[]{:S(2)}) copy-start(f32[1536,384]{0,1:T(8,128)} %fusion.9) | copy-start | bytes 7077892
  398.2 27.9 %collective-permute-start.3 = (f32[512,576]{0,1:T(8,128)S(1)}, f32[512,576]{0,1:T(8,128)S(1)}, u32[]{:S(2)}, u32[]{:S(2)}) collective-permute-start(f32[512,576]{0,1:T(8,128)S(1)} %get-tuple-element.101), channel_id=1, source_target_pairs={{0,192},{64,0},{128,64},{192,128},{1,193},{65,1},{129,65},{193,129... | collective-permute-start | bytes 3538952 | tf_op jit(solution)/shard_map/ppermute | solution.py:57
  400.7 28.8 %collective-permute-start = (f32[512,576]{0,1:T(8,128)S(1)}, f32[512,576]{0,1:T(8,128)}, u32[]{:S(2)}, u32[]{:S(2)}) collective-permute-start(f32[512,576]{0,1:T(8,128)S(1)} %get-tuple-element.102), channel_id=1, source_target_pairs={{0,64},{64,128},{128,192},{192,0},{1,65},{65,129},{129,193},{193,1... | collective-permute-start | bytes 3538952 | tf_op jit(solution)/shard_map/ppermute | solution.py:56
  433.1 26.7 %collective-permute-start.4 = (f32[512,576]{0,1:T(8,128)}, f32[512,576]{0,1:T(8,128)S(1)}, u32[]{:S(2)}, u32[]{:S(2)}) collective-permute-start(f32[512,576]{0,1:T(8,128)} %get-tuple-element.99), channel_id=1, source_target_pairs={{0,192},{64,0},{128,64},{192,128},{1,193},{65,1},{129,65},{193,129... | collective-permute-start | bytes 3538952 | tf_op jit(solution)/shard_map/ppermute | solution.py:57
  433.1 27.7 %collective-permute-start.1 = (f32[512,576]{0,1:T(8,128)S(1)}, f32[512,576]{0,1:T(8,128)}, u32[]{:S(2)}, u32[]{:S(2)}) collective-permute-start(f32[512,576]{0,1:T(8,128)S(1)} %get-tuple-element.100), channel_id=1, source_target_pairs={{0,64},{64,128},{128,192},{192,0},{1,65},{65,129},{129,193},{193,1... | collective-permute-start | bytes 3538952 | tf_op jit(solution)/shard_map/ppermute | solution.py:56
  463.3 25.6 %collective-permute-start.5 = (f32[512,576]{0,1:T(8,128)S(1)}, f32[512,576]{0,1:T(8,128)S(1)}, u32[]{:S(2)}, u32[]{:S(2)}) collective-permute-start(f32[512,576]{0,1:T(8,128)S(1)} %get-tuple-element.97), channel_id=1, source_target_pairs={{0,192},{64,0},{128,64},{192,128},{1,193},{65,1},{129,65},{193,129... | collective-permute-start | bytes 3538952 | tf_op jit(solution)/shard_map/ppermute | solution.py:57
  463.8 26.8 %collective-permute-start.2 = (f32[512,576]{0,1:T(8,128)S(1)}, f32[512,576]{0,1:T(8,128)}, u32[]{:S(2)}, u32[]{:S(2)}) collective-permute-start(f32[512,576]{0,1:T(8,128)S(1)} %get-tuple-element.98), channel_id=1, source_target_pairs={{0,64},{64,128},{128,192},{192,0},{1,65},{65,129},{129,193},{193,1... | collective-permute-start | bytes 3538952 | tf_op jit(solution)/shard_map/ppermute | solution.py:56
Sparse Core Ops, SparseCore 0:
  13.9 61.0 all-gather.7
  76.8 53.4 all-gather.9
  132.1 53.7 all-gather.5
  309.2 52.4 reduce-scatter.4
  368.8 56.9 reduce-scatter.2

commit v8 on v6

--- a/solution.py
+++ b/solution.py
@@ -51,19 +51,16 @@
     )
     near = cores * rows_of
     slots = near * planes * capacity
-    pad = 128
     half = width // 2
-    meta = (
-        jnp.zeros((tokens_dev, pad), jnp.bfloat16)
-        .at[:, :top_count]
-        .set(gates)
-        .at[:, top_count : 2 * top_count]
-        .set(routes.astype(jnp.bfloat16))
-    )
-    seen_x = lax.all_gather(jnp.concatenate([tokens, meta], axis=1), "lz", axis=0, tiled=False)
+    meta = jnp.concatenate([gates, routes.astype(jnp.bfloat16)], axis=1).reshape(1, -1)
+    meta = jnp.pad(meta, ((0, 0), (0, width - meta.shape[1])))
+    seen_x = lax.all_gather(jnp.concatenate([tokens, meta], axis=0), "lz", axis=0, tiled=False)
     seen_dy = lax.all_gather(cotangent, "lz", axis=0, tiled=False)
-    seen_gates = seen_x[:, :, width : width + top_count]
-    seen_routes = seen_x[:, :, width + top_count : width + 2 * top_count].astype(jnp.int32)
+    seen_meta = seen_x[:, tokens_dev, : 2 * tokens_dev * top_count].reshape(
+        planes, tokens_dev, 2 * top_count
+    )
+    seen_gates = seen_meta[..., :top_count]
+    seen_routes = seen_meta[..., top_count:].astype(jnp.int32)
     plane = lax.axis_index("lz")
     near_ids = jnp.arange(near, dtype=jnp.int32)
     near_experts = (near_ids // rows_of) * (planes * rows_of) + plane * rows_of + near_ids % rows_of
@@ -88,14 +85,18 @@
         ),
         axis=3,
     )
-    gate_block = (
-        jnp.zeros((near, planes, capacity, pad), jnp.bfloat16).at[..., 0].set(send_gate)
+    gate_row = jnp.pad(
+        send_gate.reshape(near, 1, planes * capacity),
+        ((0, 0), (0, 0), (0, width - planes * capacity)),
     )
     send_x = jnp.einsum(
-        "jzrt,ztd->jzrd", choose_b, seen_x[:, :, :width], preferred_element_type=jnp.float32
-    ).astype(jnp.bfloat16)
-    send_x = jnp.concatenate([send_x, gate_block], axis=3).reshape(
-        near, planes * capacity, width + pad
+        "jzrt,ztd->jzrd",
+        choose_b,
+        seen_x[:, :tokens_dev, :],
+        preferred_element_type=jnp.float32,
+    ).astype(jnp.bfloat16)
+    send_x = jnp.concatenate(
+        [send_x.reshape(near, planes * capacity, width), gate_row], axis=1
     )
     send_dy = (
         jnp.einsum("jzrt,ztd->jzrd", choose_b, seen_dy, preferred_element_type=jnp.float32)
@@ -110,31 +111,35 @@
     down_proj = all_weights[:, 2 * hidden_units :]
     recv_x = lax.all_to_all(send_x, ("node", "ly"), split_axis=0, concat_axis=0, tiled=True)
     recv_dy = lax.all_to_all(send_dy, ("node", "ly"), split_axis=0, concat_axis=0, tiled=True)
-    flat_x = recv_x.reshape(slots, width + pad)
     results = expert_rows(
-        flat_x[:, :width],
+        recv_x[:, : planes * capacity, :].reshape(slots, width),
         recv_dy.reshape(slots, width),
-        flat_x[:, width],
+        recv_x[:, planes * capacity, : planes * capacity].reshape(slots),
         gate_proj,
         up_proj,
         down_proj,
     )
-    grad_block = jnp.zeros((slots, pad), jnp.bfloat16).at[:, 0].set(results[1])
-    back_lo = jnp.concatenate([results[0][:, :half], grad_block], axis=1).reshape(
-        near, planes * capacity, half + pad
+    grad_row = jnp.pad(
+        results[1].reshape(near, 1, planes * capacity),
+        ((0, 0), (0, 0), (0, half - planes * capacity)),
+    )
+    back_lo = jnp.concatenate(
+        [results[0][:, :half].reshape(near, planes * capacity, half), grad_row], axis=1
     )
     back_hi = results[0][:, half:].reshape(near, planes * capacity, width - half)
-    home_lo = lax.all_to_all(
-        back_lo, ("node", "ly"), split_axis=0, concat_axis=0, tiled=True
-    ).reshape(near, planes, capacity, half + pad)
+    home_lo = lax.all_to_all(back_lo, ("node", "ly"), split_axis=0, concat_axis=0, tiled=True)
+    home_gate = home_lo[:, planes * capacity, : planes * capacity].reshape(
+        near, planes, capacity
+    )
+    home_lo = home_lo[:, : planes * capacity, :].reshape(near, planes, capacity, half)
     home_hi = lax.all_to_all(
         back_hi, ("node", "ly"), split_axis=0, concat_axis=0, tiled=True
     ).reshape(near, planes, capacity, width - half)
     partial_lo = jnp.einsum(
-        "jzrt,jzrd->ztd", choose_b, home_lo[..., :half], preferred_element_type=jnp.float32
+        "jzrt,jzrd->ztd", choose_b, home_lo, preferred_element_type=jnp.float32
     )
     gate_jzt = jnp.sum(
-        jnp.where(choose, home_lo[..., half][..., None], jnp.zeros((), jnp.bfloat16)), axis=2
+        jnp.where(choose, home_gate[..., None], jnp.zeros((), jnp.bfloat16)), axis=2
     )
     pick_gate = jnp.sum(
         jnp.where(
@@ -142,10 +147,9 @@
         ),
         axis=3,
     )
-    gate_cols = (
-        jnp.zeros((planes, tokens_dev, pad), jnp.float32)
-        .at[..., :top_count]
-        .set(pick_gate.astype(jnp.float32))
+    gate_cols = jnp.pad(
+        pick_gate.astype(jnp.float32).reshape(planes, 1, tokens_dev * top_count),
+        ((0, 0), (0, 0), (0, half - tokens_dev * top_count)),
     )
     summed = lax.psum_scatter(
         jnp.concatenate([results[2], results[3], results[4]], axis=1),
@@ -155,16 +159,20 @@
     )
     summed, partial_lo, gate_cols = lax.optimization_barrier((summed, partial_lo, gate_cols))
     reduced_lo = lax.psum_scatter(
-        jnp.concatenate([partial_lo, gate_cols], axis=2), "lz", scatter_dimension=0, tiled=True
+        jnp.concatenate([partial_lo, gate_cols], axis=1), "lz", scatter_dimension=0, tiled=True
     )[0]
     partial_hi = jnp.einsum(
         "jzrt,jzrd->ztd", choose_b, home_hi, preferred_element_type=jnp.float32
     )
     reduced_hi = lax.psum_scatter(partial_hi, "lz", scatter_dimension=0, tiled=True)[0]
     input_grad = jnp.concatenate(
-        [reduced_lo[:, :half], reduced_hi], axis=1
-    ).astype(jnp.bfloat16)
-    gate_grad = reduced_lo[:, half : half + top_count].astype(jnp.bfloat16)
+        [reduced_lo[:tokens_dev], reduced_hi], axis=1
+    ).astype(jnp.bfloat16)
+    gate_grad = (
+        reduced_lo[tokens_dev, : tokens_dev * top_count]
+        .reshape(tokens_dev, top_count)
+        .astype(jnp.bfloat16)
+    )
     return (
         input_grad,
         gate_grad,

time: 499 us -> 495 us (level); the launches traced: 497 us -> 488 us
    reduce_scatter x1, waiting for transfers between devices: 24.4 us -> 33.2 us  [local(): lax.psum_scatter(partial_hi, 'lz', scatter_dimension=0, tiled=True)[0]]
    slice x7 -> x9, local copies, waits for them, and re-layouts: 5.5 us -> 10.7 us  [the longest x1 6.54 us: local(): recv_x[:, :planes * capacity, :].reshape(slots, width)]
where the time goes in v8:
time: 495 us; the launch traced here: 488 us
  waiting for transfers between devices  263 us (53%)
  blocking collectives  83 us (17%)
  matrix products  62.4 us (13%)
  local copies, waits for them, and re-layouts  27.2 us (5%)
  other arithmetic  26.7 us (5%)
  between operations  14.6 us (3%)
  starting transfers between devices  10.9 us (2%)
    all_gather x1, waiting for transfers between devices, local(): lax.all_gather(jnp.concatenate([tokens, meta], axis=0), 'lz', axis=0, til...  60.5 us
    reduce_scatter x1, waiting for transfers between devices, local(): lax.psum_scatter(jnp.concatenate([partial_lo, gate_cols], axis=1), 'lz',...  52.5 us
    all_to_all x1, waiting for transfers between devices, local(): lax.all_to_all(send_dy, ('node', 'ly'), split_axis=0, concat_axis=0, tile...  42.9 us
    all_to_all x1, blocking collectives, local(): lax.all_to_all(back_lo, ('node', 'ly'), split_axis=0, concat_axis=0, tile...  41.7 us
    all_to_all x1, blocking collectives, local(): lax.all_to_all(back_hi, ('node', 'ly'), split_axis=0, concat_axis=0, tile...  41.3 us
    all_gather x1, waiting for transfers between devices, local(): seen_dy = lax.all_gather(cotangent, 'lz', axis=0, tiled=False)  37.6 us
    reduce_scatter x1, waiting for transfers between devices, local(): lax.psum_scatter(partial_hi, 'lz', scatter_dimension=0, tiled=True)[0]  33.2 us
    all_to_all x1, waiting for transfers between devices, local(): lax.all_to_all(send_x, ('node', 'ly'), split_axis=0, concat_axis=0, tiled...  28.4 us
  transfers between devices with their start and end apart: 8, of which 7 were waited for; matrix products, arithmetic and copies ran while one was open for 15% of the time, Pallas kernels for 0%

profile of v8, /device:TPU:1, one launch (start us, length us, event | category | flops | bytes accessed | tf_op | source)
XLA Modules:
  0.0 488.1 jit_solution(7383937086377410185)
XLA Ops:
  7.2 0.7 convert_element_type.92
  7.9 0.7 pad_maximum_fusion.4
  8.6 0.1 copy.63
  8.7 0.1 reshape.107
  8.8 1.9 maximum_bitcast_fusion
  10.8 0.7 all-gather.9.cloned.1.call-update
  11.5 60.5 %all-gather.11.cloned.1.call-done = bf16[8,129,2048]{2,1,0:T(8,128)(2,1)} async-done(((bf16[1,129,2048]{2,1,0:T(8,128)(2,1)}), bf16[8,129,2048]{2,1,0:T(8,128)(2,1)}) %all-gather.11.cloned.1.call-update) | async-done | bytes 4227088 | tf_op jit(solution)/shard_map/all_gather | solution.py:57
  72.0 1.1 slice_reduce_fusion
  73.1 0.2 reshape_squeeze.2
  73.3 0.1 fusion.55
  73.5 0.1 copy.66
  73.6 0.1 copy.84
  73.7 0.1 compare_reduce_fusion
  73.8 0.1 fusion.45
  73.9 0.1 fusion.26
  74.1 0.3 fusion.35
  74.5 4.0 convert_bitcast_fusion.1
  78.5 1.1 copy.65
  79.6 3.3 fusion.1
  83.0 5.5 %all-to-all-start = ((bf16[8,193,2048]{2,1,0:T(8,128)(2,1)}), bf16[8,193,2048]{2,1,0:T(8,128)(2,1)}, u32[]{:S(2)}, u32[]{:S(2)}) async-start(bf16[8,193,2048]{2,1,0:T(8,128)(2,1)} %fusion.1), calls=%async_computation | async-start | bytes 13107200 | tf_op jit(solution)/shard_map/all_to_all | solution.py:112
  88.5 1.1 pad_maximum_fusion.2
  89.6 37.6 %all-gather.9.cloned.1.call-done = bf16[1024,2048]{1,0:T(8,128)(2,1)} async-done(((bf16[128,2048]{1,0:T(8,128)(2,1)}), bf16[1024,2048]{1,0:T(8,128)(2,1)}) %all-gather.9.cloned.1.call-update) | async-done | bytes 4194320 | tf_op jit(solution)/shard_map/all_gather | solution.py:58
  127.2 4.0 convert_bitcast_fusion
  131.2 3.2 copy.69
  134.4 28.4 %all-to-all-done = bf16[8,193,2048]{2,1,0:T(8,128)(2,1)} async-done(((bf16[8,193,2048]{2,1,0:T(8,128)(2,1)}), bf16[8,193,2048]{2,1,0:T(8,128)(2,1)}, u32[]{:S(2)}, u32[]{:S(2)}) %all-to-all-start) | async-done | bytes 6324256 | tf_op jit(solution)/shard_map/all_to_all | solution.py:112
  162.8 4.8 all-to-all-start.1
  167.6 0.5 reduce-scatter.4.cloned.1.call-start
  168.1 0.8 fusion.49
  168.9 6.5 %slice.85 = bf16[8,192,2048]{2,1,0:T(8,128)(2,1)} slice(bf16[8,193,2048]{2,1,0:T(8,128)(2,1)} %all-to-all-done), slice={[0:8], [0:192], [0:2048]} | slice | bytes 12582912 | tf_op jit(solution)/shard_map/slice | solution.py:115
  175.5 7.4 %all-gather.7.cloned.1.call-done = bf16[1,2048,1152]{2,1,0:T(8,128)(2,1)} async-done(((bf16[1,512,1152]{2,1,0:T(8,128)(2,1)}), bf16[1,2048,1152]{2,1,0:T(8,128)(2,1)}) %all-gather.7.cloned.1.call-update) | async-done | bytes 4718608 | tf_op jit(solution)/shard_map/all_gather | solution.py:106
  182.9 7.4 %fusion.19 = f32[1536,384]{0,1:T(8,128)} fusion(bf16[1536,2048]{1,0:T(8,128)(2,1)} %bitcast.68, bf16[2048,1152]{1,0:T(8,128)(2,1)} %bitcast.74), kind=kOutput, calls=%fused_computation.28 | convolution fusion | flops 2415919104 | bytes 10223616 | tf_op jit(solution)/shard_map/dot_general | solution.py:8
  190.3 5.7 %fusion.22 = f32[1536,384]{0,1:T(8,128)} fusion(bf16[1536,2048]{1,0:T(8,128)(2,1)S(1)} %bitcast.69, bf16[2048,1152]{1,0:T(8,128)(2,1)} %bitcast.75), kind=kOutput, calls=%fused_computation.31 | convolution fusion | flops 2415919104 | bytes 10223616 | tf_op jit(solution)/shard_map/dot_general | solution.py:9
  196.0 42.9 %all-to-all-done.1 = bf16[8,192,2048]{2,1,0:T(8,128)(2,1)} async-done(((bf16[8,192,2048]{2,1,0:T(8,128)(2,1)}), bf16[8,192,2048]{2,1,0:T(8,128)(2,1)}, u32[]{:S(2)}, u32[]{:S(2)}) %all-to-all-start.1) | async-done | bytes 6291488 | tf_op jit(solution)/shard_map/all_to_all | solution.py:113
  238.9 8.5 %multiply_reduce_fusion = (bf16[1536]{0:T(1024)(128)(2,1)S(1)}, bf16[1536,384]{0,1:T(8,128)(2,1)S(1)}, bf16[1536,384]{0,1:T(8,128)(2,1)S(1)}) fusion(f32[1536,384]{0,1:T(8,128)} %fusion.22, f32[1536,384]{0,1:T(8,128)} %fusion.19, f32[1536]{0:T(1024)S(1)} %reshape.117, bf16[1536,2048]{1,0:T(8,128)(2,1)} %bitcast.15, bf16[2048,1152]{1,0:T(8,128)(2,1)} %bitcast.76), kind=kOutput, calls=%fused_computation.16 | convolution fusion | flops 2425944576 | bytes 14951424 | tf_op jit(solution)/shard_map/dot_general | solution.py:13
  247.4 8.1 %fusion.24 = f32[2048,384]{0,1:T(8,128)} fusion(bf16[1536,2048]{1,0:T(8,128)(2,1)} %bitcast.15, f32[1536]{0:T(1024)S(1)} %reshape.117, f32[1536,384]{0,1:T(8,128)S(1)} %copy-done.9, f32[1536,384]{0,1:T(8,128)S(1)} %copy-done.8), kind=kOutput, calls=%fused_computation.33 | convolution fusion | flops 2420047872 | bytes 14161920 | tf_op jit(solution)/shard_map/dot_general | solution.py:23
  255.6 4.5 fusion.56
  260.1 4.3 fusion.57
  264.4 8.7 %pad_maximum_fusion = f32[2048,1152]{0,1:T(8,128)} fusion(f32[2048,384]{0,1:T(8,128)} %fusion.24, f32[2048,384]{0,1:T(8,128)} %fusion.57, f32[2048,384]{0,1:T(8,128)} %fusion.56), kind=kLoop, calls=%fused_computation.3 | loop fusion | flops 4718592 | bytes 18874368 | tf_op jit(solution)/shard_map/concatenate | solution.py:155
  273.2 1.2 copy-done.4
  274.4 4.9 %fusion.17 = f32[1536,2048]{1,0:T(8,128)S(1)} fusion(bf16[1536,384]{0,1:T(8,128)(2,1)S(1)} %copy-done.4, bf16[2048,1152]{1,0:T(8,128)(2,1)} %bitcast.77), kind=kOutput, calls=%fused_computation.26 | convolution fusion | flops 2415919104 | bytes 15335424 | tf_op jit(solution)/shard_map/dot_general | solution.py:31
  279.3 5.4 %add_convert_fusion = bf16[1536,2048]{1,0:T(8,128)(2,1)S(1)} fusion(f32[1536,2048]{1,0:T(8,128)S(1)} %fusion.17, bf16[1536,384]{0,1:T(8,128)(2,1)} %copy-done.2, bf16[2048,1152]{1,0:T(8,128)(2,1)} %bitcast.78), kind=kOutput, calls=%fused_computation.2 | convolution fusion | flops 2422210560 | bytes 21626880 | tf_op jit(solution)/shard_map/dot_general | solution.py:34
  284.7 2.3 fusion.54
  287.0 41.3 %all_to_all.20 = bf16[8,192,1024]{2,1,0:T(8,128)(2,1)S(1)} all-to-all(bf16[8,192,1024]{2,1,0:T(8,128)(2,1)S(1)} %bitcast.66), channel_id=1, replica_groups=mesh['dp'=4,'node'=2,'lz'=8,'ly'=4] {'node','ly'}, dimensions={0} | all-to-all | bytes 6291456 | tf_op jit(solution)/shard_map/all_to_all | solution.py:135
  328.3 2.8 fusion.12
  331.3 1.7 copy-done
  333.0 0.4 fusion.3
  333.4 41.7 %all_to_all.21 = bf16[8,193,1024]{2,1,0:T(8,128)(2,1)S(1)} all-to-all(bf16[8,193,1024]{2,1,0:T(8,128)(2,1)S(1)} %fusion.3), channel_id=1, replica_groups=mesh['dp'=4,'node'=2,'lz'=8,'ly'=4] {'node','ly'}, dimensions={0} | all-to-all | bytes 6324224 | tf_op jit(solution)/shard_map/all_to_all | solution.py:130
  375.3 0.4 fusion.36
  375.7 0.2 fusion.46
  375.8 0.9 copy.73
  376.8 1.3 reshape.118
  378.1 0.4 slice.89
  378.5 2.7 fusion.9
  381.2 4.9 %pad_maximum_fusion.1 = f32[8,129,1024]{2,1,0:T(8,128)} fusion(f32[8,1,1024]{2,1,0:T(1,128)S(1)} %copy.74, f32[8,128,1024]{2,1,0:T(8,128)} %fusion.9), kind=kLoop, calls=%fused_computation.9 | loop fusion | flops 1056768 | bytes 8454144 | tf_op jit(solution)/shard_map/concatenate | solution.py:162
  386.2 33.2 %reduce-scatter.8.cloned.1.call-done = f32[1,128,1024]{2,1,0:T(8,128)} async-done(((f32[8,128,1024]{2,1,0:T(8,128)}), f32[1,128,1024]{2,1,0:T(8,128)}) %reduce-scatter.8.cloned.1.call-update) | async-done | bytes 524304 | tf_op jit(solution)/shard_map/reduce_scatter | solution.py:167
  419.4 1.1 convert_bitcast_fusion.2
  420.5 1.8 slice_bitcast_fusion.2
  422.3 1.1 copy.79
  423.5 1.1 copy.78
  424.6 1.1 copy.77
  425.8 52.5 %reduce-scatter.6.cloned.1.call-done = f32[1,129,1024]{2,1,0:T(8,128)} async-done(((f32[8,129,1024]{2,1,0:T(8,128)}), f32[1,129,1024]{2,1,0:T(8,128)}) %reduce-scatter.6.cloned.1.call-update) | async-done | bytes 528400 | tf_op jit(solution)/shard_map/reduce_scatter | solution.py:161
  478.3 1.1 convert.16
  479.5 0.7 copy.76
  480.2 0.8 pad_maximum_fusion.3
  (47 shorter events, 0.9 us)
Async XLA Ops:
  7.2 64.8 %all-gather.11.cloned.1.call-start = ((), (), s32[]{:S(2)}) async-start(), calls=%async_computation.12 | async-start | bytes 5013504 | tf_op jit(solution)/shard_map/all_gather | solution.py:57
  10.7 116.5 %all-gather.9.cloned.1.call-start = ((), (), s32[]{:S(2)}) async-start(), calls=%async_computation.11 | async-start | bytes 4718592 | tf_op jit(solution)/shard_map/all_gather | solution.py:58
  83.0 5.5 %copy-start.5 = (bf16[1,512,384]{2,1,0:T(8,128)(2,1)S(1)}, bf16[1,512,384]{2,1,0:T(8,128)(2,1)}, u32[]{:S(2)}) copy-start(bf16[1,512,384]{2,1,0:T(8,128)(2,1)} %param.13) | copy-start | bytes 1179652
  83.0 5.5 %copy-start.6 = (bf16[1,512,384]{2,1,0:T(8,128)(2,1)S(1)}, bf16[1,512,384]{2,1,0:T(8,128)(2,1)}, u32[]{:S(2)}) copy-start(bf16[1,512,384]{2,1,0:T(8,128)(2,1)} %param.12) | copy-start | bytes 1179652
  83.0 5.5 %copy-start.7 = (bf16[1,512,384]{2,1,0:T(8,128)(2,1)S(1)}, bf16[1,512,384]{2,1,0:T(8,128)(2,1)}, u32[]{:S(2)}) copy-start(bf16[1,512,384]{2,1,0:T(8,128)(2,1)} %param.11) | copy-start | bytes 1179652
  83.0 79.9 %all-to-all-start = ((bf16[8,193,2048]{2,1,0:T(8,128)(2,1)}), bf16[8,193,2048]{2,1,0:T(8,128)(2,1)}, u32[]{:S(2)}, u32[]{:S(2)}) async-start(bf16[8,193,2048]{2,1,0:T(8,128)(2,1)} %fusion.1), calls=%async_computation | async-start | bytes 13107200 | tf_op jit(solution)/shard_map/all_to_all | solution.py:112
  88.4 94.4 %all-gather.7.cloned.1.call-start = ((), (), s32[]{:S(2)}) async-start(), calls=%async_computation.7 | async-start | bytes 5898240 | tf_op jit(solution)/shard_map/all_gather | solution.py:106
  162.8 76.0 %all-to-all-start.1 = ((bf16[8,192,2048]{2,1,0:T(8,128)(2,1)}), bf16[8,192,2048]{2,1,0:T(8,128)(2,1)}, u32[]{:S(2)}, u32[]{:S(2)}) async-start(bf16[8,192,2048]{2,1,0:T(8,128)(2,1)} %bitcast.61), calls=%async_computation.1 | async-start | bytes 12582912 | tf_op jit(solution)/shard_map/all_to_all | solution.py:113
  167.6 213.6 %reduce-scatter.4.cloned.1.call-start = ((), (), s32[]{:S(2)}) async-start(), calls=%async_computation.8 | async-start | bytes 11796480 | tf_op jit(solution)/shard_map/reduce_scatter | solution.py:154
  182.9 7.4 %copy-start.1 = (bf16[8,192,2048]{2,1,0:T(8,128)(2,1)S(1)}, bf16[8,192,2048]{2,1,0:T(8,128)(2,1)}, u32[]{:S(2)}) copy-start(bf16[8,192,2048]{2,1,0:T(8,128)(2,1)} %slice.85) | copy-start | bytes 18874372
  190.3 65.3 %slice-start = ((s8[6291456]{0:T(1024)(128)(4,1)}), s8[2097152]{0:T(1024)(128)(4,1)S(1)}, s32[]{:S(2)}) async-start(s8[6291456]{0:T(1024)(128)(4,1)} %bitcast.70), calls=%async_computation.13 | async-start | bytes 4194304
  238.9 8.5 %copy-start.8 = (f32[1536,384]{0,1:T(8,128)S(1)}, f32[1536,384]{0,1:T(8,128)}, u32[]{:S(2)}) copy-start(f32[1536,384]{0,1:T(8,128)} %fusion.19) | copy-start | bytes 7077892
  238.9 8.6 %copy-start.9 = (f32[1536,384]{0,1:T(8,128)S(1)}, f32[1536,384]{0,1:T(8,128)}, u32[]{:S(2)}) copy-start(f32[1536,384]{0,1:T(8,128)} %fusion.22) | copy-start | bytes 7077892
  238.9 16.7 %slice-start.1 = ((s8[6291456]{0:T(1024)(128)(4,1)}), s8[4194304]{0:T(1024)(128)(4,1)S(1)}, s32[]{:S(2)}) async-start(s8[6291456]{0:T(1024)(128)(4,1)} %bitcast.70), calls=%async_computation.14 | async-start | bytes 8388608
  247.4 8.1 %copy-start.3 = (bf16[1536,384]{0,1:T(8,128)(2,1)}, bf16[1536,384]{0,1:T(8,128)(2,1)S(1)}, u32[]{:S(2)}) copy-start(bf16[1536,384]{0,1:T(8,128)(2,1)S(1)} %get-tuple-element.37) | copy-start | bytes 3538948
  247.4 12.7 %copy-start.2 = (bf16[1536,384]{0,1:T(8,128)(2,1)}, bf16[1536,384]{0,1:T(8,128)(2,1)S(1)}, u32[]{:S(2)}) copy-start(bf16[1536,384]{0,1:T(8,128)(2,1)S(1)} %get-tuple-element.40) | copy-start | bytes 3538948
  273.1 1.3 copy-start.4
  273.1 146.3 %reduce-scatter.8.cloned.1.call-start = ((), (), s32[]{:S(2)}) async-start(), calls=%async_computation.10 | async-start | bytes 4718592 | tf_op jit(solution)/shard_map/reduce_scatter | solution.py:167
  331.2 1.9 copy-start
  331.2 147.1 %reduce-scatter.6.cloned.1.call-start = ((), (), s32[]{:S(2)}) async-start(), calls=%async_computation.9 | async-start | bytes 5013504 | tf_op jit(solution)/shard_map/reduce_scatter | solution.py:161
Sparse Core Ops, SparseCore 0:
  10.9 61.0 all-gather.10
  73.8 53.4 all-gather.8
  129.1 53.7 all-gather.6
  273.3 88.6 reduce-scatter.3
  364.3 55.0 reduce-scatter.7
  421.9 56.4 reduce-scatter.5

commit v9 on v8

--- a/solution.py
+++ b/solution.py
@@ -151,13 +151,13 @@
         pick_gate.astype(jnp.float32).reshape(planes, 1, tokens_dev * top_count),
         ((0, 0), (0, 0), (0, half - tokens_dev * top_count)),
     )
+    summed_down = lax.psum_scatter(results[4], "dp", scatter_dimension=0, tiled=True)
     summed = lax.psum_scatter(
-        jnp.concatenate([results[2], results[3], results[4]], axis=1),
-        "dp",
-        scatter_dimension=0,
-        tiled=True,
-    )
-    summed, partial_lo, gate_cols = lax.optimization_barrier((summed, partial_lo, gate_cols))
+        jnp.concatenate([results[2], results[3]], axis=1), "dp", scatter_dimension=0, tiled=True
+    )
+    summed_down, summed, partial_lo, gate_cols = lax.optimization_barrier(
+        (summed_down, summed, partial_lo, gate_cols)
+    )
     reduced_lo = lax.psum_scatter(
         jnp.concatenate([partial_lo, gate_cols], axis=1), "lz", scatter_dimension=0, tiled=True
     )[0]
@@ -178,7 +178,7 @@
         gate_grad,
         summed[None, :, :hidden_units],
         summed[None, :, hidden_units : 2 * hidden_units],
-        summed[None, :, 2 * hidden_units :],
+        summed_down[None],
     )
 
 

time: 495 us -> 482 us (0.974); the launches traced: 488 us -> 481 us
  other arithmetic: 26.7 us -> 21 us
    concatenate x1, other arithmetic: 8.75 us -> 3.08 us  [local(): jnp.concatenate([results[2], results[3]], axis=1)]
  transfers between devices with their start and end apart: 8 -> 9, of which waited for: 7 -> 7; matrix products, arithmetic and copies ran while one was open for 15% -> 19% of each run, Pallas kernels for 0% -> 0%
where the time goes in v9:
time: 482 us; the launch traced here: 481 us
  waiting for transfers between devices  263 us (55%)
  blocking collectives  83.1 us (17%)
  matrix products  64.7 us (13%)
  local copies, waits for them, and re-layouts  23.3 us (5%)
  other arithmetic  21 us (4%)
  between operations  14.4 us (3%)
  starting transfers between devices  11.1 us (2%)
    all_gather x1, waiting for transfers between devices, local(): lax.all_gather(jnp.concatenate([tokens, meta], axis=0), 'lz', axis=0, til...  60.5 us
    reduce_scatter x1, waiting for transfers between devices, local(): lax.psum_scatter(jnp.concatenate([partial_lo, gate_cols], axis=1), 'lz',...  55.5 us
    all_to_all x1, waiting for transfers between devices, local(): lax.all_to_all(send_dy, ('node', 'ly'), split_axis=0, concat_axis=0, tile...  43.1 us
    all_to_all x1, blocking collectives, local(): lax.all_to_all(back_lo, ('node', 'ly'), split_axis=0, concat_axis=0, tile...  41.8 us
    all_to_all x1, blocking collectives, local(): lax.all_to_all(back_hi, ('node', 'ly'), split_axis=0, concat_axis=0, tile...  41.4 us
    all_gather x1, waiting for transfers between devices, local(): seen_dy = lax.all_gather(cotangent, 'lz', axis=0, tiled=False)  37.6 us
    reduce_scatter x1, waiting for transfers between devices, local(): lax.psum_scatter(partial_hi, 'lz', scatter_dimension=0, tiled=True)[0]  30 us
    all_to_all x1, waiting for transfers between devices, local(): lax.all_to_all(send_x, ('node', 'ly'), split_axis=0, concat_axis=0, tiled...  28.4 us
  transfers between devices with their start and end apart: 9, of which 7 were waited for; matrix products, arithmetic and copies ran while one was open for 19% of the time, Pallas kernels for 0%

profile of v9, /device:TPU:1, one launch (start us, length us, event | category | flops | bytes accessed | tf_op | source)
XLA Modules:
  0.0 481.1 jit_solution(1033211048384480134)
XLA Ops:
  7.2 0.7 convert_element_type.92
  7.9 0.7 pad_maximum_fusion.4
  8.6 0.1 copy.59
  8.7 0.1 reshape.107
  8.8 1.9 maximum_bitcast_fusion
  10.8 0.7 all-gather.9.cloned.1.call-update
  11.5 60.5 %all-gather.11.cloned.1.call-done = bf16[8,129,2048]{2,1,0:T(8,128)(2,1)} async-done(((bf16[1,129,2048]{2,1,0:T(8,128)(2,1)}), bf16[8,129,2048]{2,1,0:T(8,128)(2,1)}) %all-gather.11.cloned.1.call-update) | async-done | bytes 4227088 | tf_op jit(solution)/shard_map/all_gather | solution.py:57
  72.0 1.1 slice_reduce_fusion
  73.1 0.2 reshape_squeeze.2
  73.3 0.1 fusion.55
  73.5 0.1 copy.63
  73.6 0.1 copy.79
  73.7 0.1 compare_reduce_fusion
  73.8 0.1 fusion.45
  73.9 0.1 fusion.26
  74.1 0.3 fusion.35
  74.5 4.0 convert_bitcast_fusion
  78.5 1.1 copy.62
  79.6 3.3 fusion.1
  83.0 5.5 %all-to-all-start.1 = ((bf16[8,193,2048]{2,1,0:T(8,128)(2,1)}), bf16[8,193,2048]{2,1,0:T(8,128)(2,1)}, u32[]{:S(2)}, u32[]{:S(2)}) async-start(bf16[8,193,2048]{2,1,0:T(8,128)(2,1)} %fusion.1), calls=%async_computation.1 | async-start | bytes 13107200 | tf_op jit(solution)/shard_map/all_to_all | solution.py:112
  88.5 1.1 pad_maximum_fusion.2
  89.6 37.6 %all-gather.9.cloned.1.call-done = bf16[1024,2048]{1,0:T(8,128)(2,1)} async-done(((bf16[128,2048]{1,0:T(8,128)(2,1)}), bf16[1024,2048]{1,0:T(8,128)(2,1)}) %all-gather.9.cloned.1.call-update) | async-done | bytes 4194320 | tf_op jit(solution)/shard_map/all_gather | solution.py:58
  127.2 4.0 convert_bitcast_fusion.1
  131.2 3.2 copy.61
  134.4 28.4 %all-to-all-done.1 = bf16[8,193,2048]{2,1,0:T(8,128)(2,1)} async-done(((bf16[8,193,2048]{2,1,0:T(8,128)(2,1)}), bf16[8,193,2048]{2,1,0:T(8,128)(2,1)}, u32[]{:S(2)}, u32[]{:S(2)}) %all-to-all-start.1) | async-done | bytes 6324256 | tf_op jit(solution)/shard_map/all_to_all | solution.py:112
  162.8 4.8 all-to-all-start
  167.6 0.2 reduce-scatter.5.cloned.1.call-start
  167.8 0.8 fusion.49
  168.6 6.6 %slice.80 = bf16[8,192,2048]{2,1,0:T(8,128)(2,1)} slice(bf16[8,193,2048]{2,1,0:T(8,128)(2,1)} %all-to-all-done.1), slice={[0:8], [0:192], [0:2048]} | slice | bytes 12582912 | tf_op jit(solution)/shard_map/slice | solution.py:115
  175.2 7.6 %all-gather.7.cloned.1.call-done = bf16[1,2048,1152]{2,1,0:T(8,128)(2,1)} async-done(((bf16[1,512,1152]{2,1,0:T(8,128)(2,1)}), bf16[1,2048,1152]{2,1,0:T(8,128)(2,1)}) %all-gather.7.cloned.1.call-update) | async-done | bytes 4718608 | tf_op jit(solution)/shard_map/all_gather | solution.py:106
  182.9 7.4 %fusion.18 = f32[1536,384]{0,1:T(8,128)} fusion(bf16[1536,2048]{1,0:T(8,128)(2,1)} %bitcast.67, bf16[2048,1152]{1,0:T(8,128)(2,1)} %bitcast.71), kind=kOutput, calls=%fused_computation.27 | convolution fusion | flops 2415919104 | bytes 10223616 | tf_op jit(solution)/shard_map/dot_general | solution.py:9
  190.3 5.5 %fusion.22 = f32[1536,384]{0,1:T(8,128)} fusion(bf16[1536,2048]{1,0:T(8,128)(2,1)S(1)} %bitcast.70, bf16[2048,1152]{1,0:T(8,128)(2,1)} %bitcast.72), kind=kOutput, calls=%fused_computation.31 | convolution fusion | flops 2415919104 | bytes 10223616 | tf_op jit(solution)/shard_map/dot_general | solution.py:8
  195.8 43.1 %all-to-all-done = bf16[8,192,2048]{2,1,0:T(8,128)(2,1)} async-done(((bf16[8,192,2048]{2,1,0:T(8,128)(2,1)}), bf16[8,192,2048]{2,1,0:T(8,128)(2,1)}, u32[]{:S(2)}, u32[]{:S(2)}) %all-to-all-start) | async-done | bytes 6291488 | tf_op jit(solution)/shard_map/all_to_all | solution.py:113
  238.9 9.4 %fusion.24 = f32[2048,384]{1,0:T(8,128)} fusion(bf16[1536,2048]{1,0:T(8,128)(2,1)} %bitcast.9, f32[1536]{0:T(1024)S(1)} %reshape.117, f32[1536,384]{0,1:T(8,128)} %fusion.18, f32[1536,384]{0,1:T(8,128)} %fusion.22), kind=kOutput, calls=%fused_computation.33 | convolution fusion | flops 2420047872 | bytes 14161920 | tf_op jit(solution)/shard_map/dot_general | solution.py:23
  248.3 0.3 reduce-scatter.7.cloned.1.call-start
  248.6 8.4 %multiply_reduce_fusion = (bf16[1536]{0:T(1024)(128)(2,1)S(1)}, bf16[1536,384]{0,1:T(8,128)(2,1)S(1)}, bf16[1536,384]{0,1:T(8,128)(2,1)S(1)}) fusion(f32[1536,384]{0,1:T(8,128)} %fusion.18, f32[1536,384]{0,1:T(8,128)} %fusion.22, f32[1536]{0:T(1024)S(1)} %reshape.117, bf16[1536,2048]{1,0:T(8,128)(2,1)} %bitcast.9, bf16[2048,1152]{1,0:T(8,128)(2,1)} %bitcast.73), kind=kOutput, calls=%fused_computation.16 | convolution fusion | flops 2425944576 | bytes 14951424 | tf_op jit(solution)/shard_map/dot_general | solution.py:13
  257.0 5.2 %fusion.56 = f32[2048,384]{0,1:T(8,128)S(1)} fusion(bf16[1536,384]{0,1:T(8,128)(2,1)S(1)} %get-tuple-element.39, bf16[1536,2048]{1,0:T(8,128)(2,1)} %bitcast.68), kind=kOutput, calls=%fused_computation.82 | convolution fusion | flops 2415919104 | bytes 10616832 | tf_op jit(solution)/shard_map/dot_general | solution.py:26
  262.2 4.8 fusion.57
  266.9 3.1 pad_maximum_fusion
  270.0 0.3 reduce-scatter.11.cloned.1.call-start
  270.3 4.9 %fusion.20 = f32[1536,2048]{1,0:T(8,128)S(1)} fusion(bf16[1536,384]{0,1:T(8,128)(2,1)S(1)} %get-tuple-element.39, bf16[2048,1152]{1,0:T(8,128)(2,1)} %bitcast.74), kind=kOutput, calls=%fused_computation.29 | convolution fusion | flops 2415919104 | bytes 15335424 | tf_op jit(solution)/shard_map/dot_general | solution.py:31
  275.2 5.5 %add_convert_fusion = bf16[1536,2048]{1,0:T(8,128)(2,1)S(1)} fusion(f32[1536,2048]{1,0:T(8,128)S(1)} %fusion.20, bf16[1536,384]{0,1:T(8,128)(2,1)} %copy-done.3, bf16[2048,1152]{1,0:T(8,128)(2,1)} %bitcast.75), kind=kOutput, calls=%fused_computation.2 | convolution fusion | flops 2422210560 | bytes 21626880 | tf_op jit(solution)/shard_map/dot_general | solution.py:34
  280.7 2.5 fusion.54
  283.2 41.4 %all_to_all.20 = bf16[8,192,1024]{2,1,0:T(8,128)(2,1)S(1)} all-to-all(bf16[8,192,1024]{2,1,0:T(8,128)(2,1)S(1)} %bitcast.65), channel_id=1, replica_groups=mesh['dp'=4,'node'=2,'lz'=8,'ly'=4] {'node','ly'}, dimensions={0} | all-to-all | bytes 6291456 | tf_op jit(solution)/shard_map/all_to_all | solution.py:135
  324.5 2.8 fusion.12
  327.5 1.7 copy-done
  329.2 0.4 fusion.3
  329.6 41.8 %all_to_all.21 = bf16[8,193,1024]{2,1,0:T(8,128)(2,1)S(1)} all-to-all(bf16[8,193,1024]{2,1,0:T(8,128)(2,1)S(1)} %fusion.3), channel_id=1, replica_groups=mesh['dp'=4,'node'=2,'lz'=8,'ly'=4] {'node','ly'}, dimensions={0} | all-to-all | bytes 6324224 | tf_op jit(solution)/shard_map/all_to_all | solution.py:130
  371.5 0.4 fusion.36
  371.9 0.2 fusion.46
  372.0 0.9 copy.69
  373.0 1.3 reshape.118
  374.3 0.4 slice.85
  374.7 2.8 fusion.9
  377.6 4.9 %pad_maximum_fusion.1 = f32[8,129,1024]{2,1,0:T(8,128)} fusion(f32[8,1,1024]{2,1,0:T(1,128)S(1)} %copy.70, f32[8,128,1024]{2,1,0:T(8,128)} %fusion.9), kind=kLoop, calls=%fused_computation.9 | loop fusion | flops 1056768 | bytes 8454144 | tf_op jit(solution)/shard_map/concatenate | solution.py:162
  382.6 30.0 %reduce-scatter.11.cloned.1.call-done = f32[1,128,1024]{2,1,0:T(8,128)} async-done(((f32[8,128,1024]{2,1,0:T(8,128)}), f32[1,128,1024]{2,1,0:T(8,128)}) %reduce-scatter.11.cloned.1.call-update) | async-done | bytes 524304 | tf_op jit(solution)/shard_map/reduce_scatter | solution.py:167
  412.5 1.1 convert_bitcast_fusion.2
  413.6 0.1 slice_bitcast_fusion.2
  413.8 1.1 copy.74
  414.9 1.1 copy.73
  416.1 55.5 %reduce-scatter.9.cloned.1.call-done = f32[1,129,1024]{2,1,0:T(8,128)} async-done(((f32[8,129,1024]{2,1,0:T(8,128)}), f32[1,129,1024]{2,1,0:T(8,128)}) %reduce-scatter.9.cloned.1.call-update) | async-done | bytes 528400 | tf_op jit(solution)/shard_map/reduce_scatter | solution.py:161
  471.5 1.1 convert.16
  472.8 0.7 copy.72
  473.4 0.8 pad_maximum_fusion.3
  (38 shorter events, 0.8 us)
Async XLA Ops:
  7.2 64.8 %all-gather.11.cloned.1.call-start = ((), (), s32[]{:S(2)}) async-start(), calls=%async_computation.14 | async-start | bytes 5013504 | tf_op jit(solution)/shard_map/all_gather | solution.py:57
  10.7 116.5 %all-gather.9.cloned.1.call-start = ((), (), s32[]{:S(2)}) async-start(), calls=%async_computation.13 | async-start | bytes 4718592 | tf_op jit(solution)/shard_map/all_gather | solution.py:58
  83.0 5.5 %copy-start.4 = (bf16[1,512,384]{2,1,0:T(8,128)(2,1)S(1)}, bf16[1,512,384]{2,1,0:T(8,128)(2,1)}, u32[]{:S(2)}) copy-start(bf16[1,512,384]{2,1,0:T(8,128)(2,1)} %param.13) | copy-start | bytes 1179652
  83.0 5.5 %copy-start.5 = (bf16[1,512,384]{2,1,0:T(8,128)(2,1)S(1)}, bf16[1,512,384]{2,1,0:T(8,128)(2,1)}, u32[]{:S(2)}) copy-start(bf16[1,512,384]{2,1,0:T(8,128)(2,1)} %param.12) | copy-start | bytes 1179652
  83.0 5.5 %copy-start.6 = (bf16[1,512,384]{2,1,0:T(8,128)(2,1)S(1)}, bf16[1,512,384]{2,1,0:T(8,128)(2,1)}, u32[]{:S(2)}) copy-start(bf16[1,512,384]{2,1,0:T(8,128)(2,1)} %param.11) | copy-start | bytes 1179652
  83.0 79.8 %all-to-all-start.1 = ((bf16[8,193,2048]{2,1,0:T(8,128)(2,1)}), bf16[8,193,2048]{2,1,0:T(8,128)(2,1)}, u32[]{:S(2)}, u32[]{:S(2)}) async-start(bf16[8,193,2048]{2,1,0:T(8,128)(2,1)} %fusion.1), calls=%async_computation.1 | async-start | bytes 13107200 | tf_op jit(solution)/shard_map/all_to_all | solution.py:112
  88.4 94.4 %all-gather.7.cloned.1.call-start = ((), (), s32[]{:S(2)}) async-start(), calls=%async_computation.8 | async-start | bytes 5898240 | tf_op jit(solution)/shard_map/all_gather | solution.py:106
  162.8 76.1 %all-to-all-start = ((bf16[8,192,2048]{2,1,0:T(8,128)(2,1)}), bf16[8,192,2048]{2,1,0:T(8,128)(2,1)}, u32[]{:S(2)}, u32[]{:S(2)}) async-start(bf16[8,192,2048]{2,1,0:T(8,128)(2,1)} %bitcast.60), calls=%async_computation | async-start | bytes 12582912 | tf_op jit(solution)/shard_map/all_to_all | solution.py:113
  167.6 209.9 %reduce-scatter.5.cloned.1.call-start = ((), (), s32[]{:S(2)}) async-start(), calls=%async_computation.9 | async-start | bytes 3932160 | tf_op jit(solution)/shard_map/reduce_scatter | solution.py:154
  182.9 7.4 %copy-start.1 = (bf16[8,192,2048]{2,1,0:T(8,128)(2,1)S(1)}, bf16[8,192,2048]{2,1,0:T(8,128)(2,1)}, u32[]{:S(2)}) copy-start(bf16[8,192,2048]{2,1,0:T(8,128)(2,1)} %slice.80) | copy-start | bytes 18874372
  248.3 129.2 %reduce-scatter.7.cloned.1.call-start = ((), (), s32[]{:S(2)}) async-start(), calls=%async_computation.10 | async-start | bytes 7864320 | tf_op jit(solution)/shard_map/reduce_scatter | solution.py:155
  257.0 5.2 %copy-start.3 = (bf16[1536,384]{0,1:T(8,128)(2,1)}, bf16[1536,384]{0,1:T(8,128)(2,1)S(1)}, u32[]{:S(2)}) copy-start(bf16[1536,384]{0,1:T(8,128)(2,1)S(1)} %get-tuple-element.42) | copy-start | bytes 3538948
  270.0 142.5 %reduce-scatter.11.cloned.1.call-start = ((), (), s32[]{:S(2)}) async-start(), calls=%async_computation.12 | async-start | bytes 4718592 | tf_op jit(solution)/shard_map/reduce_scatter | solution.py:167
  327.3 1.9 copy-start
  327.4 144.2 %reduce-scatter.9.cloned.1.call-start = ((), (), s32[]{:S(2)}) async-start(), calls=%async_computation.11 | async-start | bytes 5013504 | tf_op jit(solution)/shard_map/reduce_scatter | solution.py:161
  382.5 31.1 %copy-start.2 = (f32[512,768]{0,1:T(8,128)S(1)}, f32[512,768]{0,1:T(8,128)}, u32[]{:S(2)}) copy-start(f32[512,768]{0,1:T(8,128)} %reduce-scatter.7.cloned.1.call-done) | copy-start | bytes 4718596
Sparse Core Ops, SparseCore 0:
  10.9 61.0 all-gather.10
  73.8 53.4 all-gather.8
  129.1 53.7 all-gather.6
  248.4 37.8 reduce-scatter.4
  288.8 66.2 reduce-scatter.6
  357.4 55.0 reduce-scatter.10
  415.1 56.3 reduce-scatter.8

commit v10 on v9

--- a/solution.py
+++ b/solution.py
@@ -95,14 +95,13 @@
         seen_x[:, :tokens_dev, :],
         preferred_element_type=jnp.float32,
     ).astype(jnp.bfloat16)
-    send_x = jnp.concatenate(
-        [send_x.reshape(near, planes * capacity, width), gate_row], axis=1
-    )
+    send_x = send_x.reshape(near, planes * capacity, width)
     send_dy = (
         jnp.einsum("jzrt,ztd->jzrd", choose_b, seen_dy, preferred_element_type=jnp.float32)
         .astype(jnp.bfloat16)
         .reshape(near, planes * capacity, width)
     )
+    send_dy = jnp.concatenate([send_dy, gate_row], axis=1)
     all_weights = lax.all_gather(
         jnp.concatenate([w_gate, w_up, w_down], axis=2), "dp", axis=1, tiled=True
     )[0]
@@ -112,9 +111,9 @@
     recv_x = lax.all_to_all(send_x, ("node", "ly"), split_axis=0, concat_axis=0, tiled=True)
     recv_dy = lax.all_to_all(send_dy, ("node", "ly"), split_axis=0, concat_axis=0, tiled=True)
     results = expert_rows(
-        recv_x[:, : planes * capacity, :].reshape(slots, width),
-        recv_dy.reshape(slots, width),
-        recv_x[:, planes * capacity, : planes * capacity].reshape(slots),
+        recv_x.reshape(slots, width),
+        recv_dy[:, : planes * capacity, :].reshape(slots, width),
+        recv_dy[:, planes * capacity, : planes * capacity].reshape(slots),
         gate_proj,
         up_proj,
         down_proj,

time: 482 us -> 483 us (level)
  waiting for transfers between devices: 263 us -> 268 us
    all_gather x1, waiting for transfers between devices: 7.64 us -> 19.7 us  [local(): lax.all_gather(jnp.concatenate([w_gate, w_up, w_down], axis=2), 'dp', axi...]
    all_to_all x1, waiting for transfers between devices: 28.4 us -> 22.5 us  [local(): lax.all_to_all(send_x, ('node', 'ly'), split_axis=0, concat_axis=0, tiled...]
  transfers between devices with their start and end apart: 9 -> 9, of which waited for: 7 -> 7; matrix products, arithmetic and copies ran while one was open for 19% -> 18% of each run, Pallas kernels for 0% -> 0%
where the time goes in v10:
time: 483 us; the launch traced here: 482 us
  waiting for transfers between devices  268 us (55%)
  blocking collectives  83.1 us (17%)
  matrix products  62.2 us (13%)
  local copies, waits for them, and re-layouts  22.9 us (5%)
  other arithmetic  21 us (4%)
  between operations  14.4 us (3%)
  starting transfers between devices  11.1 us (2%)
    all_gather x1, waiting for transfers between devices, local(): lax.all_gather(jnp.concatenate([tokens, meta], axis=0), 'lz', axis=0, til...  60.5 us
    reduce_scatter x1, waiting for transfers between devices, local(): lax.psum_scatter(jnp.concatenate([partial_lo, gate_cols], axis=1), 'lz',...  55.5 us
    all_to_all x1, blocking collectives, local(): lax.all_to_all(back_lo, ('node', 'ly'), split_axis=0, concat_axis=0, tile...  41.8 us
    all_to_all x1, blocking collectives, local(): lax.all_to_all(back_hi, ('node', 'ly'), split_axis=0, concat_axis=0, tile...  41.4 us
    all_to_all x1, waiting for transfers between devices, local(): lax.all_to_all(send_dy, ('node', 'ly'), split_axis=0, concat_axis=0, tile...  39.6 us
    all_gather x1, waiting for transfers between devices, local(): seen_dy = lax.all_gather(cotangent, 'lz', axis=0, tiled=False)  38.8 us
    reduce_scatter x1, waiting for transfers between devices, local(): lax.psum_scatter(partial_hi, 'lz', scatter_dimension=0, tiled=True)[0]  30.2 us
    all_to_all x1, waiting for transfers between devices, local(): lax.all_to_all(send_x, ('node', 'ly'), split_axis=0, concat_axis=0, tiled...  22.5 us
  transfers between devices with their start and end apart: 9, of which 7 were waited for; matrix products, arithmetic and copies ran while one was open for 18% of the time, Pallas kernels for 0%

profile of v10, /device:TPU:1, one launch (start us, length us, event | category | flops | bytes accessed | tf_op | source)
XLA Modules:
  0.0 482.4 jit_solution(11071271552936918525)
XLA Ops:
  7.2 0.7 convert_element_type.92
  7.9 0.7 pad_maximum_fusion.4
  8.6 0.1 copy.59
  8.8 1.9 maximum_bitcast_fusion
  10.8 0.7 all-gather.9.cloned.1.call-update
  11.5 60.5 %all-gather.11.cloned.1.call-done = bf16[8,129,2048]{2,1,0:T(8,128)(2,1)} async-done(((bf16[1,129,2048]{2,1,0:T(8,128)(2,1)}), bf16[8,129,2048]{2,1,0:T(8,128)(2,1)}) %all-gather.11.cloned.1.call-update) | async-done | bytes 4227088 | tf_op jit(solution)/shard_map/all_gather | solution.py:57
  72.0 1.1 slice_reduce_fusion
  73.1 0.2 reshape_squeeze.2
  73.3 0.1 fusion.55
  73.5 0.1 copy.79
  73.6 0.1 compare_reduce_fusion
  73.7 0.1 fusion.26
  73.8 4.0 convert_bitcast_fusion
  77.8 3.3 copy.65
  81.1 5.5 %all-to-all-start.1 = ((bf16[8,192,2048]{2,1,0:T(8,128)(2,1)}), bf16[8,192,2048]{2,1,0:T(8,128)(2,1)}, u32[]{:S(2)}, u32[]{:S(2)}) async-start(bf16[8,192,2048]{2,1,0:T(8,128)(2,1)} %bitcast.60), calls=%async_computation.1 | async-start | bytes 12582912 | tf_op jit(solution)/shard_map/all_to_all | solution.py:111
  86.6 1.1 pad_maximum_fusion.2
  87.8 0.1 copy.62
  87.9 0.1 fusion.45
  88.0 0.3 fusion.35
  88.4 38.8 %all-gather.9.cloned.1.call-done = bf16[1024,2048]{1,0:T(8,128)(2,1)} async-done(((bf16[128,2048]{1,0:T(8,128)(2,1)}), bf16[1024,2048]{1,0:T(8,128)(2,1)}) %all-gather.9.cloned.1.call-update) | async-done | bytes 4194320 | tf_op jit(solution)/shard_map/all_gather | solution.py:58
  127.2 4.0 convert_bitcast_fusion.1
  131.2 1.1 copy.61
  132.3 3.3 fusion.1
  135.6 22.5 %all-to-all-done.1 = bf16[8,192,2048]{2,1,0:T(8,128)(2,1)} async-done(((bf16[8,192,2048]{2,1,0:T(8,128)(2,1)}), bf16[8,192,2048]{2,1,0:T(8,128)(2,1)}, u32[]{:S(2)}, u32[]{:S(2)}) %all-to-all-start.1) | async-done | bytes 6291488 | tf_op jit(solution)/shard_map/all_to_all | solution.py:111
  158.2 4.8 all-to-all-start
  163.0 0.1 reduce-scatter.5.cloned.1.call-start
  163.1 19.7 %all-gather.7.cloned.1.call-done = bf16[1,2048,1152]{2,1,0:T(8,128)(2,1)} async-done(((bf16[1,512,1152]{2,1,0:T(8,128)(2,1)}), bf16[1,2048,1152]{2,1,0:T(8,128)(2,1)}) %all-gather.7.cloned.1.call-update) | async-done | bytes 4718608 | tf_op jit(solution)/shard_map/all_gather | solution.py:105
  182.8 7.3 %fusion.18 = f32[1536,384]{0,1:T(8,128)} fusion(bf16[1536,2048]{1,0:T(8,128)(2,1)} %bitcast.15, bf16[2048,1152]{1,0:T(8,128)(2,1)} %bitcast.69), kind=kOutput, calls=%fused_computation.27 | convolution fusion | flops 2415919104 | bytes 10223616 | tf_op jit(solution)/shard_map/dot_general | solution.py:9
  190.1 7.3 %fusion.22 = f32[1536,384]{0,1:T(8,128)} fusion(bf16[1536,2048]{1,0:T(8,128)(2,1)} %bitcast.15, bf16[2048,1152]{1,0:T(8,128)(2,1)} %bitcast.70), kind=kOutput, calls=%fused_computation.31 | convolution fusion | flops 2415919104 | bytes 10223616 | tf_op jit(solution)/shard_map/dot_general | solution.py:8
  197.4 39.6 %all-to-all-done = bf16[8,193,2048]{2,1,0:T(8,128)(2,1)} async-done(((bf16[8,193,2048]{2,1,0:T(8,128)(2,1)}), bf16[8,193,2048]{2,1,0:T(8,128)(2,1)}, u32[]{:S(2)}, u32[]{:S(2)}) %all-to-all-start) | async-done | bytes 6324256 | tf_op jit(solution)/shard_map/all_to_all | solution.py:112
  237.1 0.8 fusion.49
  237.9 3.5 slice.78
  241.5 2.7 copy-done.1
  244.2 5.4 %fusion.24 = f32[2048,384]{1,0:T(8,128)} fusion(bf16[1536,2048]{1,0:T(8,128)(2,1)S(1)} %bitcast.67, f32[1536]{0:T(1024)S(1)} %reshape.117, f32[1536,384]{0,1:T(8,128)S(1)} %copy-done.7, f32[1536,384]{0,1:T(8,128)S(1)} %copy-done.8), kind=kOutput, calls=%fused_computation.33 | convolution fusion | flops 2420047872 | bytes 14161920 | tf_op jit(solution)/shard_map/dot_general | solution.py:23
  249.6 0.3 reduce-scatter.7.cloned.1.call-start
  249.9 8.4 %multiply_reduce_fusion = (bf16[1536]{0:T(1024)(128)(2,1)S(1)}, bf16[1536,384]{0,1:T(8,128)(2,1)S(1)}, bf16[1536,384]{0,1:T(8,128)(2,1)S(1)}) fusion(f32[1536,384]{0,1:T(8,128)} %fusion.18, f32[1536,384]{0,1:T(8,128)} %fusion.22, f32[1536]{0:T(1024)S(1)} %reshape.117, bf16[1536,2048]{1,0:T(8,128)(2,1)} %bitcast.68, bf16[2048,1152]{1,0:T(8,128)(2,1)} %bitcast.71), kind=kOutput, calls=%fused_computation.16 | convolution fusion | flops 2425944576 | bytes 14951424 | tf_op jit(solution)/shard_map/dot_general | solution.py:13
  258.3 5.2 %fusion.56 = f32[2048,384]{0,1:T(8,128)S(1)} fusion(bf16[1536,384]{0,1:T(8,128)(2,1)S(1)} %get-tuple-element.39, bf16[1536,2048]{1,0:T(8,128)(2,1)} %bitcast.15), kind=kOutput, calls=%fused_computation.82 | convolution fusion | flops 2415919104 | bytes 10616832 | tf_op jit(solution)/shard_map/dot_general | solution.py:26
  263.5 4.8 fusion.57
  268.3 3.0 pad_maximum_fusion
  271.3 0.3 reduce-scatter.11.cloned.1.call-start
  271.6 4.9 %fusion.20 = f32[1536,2048]{1,0:T(8,128)S(1)} fusion(bf16[1536,384]{0,1:T(8,128)(2,1)S(1)} %get-tuple-element.39, bf16[2048,1152]{1,0:T(8,128)(2,1)} %bitcast.72), kind=kOutput, calls=%fused_computation.29 | convolution fusion | flops 2415919104 | bytes 15335424 | tf_op jit(solution)/shard_map/dot_general | solution.py:31
  276.5 5.5 %add_convert_fusion = bf16[1536,2048]{1,0:T(8,128)(2,1)S(1)} fusion(f32[1536,2048]{1,0:T(8,128)S(1)} %fusion.20, bf16[1536,384]{0,1:T(8,128)(2,1)} %copy-done.3, bf16[2048,1152]{1,0:T(8,128)(2,1)} %bitcast.73), kind=kOutput, calls=%fused_computation.2 | convolution fusion | flops 2422210560 | bytes 21626880 | tf_op jit(solution)/shard_map/dot_general | solution.py:34
  282.0 2.4 fusion.54
  284.4 41.4 %all_to_all.20 = bf16[8,192,1024]{2,1,0:T(8,128)(2,1)S(1)} all-to-all(bf16[8,192,1024]{2,1,0:T(8,128)(2,1)S(1)} %bitcast.65), channel_id=1, replica_groups=mesh['dp'=4,'node'=2,'lz'=8,'ly'=4] {'node','ly'}, dimensions={0} | all-to-all | bytes 6291456 | tf_op jit(solution)/shard_map/all_to_all | solution.py:134
  325.7 2.7 fusion.12
  328.6 1.7 copy-done
  330.3 0.4 fusion.3
  330.7 41.8 %all_to_all.21 = bf16[8,193,1024]{2,1,0:T(8,128)(2,1)S(1)} all-to-all(bf16[8,193,1024]{2,1,0:T(8,128)(2,1)S(1)} %fusion.3), channel_id=1, replica_groups=mesh['dp'=4,'node'=2,'lz'=8,'ly'=4] {'node','ly'}, dimensions={0} | all-to-all | bytes 6324224 | tf_op jit(solution)/shard_map/all_to_all | solution.py:129
  372.6 0.4 fusion.36
  373.0 0.2 fusion.46
  373.1 0.9 copy.69
  374.1 1.3 reshape.118
  375.4 0.4 slice.85
  375.8 2.7 fusion.9
  378.6 5.0 %pad_maximum_fusion.1 = f32[8,129,1024]{2,1,0:T(8,128)} fusion(f32[8,1,1024]{2,1,0:T(1,128)S(1)} %copy.70, f32[8,128,1024]{2,1,0:T(8,128)} %fusion.9), kind=kLoop, calls=%fused_computation.9 | loop fusion | flops 1056768 | bytes 8454144 | tf_op jit(solution)/shard_map/concatenate | solution.py:161
  383.6 30.2 %reduce-scatter.11.cloned.1.call-done = f32[1,128,1024]{2,1,0:T(8,128)} async-done(((f32[8,128,1024]{2,1,0:T(8,128)}), f32[1,128,1024]{2,1,0:T(8,128)}) %reduce-scatter.11.cloned.1.call-update) | async-done | bytes 524304 | tf_op jit(solution)/shard_map/reduce_scatter | solution.py:166
  413.8 1.1 convert_bitcast_fusion.2
  414.9 0.1 slice_bitcast_fusion.2
  415.0 1.1 copy.74
  416.2 1.1 copy.73
  417.3 55.5 %reduce-scatter.9.cloned.1.call-done = f32[1,129,1024]{2,1,0:T(8,128)} async-done(((f32[8,129,1024]{2,1,0:T(8,128)}), f32[1,129,1024]{2,1,0:T(8,128)}) %reduce-scatter.9.cloned.1.call-update) | async-done | bytes 528400 | tf_op jit(solution)/shard_map/reduce_scatter | solution.py:160
  472.8 1.1 convert.16
  474.1 0.7 copy.72
  474.7 0.8 pad_maximum_fusion.3
  (42 shorter events, 0.9 us)
Async XLA Ops:
  7.2 64.8 %all-gather.11.cloned.1.call-start = ((), (), s32[]{:S(2)}) async-start(), calls=%async_computation.14 | async-start | bytes 5013504 | tf_op jit(solution)/shard_map/all_gather | solution.py:57
  10.7 116.5 %all-gather.9.cloned.1.call-start = ((), (), s32[]{:S(2)}) async-start(), calls=%async_computation.13 | async-start | bytes 4718592 | tf_op jit(solution)/shard_map/all_gather | solution.py:58
  81.1 5.5 %copy-start.4 = (bf16[1,512,384]{2,1,0:T(8,128)(2,1)S(1)}, bf16[1,512,384]{2,1,0:T(8,128)(2,1)}, u32[]{:S(2)}) copy-start(bf16[1,512,384]{2,1,0:T(8,128)(2,1)} %param.13) | copy-start | bytes 1179652
  81.1 5.5 %copy-start.5 = (bf16[1,512,384]{2,1,0:T(8,128)(2,1)S(1)}, bf16[1,512,384]{2,1,0:T(8,128)(2,1)}, u32[]{:S(2)}) copy-start(bf16[1,512,384]{2,1,0:T(8,128)(2,1)} %param.12) | copy-start | bytes 1179652
  81.1 5.5 %copy-start.6 = (bf16[1,512,384]{2,1,0:T(8,128)(2,1)S(1)}, bf16[1,512,384]{2,1,0:T(8,128)(2,1)}, u32[]{:S(2)}) copy-start(bf16[1,512,384]{2,1,0:T(8,128)(2,1)} %param.11) | copy-start | bytes 1179652
  81.1 77.1 %all-to-all-start.1 = ((bf16[8,192,2048]{2,1,0:T(8,128)(2,1)}), bf16[8,192,2048]{2,1,0:T(8,128)(2,1)}, u32[]{:S(2)}, u32[]{:S(2)}) async-start(bf16[8,192,2048]{2,1,0:T(8,128)(2,1)} %bitcast.60), calls=%async_computation.1 | async-start | bytes 12582912 | tf_op jit(solution)/shard_map/all_to_all | solution.py:111
  86.6 96.2 %all-gather.7.cloned.1.call-start = ((), (), s32[]{:S(2)}) async-start(), calls=%async_computation.8 | async-start | bytes 5898240 | tf_op jit(solution)/shard_map/all_gather | solution.py:105
  158.2 78.9 %all-to-all-start = ((bf16[8,193,2048]{2,1,0:T(8,128)(2,1)}), bf16[8,193,2048]{2,1,0:T(8,128)(2,1)}, u32[]{:S(2)}, u32[]{:S(2)}) async-start(bf16[8,193,2048]{2,1,0:T(8,128)(2,1)} %fusion.1), calls=%async_computation | async-start | bytes 13107200 | tf_op jit(solution)/shard_map/all_to_all | solution.py:112
  163.0 215.5 %reduce-scatter.5.cloned.1.call-start = ((), (), s32[]{:S(2)}) async-start(), calls=%async_computation.9 | async-start | bytes 3932160 | tf_op jit(solution)/shard_map/reduce_scatter | solution.py:153
  237.9 6.2 %copy-start.7 = (f32[1536,384]{0,1:T(8,128)S(1)}, f32[1536,384]{0,1:T(8,128)}, u32[]{:S(2)}) copy-start(f32[1536,384]{0,1:T(8,128)} %fusion.18) | copy-start | bytes 7077892
  237.9 6.2 %copy-start.8 = (f32[1536,384]{0,1:T(8,128)S(1)}, f32[1536,384]{0,1:T(8,128)}, u32[]{:S(2)}) copy-start(f32[1536,384]{0,1:T(8,128)} %fusion.22) | copy-start | bytes 7077892
  241.5 2.7 copy-start.1
  249.6 128.9 %reduce-scatter.7.cloned.1.call-start = ((), (), s32[]{:S(2)}) async-start(), calls=%async_computation.10 | async-start | bytes 7864320 | tf_op jit(solution)/shard_map/reduce_scatter | solution.py:154
  258.3 5.2 %copy-start.3 = (bf16[1536,384]{0,1:T(8,128)(2,1)}, bf16[1536,384]{0,1:T(8,128)(2,1)S(1)}, u32[]{:S(2)}) copy-start(bf16[1536,384]{0,1:T(8,128)(2,1)S(1)} %get-tuple-element.42) | copy-start | bytes 3538948
  271.3 142.5 %reduce-scatter.11.cloned.1.call-start = ((), (), s32[]{:S(2)}) async-start(), calls=%async_computation.12 | async-start | bytes 4718592 | tf_op jit(solution)/shard_map/reduce_scatter | solution.py:166
  328.4 1.9 copy-start
  328.4 144.4 %reduce-scatter.9.cloned.1.call-start = ((), (), s32[]{:S(2)}) async-start(), calls=%async_computation.11 | async-start | bytes 5013504 | tf_op jit(solution)/shard_map/reduce_scatter | solution.py:160
  383.6 31.3 %copy-start.2 = (f32[512,768]{0,1:T(8,128)S(1)}, f32[512,768]{0,1:T(8,128)}, u32[]{:S(2)}) copy-start(f32[512,768]{0,1:T(8,128)} %reduce-scatter.7.cloned.1.call-done) | copy-start | bytes 4718596
Sparse Core Ops, SparseCore 0:
  10.9 61.0 all-gather.10
  73.8 53.4 all-gather.8
  129.0 53.7 all-gather.6
  249.8 37.8 reduce-scatter.4
  290.0 66.2 reduce-scatter.6
  358.7 55.0 reduce-scatter.10
  416.4 56.3 reduce-scatter.8

commit v11 on v9

--- a/solution.py
+++ b/solution.py
@@ -54,9 +54,10 @@
     half = width // 2
     meta = jnp.concatenate([gates, routes.astype(jnp.bfloat16)], axis=1).reshape(1, -1)
     meta = jnp.pad(meta, ((0, 0), (0, width - meta.shape[1])))
-    seen_x = lax.all_gather(jnp.concatenate([tokens, meta], axis=0), "lz", axis=0, tiled=False)
+    seen_row = lax.all_gather(meta, "lz", axis=0, tiled=False)
+    seen_x = lax.all_gather(tokens, "lz", axis=0, tiled=False)
     seen_dy = lax.all_gather(cotangent, "lz", axis=0, tiled=False)
-    seen_meta = seen_x[:, tokens_dev, : 2 * tokens_dev * top_count].reshape(
+    seen_meta = seen_row[:, 0, : 2 * tokens_dev * top_count].reshape(
         planes, tokens_dev, 2 * top_count
     )
     seen_gates = seen_meta[..., :top_count]
@@ -92,7 +93,7 @@
     send_x = jnp.einsum(
         "jzrt,ztd->jzrd",
         choose_b,
-        seen_x[:, :tokens_dev, :],
+        seen_x,
         preferred_element_type=jnp.float32,
     ).astype(jnp.bfloat16)
     send_x = jnp.concatenate(

time: 482 us -> 476 us (0.988)
  waiting for transfers between devices: 263 us -> 237 us
  blocking collectives: 83.1 us -> 107 us
    all_gather x1, waiting for transfers between devices: 60.5 us -> 33.4 us  [local(): seen_x = lax.all_gather(tokens, 'lz', axis=0, tiled=False)]
    all_gather x0 -> x1, blocking collectives: none -> 23.4 us  [local(): seen_row = lax.all_gather(meta, 'lz', axis=0, tiled=False)]
where the time goes in v11:
time: 476 us; the launch traced here: 475 us
  waiting for transfers between devices  237 us (50%)
  blocking collectives  107 us (22%)
  matrix products  64.7 us (14%)
  local copies, waits for them, and re-layouts  22.2 us (5%)
  other arithmetic  19.3 us (4%)
  between operations  14.4 us (3%)
  starting transfers between devices  11.1 us (2%)
    reduce_scatter x1, waiting for transfers between devices, local(): lax.psum_scatter(jnp.concatenate([partial_lo, gate_cols], axis=1), 'lz',...  55.5 us
    all_to_all x1, blocking collectives, local(): lax.all_to_all(back_lo, ('node', 'ly'), split_axis=0, concat_axis=0, tile...  41.8 us
    all_to_all x1, blocking collectives, local(): lax.all_to_all(back_hi, ('node', 'ly'), split_axis=0, concat_axis=0, tile...  41.4 us
    all_to_all x1, waiting for transfers between devices, local(): lax.all_to_all(send_dy, ('node', 'ly'), split_axis=0, concat_axis=0, tile...  40.5 us
    all_gather x1, waiting for transfers between devices, local(): seen_dy = lax.all_gather(cotangent, 'lz', axis=0, tiled=False)  40.2 us
    all_gather x1, waiting for transfers between devices, local(): seen_x = lax.all_gather(tokens, 'lz', axis=0, tiled=False)  33.4 us
    reduce_scatter x1, waiting for transfers between devices, local(): lax.psum_scatter(partial_hi, 'lz', scatter_dimension=0, tiled=True)[0]  30 us
    all_to_all x1, waiting for transfers between devices, local(): lax.all_to_all(send_x, ('node', 'ly'), split_axis=0, concat_axis=0, tiled...  25.9 us
  transfers between devices with their start and end apart: 9, of which 7 were waited for; matrix products, arithmetic and copies ran while one was open for 19% of the time, Pallas kernels for 0%

profile of v11, /device:TPU:1, one launch (start us, length us, event | category | flops | bytes accessed | tf_op | source)
XLA Modules:
  0.0 475.3 jit_solution(9930952564812045546)
XLA Ops:
  7.2 0.7 all-gather.10.cloned.1.call-update
  7.9 0.7 all-gather.8.cloned.1.call-update
  8.7 0.7 convert_element_type.92
  9.3 0.7 pad_maximum_fusion.4
  10.0 0.1 copy.58
  10.3 23.4 %all_gather.22 = bf16[8,1,2048]{2,1,0:T(2,128)(2,1)S(1)} all-gather(bf16[1,1,2048]{2,1,0:T(2,128)(2,1)S(1)} %all_gather.21), channel_id=1, replica_groups=mesh['dp'=4,'node'=2,'lz'=8,'ly'=4] {'lz'}, dimensions={0}, use_global_device_ids=true | all-gather | bytes 36864 | tf_op jit(solution)/shard_map/all_gather | solution.py:57
  33.7 0.2 reduce.4
  33.9 0.2 reshape_squeeze.2
  34.1 0.1 fusion.55
  34.2 0.1 copy.62
  34.4 0.1 copy.78
  34.5 0.1 compare_reduce_fusion
  34.6 0.1 fusion.45
  34.7 0.1 fusion.26
  34.9 0.3 fusion.35
  35.3 33.4 %all-gather.10.cloned.1.call-done = bf16[1024,2048]{1,0:T(8,128)(2,1)} async-done(((bf16[128,2048]{1,0:T(8,128)(2,1)}), bf16[1024,2048]{1,0:T(8,128)(2,1)}) %all-gather.10.cloned.1.call-update) | async-done | bytes 4194320 | tf_op jit(solution)/shard_map/all_gather | solution.py:58
  68.7 4.0 convert_bitcast_fusion
  72.7 1.1 copy.61
  73.8 3.3 fusion.1
  77.1 5.5 %all-to-all-start.1 = ((bf16[8,193,2048]{2,1,0:T(8,128)(2,1)}), bf16[8,193,2048]{2,1,0:T(8,128)(2,1)}, u32[]{:S(2)}, u32[]{:S(2)}) async-start(bf16[8,193,2048]{2,1,0:T(8,128)(2,1)} %fusion.1), calls=%async_computation.1 | async-start | bytes 13107200 | tf_op jit(solution)/shard_map/all_to_all | solution.py:113
  82.6 1.1 pad_maximum_fusion.2
  83.8 40.2 %all-gather.8.cloned.1.call-done = bf16[1024,2048]{1,0:T(8,128)(2,1)} async-done(((bf16[128,2048]{1,0:T(8,128)(2,1)}), bf16[1024,2048]{1,0:T(8,128)(2,1)}) %all-gather.8.cloned.1.call-update) | async-done | bytes 4194320 | tf_op jit(solution)/shard_map/all_gather | solution.py:59
  123.9 4.0 convert_bitcast_fusion.1
  127.9 3.2 copy.60
  131.1 25.9 %all-to-all-done.1 = bf16[8,193,2048]{2,1,0:T(8,128)(2,1)} async-done(((bf16[8,193,2048]{2,1,0:T(8,128)(2,1)}), bf16[8,193,2048]{2,1,0:T(8,128)(2,1)}, u32[]{:S(2)}, u32[]{:S(2)}) %all-to-all-start.1) | async-done | bytes 6324256 | tf_op jit(solution)/shard_map/all_to_all | solution.py:113
  157.0 4.8 %all-to-all-start = ((bf16[8,192,2048]{2,1,0:T(8,128)(2,1)}), bf16[8,192,2048]{2,1,0:T(8,128)(2,1)}, u32[]{:S(2)}, u32[]{:S(2)}) async-start(bf16[8,192,2048]{2,1,0:T(8,128)(2,1)} %bitcast.59), calls=%async_computation | async-start | bytes 12582912 | tf_op jit(solution)/shard_map/all_to_all | solution.py:114
  161.8 0.2 reduce-scatter.5.cloned.1.call-start
  161.9 0.8 fusion.49
  162.8 6.6 %slice.70 = bf16[8,192,2048]{2,1,0:T(8,128)(2,1)} slice(bf16[8,193,2048]{2,1,0:T(8,128)(2,1)} %all-to-all-done.1), slice={[0:8], [0:192], [0:2048]} | slice | bytes 12582912 | tf_op jit(solution)/shard_map/slice | solution.py:116
  169.4 10.1 %all-gather.6.cloned.1.call-done = bf16[1,2048,1152]{2,1,0:T(8,128)(2,1)} async-done(((bf16[1,512,1152]{2,1,0:T(8,128)(2,1)}), bf16[1,2048,1152]{2,1,0:T(8,128)(2,1)}) %all-gather.6.cloned.1.call-update) | async-done | bytes 4718608 | tf_op jit(solution)/shard_map/all_gather | solution.py:107
  179.6 7.4 %fusion.18 = f32[1536,384]{0,1:T(8,128)} fusion(bf16[1536,2048]{1,0:T(8,128)(2,1)} %bitcast.67, bf16[2048,1152]{1,0:T(8,128)(2,1)} %bitcast.71), kind=kOutput, calls=%fused_computation.26 | convolution fusion | flops 2415919104 | bytes 10223616 | tf_op jit(solution)/shard_map/dot_general | solution.py:9
  187.0 5.5 %fusion.22 = f32[1536,384]{0,1:T(8,128)} fusion(bf16[1536,2048]{1,0:T(8,128)(2,1)S(1)} %bitcast.70, bf16[2048,1152]{1,0:T(8,128)(2,1)} %bitcast.72), kind=kOutput, calls=%fused_computation.30 | convolution fusion | flops 2415919104 | bytes 10223616 | tf_op jit(solution)/shard_map/dot_general | solution.py:8
  192.5 40.5 %all-to-all-done = bf16[8,192,2048]{2,1,0:T(8,128)(2,1)} async-done(((bf16[8,192,2048]{2,1,0:T(8,128)(2,1)}), bf16[8,192,2048]{2,1,0:T(8,128)(2,1)}, u32[]{:S(2)}, u32[]{:S(2)}) %all-to-all-start) | async-done | bytes 6291488 | tf_op jit(solution)/shard_map/all_to_all | solution.py:114
  233.0 9.4 %fusion.24 = f32[2048,384]{1,0:T(8,128)} fusion(bf16[1536,2048]{1,0:T(8,128)(2,1)} %bitcast.8, f32[1536]{0:T(1024)S(1)} %reshape.115, f32[1536,384]{0,1:T(8,128)} %fusion.18, f32[1536,384]{0,1:T(8,128)} %fusion.22), kind=kOutput, calls=%fused_computation.32 | convolution fusion | flops 2420047872 | bytes 14161920 | tf_op jit(solution)/shard_map/dot_general | solution.py:23
  242.5 0.3 reduce-scatter.7.cloned.1.call-start
  242.8 8.4 %multiply_reduce_fusion = (bf16[1536]{0:T(1024)(128)(2,1)S(1)}, bf16[1536,384]{0,1:T(8,128)(2,1)S(1)}, bf16[1536,384]{0,1:T(8,128)(2,1)S(1)}) fusion(f32[1536,384]{0,1:T(8,128)} %fusion.18, f32[1536,384]{0,1:T(8,128)} %fusion.22, f32[1536]{0:T(1024)S(1)} %reshape.115, bf16[1536,2048]{1,0:T(8,128)(2,1)} %bitcast.8, bf16[2048,1152]{1,0:T(8,128)(2,1)} %bitcast.73), kind=kOutput, calls=%fused_computation.15 | convolution fusion | flops 2425944576 | bytes 14951424 | tf_op jit(solution)/shard_map/dot_general | solution.py:13
  251.2 5.2 %fusion.56 = f32[2048,384]{0,1:T(8,128)S(1)} fusion(bf16[1536,384]{0,1:T(8,128)(2,1)S(1)} %get-tuple-element.39, bf16[1536,2048]{1,0:T(8,128)(2,1)} %bitcast.68), kind=kOutput, calls=%fused_computation.79 | convolution fusion | flops 2415919104 | bytes 10616832 | tf_op jit(solution)/shard_map/dot_general | solution.py:26
  256.3 4.8 %fusion.57 = f32[2048,384]{0,1:T(8,128)S(1)} fusion(bf16[1536,384]{0,1:T(8,128)(2,1)S(1)} %get-tuple-element.42, bf16[1536,2048]{1,0:T(8,128)(2,1)} %bitcast.69), kind=kOutput, calls=%fused_computation.80 | convolution fusion | flops 2415919104 | bytes 10616832 | tf_op jit(solution)/shard_map/dot_general | solution.py:29
  261.1 3.1 pad_maximum_fusion
  264.2 0.3 reduce-scatter.11.cloned.1.call-start
  264.5 4.9 %fusion.20 = f32[1536,2048]{1,0:T(8,128)S(1)} fusion(bf16[1536,384]{0,1:T(8,128)(2,1)S(1)} %get-tuple-element.39, bf16[2048,1152]{1,0:T(8,128)(2,1)} %bitcast.74), kind=kOutput, calls=%fused_computation.28 | convolution fusion | flops 2415919104 | bytes 15335424 | tf_op jit(solution)/shard_map/dot_general | solution.py:31
  269.4 5.5 %add_convert_fusion = bf16[1536,2048]{1,0:T(8,128)(2,1)S(1)} fusion(f32[1536,2048]{1,0:T(8,128)S(1)} %fusion.20, bf16[1536,384]{0,1:T(8,128)(2,1)} %copy-done.3, bf16[2048,1152]{1,0:T(8,128)(2,1)} %bitcast.75), kind=kOutput, calls=%fused_computation.2 | convolution fusion | flops 2422210560 | bytes 21626880 | tf_op jit(solution)/shard_map/dot_general | solution.py:34
  274.9 2.5 fusion.54
  277.3 41.4 %all_to_all.20 = bf16[8,192,1024]{2,1,0:T(8,128)(2,1)S(1)} all-to-all(bf16[8,192,1024]{2,1,0:T(8,128)(2,1)S(1)} %bitcast.64), channel_id=1, replica_groups=mesh['dp'=4,'node'=2,'lz'=8,'ly'=4] {'node','ly'}, dimensions={0} | all-to-all | bytes 6291456 | tf_op jit(solution)/shard_map/all_to_all | solution.py:136
  318.7 2.8 fusion.12
  321.7 1.7 copy-done
  323.4 0.4 fusion.3
  323.8 41.8 %all_to_all.21 = bf16[8,193,1024]{2,1,0:T(8,128)(2,1)S(1)} all-to-all(bf16[8,193,1024]{2,1,0:T(8,128)(2,1)S(1)} %fusion.3), channel_id=1, replica_groups=mesh['dp'=4,'node'=2,'lz'=8,'ly'=4] {'node','ly'}, dimensions={0} | all-to-all | bytes 6324224 | tf_op jit(solution)/shard_map/all_to_all | solution.py:131
  365.6 0.4 fusion.36
  366.0 0.2 fusion.46
  366.2 0.9 copy.68
  367.1 1.3 reshape.116
  368.4 0.4 slice.75
  368.9 2.8 fusion.9
  371.7 4.9 %pad_maximum_fusion.1 = f32[8,129,1024]{2,1,0:T(8,128)} fusion(f32[8,1,1024]{2,1,0:T(1,128)S(1)} %copy.69, f32[8,128,1024]{2,1,0:T(8,128)} %fusion.9), kind=kLoop, calls=%fused_computation.9 | loop fusion | flops 1056768 | bytes 8454144 | tf_op jit(solution)/shard_map/concatenate | solution.py:163
  376.7 30.0 %reduce-scatter.11.cloned.1.call-done = f32[1,128,1024]{2,1,0:T(8,128)} async-done(((f32[8,128,1024]{2,1,0:T(8,128)}), f32[1,128,1024]{2,1,0:T(8,128)}) %reduce-scatter.11.cloned.1.call-update) | async-done | bytes 524304 | tf_op jit(solution)/shard_map/reduce_scatter | solution.py:168
  406.7 1.1 convert_bitcast_fusion.2
  407.8 0.1 slice_bitcast_fusion
  407.9 1.1 copy.73
  409.0 1.1 copy.72
  410.2 55.5 %reduce-scatter.9.cloned.1.call-done = f32[1,129,1024]{2,1,0:T(8,128)} async-done(((f32[8,129,1024]{2,1,0:T(8,128)}), f32[1,129,1024]{2,1,0:T(8,128)}) %reduce-scatter.9.cloned.1.call-update) | async-done | bytes 528400 | tf_op jit(solution)/shard_map/reduce_scatter | solution.py:162
  465.7 1.1 convert.16
  466.9 0.7 copy.71
  467.6 0.8 pad_maximum_fusion.3
  (38 shorter events, 0.9 us)
Async XLA Ops:
  7.2 61.5 %all-gather.10.cloned.1.call-start = ((), (), s32[]{:S(2)}) async-start(), calls=%async_computation.14 | async-start | bytes 4718592 | tf_op jit(solution)/shard_map/all_gather | solution.py:58
  7.9 116.0 %all-gather.8.cloned.1.call-start = ((), (), s32[]{:S(2)}) async-start(), calls=%async_computation.13 | async-start | bytes 4718592 | tf_op jit(solution)/shard_map/all_gather | solution.py:59
  77.1 5.5 %copy-start.4 = (bf16[1,512,384]{2,1,0:T(8,128)(2,1)S(1)}, bf16[1,512,384]{2,1,0:T(8,128)(2,1)}, u32[]{:S(2)}) copy-start(bf16[1,512,384]{2,1,0:T(8,128)(2,1)} %param.13) | copy-start | bytes 1179652
  77.1 5.5 %copy-start.5 = (bf16[1,512,384]{2,1,0:T(8,128)(2,1)S(1)}, bf16[1,512,384]{2,1,0:T(8,128)(2,1)}, u32[]{:S(2)}) copy-start(bf16[1,512,384]{2,1,0:T(8,128)(2,1)} %param.12) | copy-start | bytes 1179652
  77.1 5.5 %copy-start.6 = (bf16[1,512,384]{2,1,0:T(8,128)(2,1)S(1)}, bf16[1,512,384]{2,1,0:T(8,128)(2,1)}, u32[]{:S(2)}) copy-start(bf16[1,512,384]{2,1,0:T(8,128)(2,1)} %param.11) | copy-start | bytes 1179652
  77.1 79.8 %all-to-all-start.1 = ((bf16[8,193,2048]{2,1,0:T(8,128)(2,1)}), bf16[8,193,2048]{2,1,0:T(8,128)(2,1)}, u32[]{:S(2)}, u32[]{:S(2)}) async-start(bf16[8,193,2048]{2,1,0:T(8,128)(2,1)} %fusion.1), calls=%async_computation.1 | async-start | bytes 13107200 | tf_op jit(solution)/shard_map/all_to_all | solution.py:113
  82.6 96.9 %all-gather.6.cloned.1.call-start = ((), (), s32[]{:S(2)}) async-start(), calls=%async_computation.8 | async-start | bytes 5898240 | tf_op jit(solution)/shard_map/all_gather | solution.py:107
  157.0 76.1 %all-to-all-start = ((bf16[8,192,2048]{2,1,0:T(8,128)(2,1)}), bf16[8,192,2048]{2,1,0:T(8,128)(2,1)}, u32[]{:S(2)}, u32[]{:S(2)}) async-start(bf16[8,192,2048]{2,1,0:T(8,128)(2,1)} %bitcast.59), calls=%async_computation | async-start | bytes 12582912 | tf_op jit(solution)/shard_map/all_to_all | solution.py:114
  161.8 209.9 %reduce-scatter.5.cloned.1.call-start = ((), (), s32[]{:S(2)}) async-start(), calls=%async_computation.9 | async-start | bytes 3932160 | tf_op jit(solution)/shard_map/reduce_scatter | solution.py:155
  179.5 7.4 %copy-start.1 = (bf16[8,192,2048]{2,1,0:T(8,128)(2,1)S(1)}, bf16[8,192,2048]{2,1,0:T(8,128)(2,1)}, u32[]{:S(2)}) copy-start(bf16[8,192,2048]{2,1,0:T(8,128)(2,1)} %slice.70) | copy-start | bytes 18874372
  242.5 129.2 %reduce-scatter.7.cloned.1.call-start = ((), (), s32[]{:S(2)}) async-start(), calls=%async_computation.10 | async-start | bytes 7864320 | tf_op jit(solution)/shard_map/reduce_scatter | solution.py:156
  251.1 5.2 %copy-start.3 = (bf16[1536,384]{0,1:T(8,128)(2,1)}, bf16[1536,384]{0,1:T(8,128)(2,1)S(1)}, u32[]{:S(2)}) copy-start(bf16[1536,384]{0,1:T(8,128)(2,1)S(1)} %get-tuple-element.42) | copy-start | bytes 3538948
  264.2 142.5 %reduce-scatter.11.cloned.1.call-start = ((), (), s32[]{:S(2)}) async-start(), calls=%async_computation.12 | async-start | bytes 4718592 | tf_op jit(solution)/shard_map/reduce_scatter | solution.py:168
  321.5 1.9 copy-start
  321.5 144.2 %reduce-scatter.9.cloned.1.call-start = ((), (), s32[]{:S(2)}) async-start(), calls=%async_computation.11 | async-start | bytes 5013504 | tf_op jit(solution)/shard_map/reduce_scatter | solution.py:162
  376.7 31.1 %copy-start.2 = (f32[512,768]{0,1:T(8,128)S(1)}, f32[512,768]{0,1:T(8,128)}, u32[]{:S(2)}) copy-start(f32[512,768]{0,1:T(8,128)} %reduce-scatter.7.cloned.1.call-done) | copy-start | bytes 4718596
Sparse Core Ops, SparseCore 0:
  9.8 58.8 all-gather.9
  70.5 53.4 all-gather.7
  125.8 53.7 all-gather.5
  242.6 37.8 reduce-scatter.4
  282.9 66.2 reduce-scatter.6
  351.6 55.0 reduce-scatter.10
  409.2 56.4 reduce-scatter.8
